TPU v7x, 128 devices: a whole 4x4x4 slice. The times are simulated.
128 devices in a mesh: blk: 16 (over z_hi, y, core), freq: 8 (over z_lo, x).
Axes of the slice: x: 4, y: 4, z: 4 (z_hi: 2, z_lo: 2; z = z_hi * 2 + z_lo), core: 2. Of those that a mesh axis runs over, the one named last changes fastest.
Arguments:
- raw_voltages: bfloat16 [512, 530432], P(('blk', 'freq')), may hold values from -6 to 6
- filter_taps: float32 [4, 2048], replicated, may hold values from -3 to 3
- input_order: int32 [512], P('blk'), may hold values from 0 to 511, as said below
- chan_order: int32 [1024], replicated, may hold values from 0 to 1023, each once
Outputs:
- visibilities: float32 [2, 9, 32, 512, 1024], P(None, None, None, 'blk', 'freq')
Inputs may be any that keep to these rules, and one draw needn't show every extreme that they name: input_order is a permutation, and slot k holds a raw input of the same aligned block of 32 slots as k. `chan_order`: each channel once.
All inputs are finite; a program needn't handle non-finite values.
Results may differ from a plain program's by a relative error of at most 0.0029.
Values may be sent and summed in bfloat16 or wider, within the bound.
No kernel may reach another device: no remote copies, remote signals or barrier semaphores. Data moves between devices by JAX's collectives and lax.ppermute only.
A program may use at most 128 MiB of HBM per device.

v0:
```python
import math

import jax
import jax.numpy as jnp
from jax import lax
from jax.sharding import PartitionSpec as P

TAPS = 4
SPECTRA = 256


def from_partner(value, axis, distance):
    mask = 2**distance
    pairs = [(source, source ^ mask) for source in range(lax.axis_size(axis))]
    return lax.ppermute(value, axis, pairs)


def passed_along(value, axis, steps):
    count = lax.axis_size(axis)
    pairs = [(source, (source + steps) % count) for source in range(count)]
    return lax.ppermute(value, axis, pairs)


def make_table(chan_order):
    channel_count = chan_order.shape[0]
    sample_index = jnp.arange(2 * channel_count, dtype=jnp.int32)
    product = sample_index[:, None] * chan_order[None, :] % (2 * channel_count)
    phase_arg = product.astype(jnp.float32) * (math.pi / channel_count)
    return jnp.concatenate([jnp.cos(phase_arg), -jnp.sin(phase_arg)], axis=1) / math.sqrt(
        channel_count
    )


def filter_bank(raw_voltages, filter_taps, dft_table):
    input_count = raw_voltages.shape[0]
    channel_count = dft_table.shape[1] // 2
    frames = raw_voltages.astype(jnp.float32).reshape(
        input_count, SPECTRA + TAPS - 1, 2 * channel_count
    )
    filtered = filter_taps[0] * frames[:, 0:SPECTRA]
    for tap_index in range(1, TAPS):
        filtered = filtered + filter_taps[tap_index] * frames[:, tap_index : tap_index + SPECTRA]
    transformed = jnp.dot(
        filtered.reshape(input_count * SPECTRA, 2 * channel_count),
        dft_table,
        precision=lax.Precision.HIGHEST,
    )
    transformed = transformed.reshape(input_count, SPECTRA, 2, channel_count).transpose(0, 2, 1, 3)
    return transformed.astype(jnp.bfloat16)


def sectioned_turn(spectra_local):
    input_count, parts_count, spectra_count, channel_count = spectra_local.shape
    ranks = lax.axis_size("freq")
    block_width = channel_count // ranks
    current = spectra_local.reshape(input_count, parts_count, spectra_count, ranks, block_width)
    position = lax.axis_index("freq")
    for bit_level in range(ranks.bit_length() - 1):
        inputs_now = current.shape[0]
        groups = current.shape[3]
        split_view = current.reshape(
            inputs_now, parts_count, spectra_count, groups // 2, 2, block_width
        )
        my_bit = position >> bit_level & 1
        kept = lax.dynamic_index_in_dim(split_view, my_bit, 4, keepdims=False)
        outgoing = lax.dynamic_index_in_dim(split_view, 1 - my_bit, 4, keepdims=False)
        incoming = from_partner(outgoing, "freq", bit_level)
        lower = jnp.where(my_bit == 0, kept, incoming)
        upper = jnp.where(my_bit == 0, incoming, kept)
        current = jnp.concatenate([lower, upper], axis=0)
    return current.reshape(current.shape[0], parts_count, spectra_count, block_width)


def per_device(raw_voltages, filter_taps, input_order, chan_order):
    dft_table = make_table(chan_order)
    spectra_local = filter_bank(raw_voltages, filter_taps, dft_table)
    turned = sectioned_turn(spectra_local)
    tile_size = turned.shape[0]
    spectra_count = turned.shape[2]
    block_width = turned.shape[3]
    row_index = input_order - lax.axis_index("blk") * tile_size
    own_tile = jnp.take(turned, row_index, axis=0)
    plain = own_tile.reshape(tile_size, 2 * spectra_count, block_width)
    rotated = jnp.concatenate([own_tile[:, 1], -own_tile[:, 0]], axis=1)

    def correlate(partner):
        vis_real = (
            jnp.einsum("jtc,itc->jic", partner, plain, preferred_element_type=jnp.float32)
            / spectra_count
        )
        vis_imag = (
            jnp.einsum("jtc,itc->jic", partner, rotated, preferred_element_type=jnp.float32)
            / spectra_count
        )
        return jnp.stack([vis_real, vis_imag])

    half_loop = lax.axis_size("blk") // 2
    local_block = correlate(plain)

    def advance(carried, unused):
        arrived = passed_along(carried, "blk", 1)
        return (arrived, correlate(arrived))

    _, later_blocks = lax.scan(advance, plain, None, length=half_loop)
    stacked = jnp.concatenate([local_block[None], later_blocks], axis=0)
    return stacked.transpose(1, 0, 2, 3, 4)


def solution(mesh):
    placed = (P(("blk", "freq"), None), P(), P("blk"), P())
    return jax.shard_map(
        per_device,
        mesh=mesh,
        in_specs=placed,
        out_specs=P(None, None, None, "blk", "freq"),
        check_vma=False,
    )
```

profile of v0, /device:TPU:0, one launch (start us, length us, event | category | flops | bytes accessed | tf_op | source)
XLA Modules:
  0.0 914.8 jit_solution(9450765005196086866)
XLA Ops:
  0.9 37.9 %fusion.15 = (f32[2048,1024]{0,1:T(8,128)}, f32[2048,1024]{0,1:T(8,128)}) fusion(s32[1024]{0:T(1024)} %param.9), kind=kLoop, calls=%fused_computation.35 | loop fusion | flops 31457280 | bytes 16781312 | tf_op jit(solution)/shard_map/cos | solution.py:29
  38.9 7.9 reshape.40
  46.8 11.8 %maximum_multiply_fusion = f32[2048,2048]{0,1:T(8,128)} fusion(f32[2048,1024]{0,1:T(8,128)} %get-tuple-element.70, f32[2048,1024]{0,1:T(8,128)} %get-tuple-element.69), kind=kLoop, calls=%fused_computation.5 | loop fusion | flops 8388608 | bytes 33554432 | tf_op jit(solution)/shard_map/div | solution.py:29
  58.5 63.8 %convert_bitcast_fusion = bf16[4,2,256,1024]{3,2,1,0:T(8,128)(2,1)} fusion(f32[2,1024,2048,1]{2,1,0,3:T(8,128)} %bitcast.99, f32[4,259,2048]{2,1,0:T(8,128)} %reshape.40, f32[2048]{0:T(1024)S(1)} %bitcast.103, f32[2048]{0:T(1024)S(1)} %bitcast.104, f32[2048]{0:T(1024)S(1)} %bitcast.102, f32[2048]{0:T(1024)S(1)} %bitcast.101), kind=kOutput, calls=%fused_computation.34 | convolution fusion | flops 51556384768 | bytes 54558720 | tf_op jit(solution)/shard_map/dot_general | solution.py:43
  122.3 7.7 reshape_reshape.3
  130.0 11.1 %constant_dynamic-slice_fusion.1 = (bf16[4,2,256,4,1,128]{5,4,3,2,1,0:T(2,128)(2,1)}, bf16[4,2,256,4,1,128]{5,4,3,2,1,0:T(2,128)(2,1)S(1)}) fusion(bf16[4,2,256,4,2,128]{5,4,3,2,1,0:T(2,128)(2,1)} %reshape_reshape.3, s32[]{:T(128)S(6)} %select_n.81, s32[]{:T(128)S(6)} %select_n.82), kind=kLoop, calls=%fused_computation.61 | loop fusion | bytes 8388616 | tf_op jit(solution)/shard_map/jit(dynamic_index_in_dim)/dynamic_slice | solution.py:65
  143.4 45.7 %collective-permute-done.1 = bf16[4,2,256,4,128]{4,2,3,1,0:T(8,128)(2,1)} collective-permute-done((bf16[4,2,256,4,128]{4,2,3,1,0:T(8,128)(2,1)S(1)}, bf16[4,2,256,4,128]{4,2,3,1,0:T(8,128)(2,1)}, u32[]{:S(2)}, u32[]{:S(2)}) %collective-permute-start.1) | collective-permute-done | bytes 2097184 | tf_op jit(solution)/shard_map/ppermute | solution.py:15
  198.3 44.9 %collective-permute-done.2 = bf16[8,2,256,2,128]{4,2,3,1,0:T(8,128)(2,1)} collective-permute-done((bf16[8,2,256,2,128]{4,2,3,1,0:T(8,128)(2,1)S(1)}, bf16[8,2,256,2,128]{4,2,3,1,0:T(8,128)(2,1)}, u32[]{:S(2)}, u32[]{:S(2)}) %collective-permute-start.2) | collective-permute-done | bytes 2097184 | tf_op jit(solution)/shard_map/ppermute | solution.py:15
  250.7 44.2 %collective-permute-done.3 = bf16[16,2,256,1,128]{4,2,3,1,0:T(8,128)(2,1)} collective-permute-done((bf16[16,2,256,1,128]{4,2,3,1,0:T(8,128)(2,1)}, bf16[16,2,256,1,128]{4,2,3,1,0:T(8,128)(2,1)}, u32[]{:S(2)}, u32[]{:S(2)}) %collective-permute-start.3) | collective-permute-done | bytes 2097184 | tf_op jit(solution)/shard_map/ppermute | solution.py:15
  299.6 5.2 gather_fusion
  304.9 7.9 copy.23
  312.8 4.8 bitcast_select_fusion
  320.3 7.9 copy.21
  328.2 4.8 multiply_bitcast_fusion.3
  346.4 559.6 %while.12 = (s32[]{:T(128)}, bf16[32,512,128]{1,0,2:T(8,128)(2,1)}, f32[8,2,32,32,128]{4,3,2,0,1:T(8,128)}, bf16[32,512,128]{1,0,2:T(8,128)(2,1)}, bf16[32,512,128]{1,0,2:T(8,128)(2,1)}, /*index=5*/s32[]{:T(128)}) while((s32[]{:T(128)}, bf16[32,512,128]{1,0,2:T(8,128)(2,1)}, f32[8,2,32,32,128]{4,3,2,0,1:T(8,128)}, ...), condition=%wide.region_1.2_spmd, body=%wide.region_0.1_spmd.sunk | while | flops 268959744 | bytes 47186040 | solution.py:104
  346.4 51.9 %collective-permute-done = bf16[32,512,128]{1,0,2:T(8,128)(2,1)} collective-permute-done((bf16[32,512,128]{1,0,2:T(8,128)(2,1)}, bf16[32,512,128]{1,0,2:T(8,128)(2,1)}, u32[]{:S(2)}, u32[]{:S(2)}) %collective-permute-start) | collective-permute-done | bytes 4194336 | tf_op jit(solution)/shard_map/while/body/eval_jaxpr/ppermute | solution.py:21
  398.2 4.7 multiply_bitcast_fusion.6
  404.3 4.7 multiply_bitcast_fusion.7
  411.5 4.8 copy.55
  416.3 51.9 %collective-permute-done = bf16[32,512,128]{1,0,2:T(8,128)(2,1)} collective-permute-done((bf16[32,512,128]{1,0,2:T(8,128)(2,1)}, bf16[32,512,128]{1,0,2:T(8,128)(2,1)}, u32[]{:S(2)}, u32[]{:S(2)}) %collective-permute-start) | collective-permute-done | bytes 4194336 | tf_op jit(solution)/shard_map/while/body/eval_jaxpr/ppermute | solution.py:21
  468.2 4.7 multiply_bitcast_fusion.6
  474.3 4.7 multiply_bitcast_fusion.7
  481.4 4.8 copy.55
  486.2 51.9 %collective-permute-done = bf16[32,512,128]{1,0,2:T(8,128)(2,1)} collective-permute-done((bf16[32,512,128]{1,0,2:T(8,128)(2,1)}, bf16[32,512,128]{1,0,2:T(8,128)(2,1)}, u32[]{:S(2)}, u32[]{:S(2)}) %collective-permute-start) | collective-permute-done | bytes 4194336 | tf_op jit(solution)/shard_map/while/body/eval_jaxpr/ppermute | solution.py:21
  538.1 4.7 multiply_bitcast_fusion.6
  544.2 4.7 multiply_bitcast_fusion.7
  551.4 4.8 copy.55
  556.2 51.9 %collective-permute-done = bf16[32,512,128]{1,0,2:T(8,128)(2,1)} collective-permute-done((bf16[32,512,128]{1,0,2:T(8,128)(2,1)}, bf16[32,512,128]{1,0,2:T(8,128)(2,1)}, u32[]{:S(2)}, u32[]{:S(2)}) %collective-permute-start) | collective-permute-done | bytes 4194336 | tf_op jit(solution)/shard_map/while/body/eval_jaxpr/ppermute | solution.py:21
  608.1 4.7 multiply_bitcast_fusion.6
  614.2 4.7 multiply_bitcast_fusion.7
  621.3 4.8 copy.55
  626.1 51.9 %collective-permute-done = bf16[32,512,128]{1,0,2:T(8,128)(2,1)} collective-permute-done((bf16[32,512,128]{1,0,2:T(8,128)(2,1)}, bf16[32,512,128]{1,0,2:T(8,128)(2,1)}, u32[]{:S(2)}, u32[]{:S(2)}) %collective-permute-start) | collective-permute-done | bytes 4194336 | tf_op jit(solution)/shard_map/while/body/eval_jaxpr/ppermute | solution.py:21
  678.0 4.7 multiply_bitcast_fusion.6
  684.1 4.7 multiply_bitcast_fusion.7
  691.3 4.8 copy.55
  696.1 51.9 %collective-permute-done = bf16[32,512,128]{1,0,2:T(8,128)(2,1)} collective-permute-done((bf16[32,512,128]{1,0,2:T(8,128)(2,1)}, bf16[32,512,128]{1,0,2:T(8,128)(2,1)}, u32[]{:S(2)}, u32[]{:S(2)}) %collective-permute-start) | collective-permute-done | bytes 4194336 | tf_op jit(solution)/shard_map/while/body/eval_jaxpr/ppermute | solution.py:21
  747.9 4.7 multiply_bitcast_fusion.6
  754.1 4.7 multiply_bitcast_fusion.7
  761.2 4.8 copy.55
  766.0 51.9 %collective-permute-done = bf16[32,512,128]{1,0,2:T(8,128)(2,1)} collective-permute-done((bf16[32,512,128]{1,0,2:T(8,128)(2,1)}, bf16[32,512,128]{1,0,2:T(8,128)(2,1)}, u32[]{:S(2)}, u32[]{:S(2)}) %collective-permute-start) | collective-permute-done | bytes 4194336 | tf_op jit(solution)/shard_map/while/body/eval_jaxpr/ppermute | solution.py:21
  817.9 4.7 multiply_bitcast_fusion.6
  824.0 4.7 multiply_bitcast_fusion.7
  831.2 4.8 copy.55
  835.9 51.9 %collective-permute-done = bf16[32,512,128]{1,0,2:T(8,128)(2,1)} collective-permute-done((bf16[32,512,128]{1,0,2:T(8,128)(2,1)}, bf16[32,512,128]{1,0,2:T(8,128)(2,1)}, u32[]{:S(2)}, u32[]{:S(2)}) %collective-permute-start) | collective-permute-done | bytes 4194336 | tf_op jit(solution)/shard_map/while/body/eval_jaxpr/ppermute | solution.py:21
  887.8 4.7 multiply_bitcast_fusion.6
  893.9 4.7 multiply_bitcast_fusion.7
  901.2 4.8 copy.55
  906.0 8.9 maximum_bitcast_fusion.1
  (69 shorter events, 71.7 us)
Async XLA Ops:
  141.7 47.4 %collective-permute-start.1 = (bf16[4,2,256,4,128]{4,2,3,1,0:T(8,128)(2,1)S(1)}, bf16[4,2,256,4,128]{4,2,3,1,0:T(8,128)(2,1)}, u32[]{:S(2)}, u32[]{:S(2)}) collective-permute-start(bf16[4,2,256,4,128]{4,2,3,1,0:T(8,128)(2,1)S(1)} %bitcast.100), channel_id=1, source_target_pairs={{0,1},{1,0},{2,3},{3,2},{4,5},{5,4},{6,7},{7,6},{8,9},{9,8},{10,11... | collective-permute-start | bytes 6291464 | tf_op jit(solution)/shard_map/ppermute | solution.py:15
  192.8 2.0 copy-start.2
  194.9 48.2 %collective-permute-start.2 = (bf16[8,2,256,2,128]{4,2,3,1,0:T(8,128)(2,1)S(1)}, bf16[8,2,256,2,128]{4,2,3,1,0:T(8,128)(2,1)}, u32[]{:S(2)}, u32[]{:S(2)}) collective-permute-start(bf16[8,2,256,2,128]{4,2,3,1,0:T(8,128)(2,1)S(1)} %dynamic-slice_bitcast_fusion), channel_id=1, source_target_pairs={{0,2},{1,3},{2,0},{3,1},{4,6},{5,7},{6,4},{7,5},{8,10},{9,11},{10,... | collective-permute-start | bytes 6291464 | tf_op jit(solution)/shard_map/ppermute | solution.py:15
  245.7 1.3 copy-start.1
  245.7 5.0 copy-start.6
  248.5 46.4 %collective-permute-start.3 = (bf16[16,2,256,1,128]{4,2,3,1,0:T(8,128)(2,1)}, bf16[16,2,256,1,128]{4,2,3,1,0:T(8,128)(2,1)}, u32[]{:S(2)}, u32[]{:S(2)}) collective-permute-start(bf16[16,2,256,1,128]{4,2,3,1,0:T(8,128)(2,1)} %fusion.22), channel_id=1, source_target_pairs={{0,4},{1,5},{2,6},{3,7},{4,0},{5,1},{6,2},{7,3},{8,12},{9,13},{10,... | collective-permute-start | bytes 6291464 | tf_op jit(solution)/shard_map/ppermute | solution.py:15
  312.8 4.8 copy-start.3
  328.2 4.8 copy-start
  328.2 5.3 copy-start.4
  328.2 5.9 copy-start.5
  346.4 51.9 %collective-permute-start = (bf16[32,512,128]{1,0,2:T(8,128)(2,1)}, bf16[32,512,128]{1,0,2:T(8,128)(2,1)}, u32[]{:S(2)}, u32[]{:S(2)}) collective-permute-start(bf16[32,512,128]{1,0,2:T(8,128)(2,1)} %get-tuple-element.109), channel_id=1, source_target_pairs={{0,8},{8,16},{16,24},{24,32},{32,40},{40,48},{48,56},{56,64},{64,7... | collective-permute-start | bytes 12582920 | tf_op jit(solution)/shard_map/while/body/eval_jaxpr/ppermute | solution.py:21
  416.3 51.9 %collective-permute-start = (bf16[32,512,128]{1,0,2:T(8,128)(2,1)}, bf16[32,512,128]{1,0,2:T(8,128)(2,1)}, u32[]{:S(2)}, u32[]{:S(2)}) collective-permute-start(bf16[32,512,128]{1,0,2:T(8,128)(2,1)} %get-tuple-element.109), channel_id=1, source_target_pairs={{0,8},{8,16},{16,24},{24,32},{32,40},{40,48},{48,56},{56,64},{64,7... | collective-permute-start | bytes 12582920 | tf_op jit(solution)/shard_map/while/body/eval_jaxpr/ppermute | solution.py:21
  486.2 51.9 %collective-permute-start = (bf16[32,512,128]{1,0,2:T(8,128)(2,1)}, bf16[32,512,128]{1,0,2:T(8,128)(2,1)}, u32[]{:S(2)}, u32[]{:S(2)}) collective-permute-start(bf16[32,512,128]{1,0,2:T(8,128)(2,1)} %get-tuple-element.109), channel_id=1, source_target_pairs={{0,8},{8,16},{16,24},{24,32},{32,40},{40,48},{48,56},{56,64},{64,7... | collective-permute-start | bytes 12582920 | tf_op jit(solution)/shard_map/while/body/eval_jaxpr/ppermute | solution.py:21
  556.2 51.9 %collective-permute-start = (bf16[32,512,128]{1,0,2:T(8,128)(2,1)}, bf16[32,512,128]{1,0,2:T(8,128)(2,1)}, u32[]{:S(2)}, u32[]{:S(2)}) collective-permute-start(bf16[32,512,128]{1,0,2:T(8,128)(2,1)} %get-tuple-element.109), channel_id=1, source_target_pairs={{0,8},{8,16},{16,24},{24,32},{32,40},{40,48},{48,56},{56,64},{64,7... | collective-permute-start | bytes 12582920 | tf_op jit(solution)/shard_map/while/body/eval_jaxpr/ppermute | solution.py:21
  626.1 51.9 %collective-permute-start = (bf16[32,512,128]{1,0,2:T(8,128)(2,1)}, bf16[32,512,128]{1,0,2:T(8,128)(2,1)}, u32[]{:S(2)}, u32[]{:S(2)}) collective-permute-start(bf16[32,512,128]{1,0,2:T(8,128)(2,1)} %get-tuple-element.109), channel_id=1, source_target_pairs={{0,8},{8,16},{16,24},{24,32},{32,40},{40,48},{48,56},{56,64},{64,7... | collective-permute-start | bytes 12582920 | tf_op jit(solution)/shard_map/while/body/eval_jaxpr/ppermute | solution.py:21
  696.1 51.9 %collective-permute-start = (bf16[32,512,128]{1,0,2:T(8,128)(2,1)}, bf16[32,512,128]{1,0,2:T(8,128)(2,1)}, u32[]{:S(2)}, u32[]{:S(2)}) collective-permute-start(bf16[32,512,128]{1,0,2:T(8,128)(2,1)} %get-tuple-element.109), channel_id=1, source_target_pairs={{0,8},{8,16},{16,24},{24,32},{32,40},{40,48},{48,56},{56,64},{64,7... | collective-permute-start | bytes 12582920 | tf_op jit(solution)/shard_map/while/body/eval_jaxpr/ppermute | solution.py:21
  766.0 51.9 %collective-permute-start = (bf16[32,512,128]{1,0,2:T(8,128)(2,1)}, bf16[32,512,128]{1,0,2:T(8,128)(2,1)}, u32[]{:S(2)}, u32[]{:S(2)}) collective-permute-start(bf16[32,512,128]{1,0,2:T(8,128)(2,1)} %get-tuple-element.109), channel_id=1, source_target_pairs={{0,8},{8,16},{16,24},{24,32},{32,40},{40,48},{48,56},{56,64},{64,7... | collective-permute-start | bytes 12582920 | tf_op jit(solution)/shard_map/while/body/eval_jaxpr/ppermute | solution.py:21
  835.9 51.9 %collective-permute-start = (bf16[32,512,128]{1,0,2:T(8,128)(2,1)}, bf16[32,512,128]{1,0,2:T(8,128)(2,1)}, u32[]{:S(2)}, u32[]{:S(2)}) collective-permute-start(bf16[32,512,128]{1,0,2:T(8,128)(2,1)} %get-tuple-element.109), channel_id=1, source_target_pairs={{0,8},{8,16},{16,24},{24,32},{32,40},{40,48},{48,56},{56,64},{64,7... | collective-permute-start | bytes 12582920 | tf_op jit(solution)/shard_map/while/body/eval_jaxpr/ppermute | solution.py:21
where the time goes:
time: 916 us; the launch traced here: 915 us
  waiting for transfers between devices  550 us (60%)
  matrix products  146 us (16%)
  local copies, waits for them, and re-layouts  121 us (13%)
  other arithmetic  90.2 us (10%)
    ppermute x8, waiting for transfers between devices, passed_along(): return lax.ppermute(value, axis, pairs)  415 us
    ppermute x3, waiting for transfers between devices, from_partner(): return lax.ppermute(value, axis, pairs)  135 us
    dot_general x1, matrix products, filter_bank(): jnp.dot(filtered.reshape(input_count * SPECTRA, 2 * channel_count), dft_t...  63.8 us
    dot_general x9, matrix products, correlate(): jnp.einsum('jtc,itc->jic', partner, plain, preferred_element_type=jnp.flo...  42.4 us
    dot_general x9, matrix products, correlate(): jnp.einsum('jtc,itc->jic', partner, rotated, preferred_element_type=jnp.f...  40.1 us
    while x8, local copies, waits for them, and re-layouts  38.3 us
    cos x1, other arithmetic, make_table(): jnp.cos(phase_arg)  37.9 us
    another operation x18, local copies, waits for them, and re-layouts, correlate(): return jnp.stack([vis_real, vis_imag])  27 us
  transfers between devices with their start and end apart: 11, of which 11 were waited for; matrix products, arithmetic and copies ran while one was open for 0% of the time, Pallas kernels for 0%

commit v1 on v0

v1 whole, which is shorter than its diff:
```python
import math

import numpy as np
import jax
import jax.numpy as jnp
from jax import lax
from jax.sharding import PartitionSpec as P

TAPS = 4
SPECTRA = 256


def phase_table(chans, rows, period):
    sample_index = jnp.arange(rows, dtype=jnp.int32)
    product = sample_index[:, None] * chans[None, :] % period
    phase_arg = product.astype(jnp.float32) * (math.pi / (period // 2))
    return jnp.cos(phase_arg), jnp.sin(phase_arg)


def make_table(chans):
    channel_count = chans.shape[0]
    period = 2 * channel_count
    inner_rows = 64
    outer_rows = period // inner_rows
    inner_cos, inner_sin = phase_table(chans, inner_rows, period)
    outer_chans = chans * inner_rows % period
    outer_cos, outer_sin = phase_table(outer_chans, outer_rows, period)
    cos = outer_cos[:, None, :] * inner_cos[None] - outer_sin[:, None, :] * inner_sin[None]
    sin = outer_sin[:, None, :] * inner_cos[None] + outer_cos[:, None, :] * inner_sin[None]
    scale = 1.0 / math.sqrt(channel_count)
    table = jnp.stack([cos * scale, -sin * scale], axis=-1)
    return table.reshape(period, 2 * channel_count)


def per_device(raw_voltages, filter_taps, input_order, chan_order):
    n_blk = lax.axis_size("blk")
    n_freq = lax.axis_size("freq")
    n_dev = n_blk * n_freq
    channel_count = chan_order.shape[0]
    width = channel_count // n_freq
    chunk = width // n_blk
    steps = n_blk // 2 + 1
    tile = input_order.shape[0]
    local_inputs = raw_voltages.shape[0]
    frame = 2 * channel_count

    dest_b = np.arange(n_blk)[:, None, None]
    dest_f = np.arange(n_freq)[None, :, None]
    within = np.arange(chunk)[None, None, :]
    position = (dest_f * width + dest_b * chunk + within).reshape(-1)
    table = make_table(chan_order[position])

    frames = raw_voltages.astype(jnp.float32).reshape(local_inputs, SPECTRA + TAPS - 1, frame)
    filtered = filter_taps[0] * frames[:, 0:SPECTRA]
    for tap_index in range(1, TAPS):
        filtered = filtered + filter_taps[tap_index] * frames[:, tap_index : tap_index + SPECTRA]
    spectra = jnp.dot(
        filtered.reshape(local_inputs * SPECTRA, frame),
        table,
        precision=lax.Precision.HIGHEST,
    ).astype(jnp.bfloat16)
    spectra = spectra.reshape(local_inputs, SPECTRA, n_dev, chunk, 2).transpose(2, 3, 0, 4, 1)

    gathered = lax.all_to_all(spectra, ("blk", "freq"), 0, 0, tiled=True)
    total_inputs = n_dev * local_inputs
    gathered = gathered.transpose(1, 0, 2, 3, 4).reshape(chunk, total_inputs, 2, SPECTRA)

    slot_order = lax.all_gather(input_order, "blk", tiled=True)
    slotted = jnp.take(gathered, slot_order, axis=1)
    plain = slotted.reshape(chunk, total_inputs, 2 * SPECTRA)
    rotated = jnp.concatenate([slotted[:, :, 1], -slotted[:, :, 0]], axis=2)

    scale = 1.0 / SPECTRA
    doubled = jnp.concatenate([plain, plain], axis=1)
    rows = steps * tile
    blocks = []
    for own in range(n_blk):
        start = (own - steps + 1) % n_blk * tile
        partners = doubled[:, start : start + rows]
        mine = jnp.concatenate(
            [plain[:, own * tile : (own + 1) * tile], rotated[:, own * tile : (own + 1) * tile]],
            axis=1,
        )
        blocks.append(
            jnp.einsum("kpt,kit->kpi", partners, mine, preferred_element_type=jnp.float32)
        )
    banded = jnp.stack(blocks).reshape(n_blk, chunk, steps, tile, 2, tile)[:, :, ::-1]
    banded = banded.transpose(0, 4, 2, 3, 1, 5).reshape(n_blk, 2, steps, tile, chunk * tile) * scale

    returned = lax.all_to_all(banded, "blk", 0, 0, tiled=True)
    returned = returned.reshape(n_blk, 2, steps, tile, chunk, tile)
    return returned.transpose(1, 2, 3, 5, 0, 4).reshape(2, steps, tile, tile, n_blk * chunk)


def solution(mesh):
    placed = (P(("blk", "freq"), None), P(), P("blk"), P())
    return jax.shard_map(
        per_device,
        mesh=mesh,
        in_specs=placed,
        out_specs=P(None, None, None, "blk", "freq"),
        check_vma=False,
    )
```

time: 916 us -> 709 us (0.77)
  the two profiles are of different devices: /device:TPU:0 before, /device:TPU:1 now
where the time goes in v1:
time: 709 us; the launch traced here: 696 us
  local copies, waits for them, and re-layouts  315 us (44%)
  blocking collectives  126 us (18%)
  matrix products  111 us (16%)
  other arithmetic  83.6 us (12%)
  waiting for transfers between devices  51.2 us (7%)
  starting transfers between devices  7.96 us (1%)
    all_to_all x1, blocking collectives, per_device(): returned = lax.all_to_all(banded, 'blk', 0, 0, tiled=True)  112 us
    mul x2, local copies, waits for them, and re-layouts, per_device(): banded.transpose(0, 4, 2, 3, 1, 5)  66.6 us
    another operation x17, local copies, waits for them, and re-layouts, per_device(): jnp.stack(blocks).reshape(n_blk, chunk, steps, tile, 2, tile)[:, :, ::-1]  60.5 us
    dot_general x1, matrix products, per_device(): jnp.dot(filtered.reshape(local_inputs * SPECTRA, frame), table, precision...  56.5 us
    dot_general x16, matrix products, per_device(): jnp.einsum('kpt,kit->kpi', partners, mine, preferred_element_type=jnp.flo...  54 us
    all_to_all x1, waiting for transfers between devices, per_device(): gathered = lax.all_to_all(spectra, ('blk', 'freq'), 0, 0, tiled=True)  51.2 us
    reshape x2, local copies, waits for them, and re-layouts, per_device(): returned.transpose(1, 2, 3, 5, 0, 4)  51.1 us
    mul x1, other arithmetic, per_device(): banded.transpose(0, 4, 2, 3, 1, 5)  33.4 us
  transfers between devices with their start and end apart: 1, of which 1 were waited for; matrix products, arithmetic and copies ran while one was open for 0% of the time, Pallas kernels for 0%

profile of v1, /device:TPU:1, one launch (start us, length us, event | category | flops | bytes accessed | tf_op | source)
XLA Modules:
  0.0 695.7 jit_solution(13180381505218530336)
XLA Ops:
  2.8 13.4 %all-reduce = s32[512]{0:T(512)S(1)} all-reduce(s32[512]{0:T(512)S(1)} %dynamic-update-slice), channel_id=1, replica_groups=mesh['blk'=16,'freq'=8] {'blk'}, use_global_device_ids=true, to_apply=%add | all-reduce | flops 512 | bytes 4096
  16.8 4.5 gather_fusion
  23.5 7.9 %reshape.222 = f32[4,259,2048]{2,1,0:T(8,128)} reshape(bf16[4,530432]{1,0:T(4,128)(2,1)} %param.6) | data formatting | bytes 12730368 | tf_op jit(solution)/shard_map/reshape | solution.py:53
  33.5 8.9 %subtract_multiply_fusion = (f32[32,64,1024,1]{1,0,3,2:T(8,128)S(1)}, f32[32,64,1024,1]{1,0,3,2:T(8,128)S(1)}) fusion(f32[64,1024]{0,1:T(8,128)S(1)} %get-tuple-element.47, f32[32,1024]{0,1:T(8,128)S(1)} %get-tuple-element.45, f32[64,1024]{0,1:T(8,128)S(1)} %get-tuple-element.46, f32[32,1024]{0,1:T(8,128)S(1)} %get-tuple-element.44), kind=kLoop, calls=%fused_computation.6 | loop fusion | flops 18874368 | bytes 17563648 | tf_op jit(solution)/shard_map/mul | solution.py:31
  42.5 11.6 %pad_maximum_fusion = f32[32,64,1024,2]{1,0,3,2:T(8,128)} fusion(f32[32,64,1024,1]{1,0,3,2:T(8,128)S(1)} %get-tuple-element.39, f32[32,64,1024,1]{1,0,3,2:T(8,128)S(1)} %get-tuple-element.38), kind=kLoop, calls=%fused_computation.4 | loop fusion | flops 4194304 | bytes 33554432 | tf_op jit(solution)/shard_map/stack | solution.py:31
  54.0 28.9 %reshape.216 = f32[2048,2048]{0,1:T(8,128)} reshape(f32[32,64,1024,2]{1,0,3,2:T(8,128)} %pad_maximum_fusion) | data formatting | bytes 33554432 | tf_op jit(solution)/shard_map/reshape | solution.py:32
  82.9 14.3 %fusion = f32[4,256,2048]{2,1,0:T(8,128)S(1)} fusion(f32[4,259,2048]{2,1,0:T(8,128)} %reshape.222, f32[2048]{0:T(1024)S(1)} %bitcast.41, f32[2048]{0:T(1024)S(1)} %bitcast.42, f32[2048]{0:T(1024)S(1)} %bitcast.40, f32[2048]{0:T(1024)S(1)} %bitcast.39), kind=kLoop, calls=%fused_computation.52 | loop fusion | flops 14680064 | bytes 41975808 | tf_op jit(solution)/shard_map/add | solution.py:56
  97.2 56.5 %convolution_convert_fusion = bf16[1024,2048]{1,0:T(8,128)(2,1)} fusion(f32[1024,2048]{1,0:T(8,128)S(1)} %bitcast.38, f32[2048,2048]{0,1:T(8,128)} %reshape.216), kind=kOutput, calls=%fused_computation.60 | convolution fusion | flops 51541704704 | bytes 29360128 | tf_op jit(solution)/shard_map/dot_general | solution.py:57
  153.7 6.4 copy.8
  160.1 7.8 %reshape.217 = bf16[4,256,128,8,2]{1,0,4,3,2:T(4,128)(2,1)} reshape(bf16[1024,2048]{0,1:T(8,128)(2,1)} %copy.8) | data formatting | bytes 8388608 | tf_op jit(solution)/shard_map/reshape | solution.py:62
  168.0 8.0 %all-to-all-start = ((bf16[128,8,4,2,256]{4,2,3,1,0:T(4,128)(2,1)}), bf16[128,8,4,2,256]{4,2,3,1,0:T(4,128)(2,1)}, u32[]{:S(2)}, u32[]{:S(2)}) async-start(bf16[128,8,4,2,256]{4,2,3,1,0:T(4,128)(2,1)} %bitcast.37), calls=%async_computation | async-start | bytes 8388608 | tf_op jit(solution)/shard_map/all_to_all | solution.py:64
  175.9 51.2 %all-to-all-done = bf16[128,8,4,2,256]{4,2,3,1,0:T(4,128)(2,1)} async-done(((bf16[128,8,4,2,256]{4,2,3,1,0:T(4,128)(2,1)}), bf16[128,8,4,2,256]{4,2,3,1,0:T(4,128)(2,1)}, u32[]{:S(2)}, u32[]{:S(2)}) %all-to-all-start) | async-done | bytes 4194336 | tf_op jit(solution)/shard_map/all_to_all | solution.py:64
  227.2 5.7 copy.9
  232.8 5.1 gather_fusion.1
  238.0 5.0 bitcast_select_fusion
  247.4 5.2 copy.11
  252.7 7.6 %gather.11 = bf16[8,512,512]{2,1,0:T(8,128)(2,1)} reshape(bf16[8,512,2,256]{3,2,1,0:T(2,128)(2,1)} %copy.11) | data formatting | bytes 8388608 | tf_op jit(solution)/shard_map/jit(_take)/gather | solution.py:69
  267.8 4.0 stack.57
  278.7 3.6 stack.58
  282.4 3.5 fusion.34
  285.9 3.6 stack.59
  289.5 3.5 fusion.32
  293.0 3.6 stack.60
  300.1 3.6 stack.61
  307.2 3.6 stack.62
  310.8 3.5 fusion.40
  314.3 3.6 stack.63
  317.9 3.5 fusion.26
  321.4 3.8 stack.64
  328.7 3.6 stack.65
  332.3 3.5 fusion.22
  335.9 3.6 stack.66
  339.5 3.5 fusion.20
  343.0 3.6 stack.67
  346.5 3.5 fusion.18
  350.0 3.6 stack.68
  357.1 3.6 stack.69
  360.8 3.5 fusion.14
  364.3 3.8 stack.70
  371.5 3.6 stack.71
  378.6 3.7 stack.72
  408.9 33.4 %multiply_bitcast_fusion = f32[16,2,9,32,8,32]{5,1,3,2,4,0:T(2,128)} fusion(f32[16,8,9,32,2,32]{5,4,3,2,1,0:T(2,128)} %constant_dynamic-update-slice_fusion), kind=kLoop, calls=%fused_computation.3 | loop fusion | flops 2359296 | bytes 18874368 | tf_op jit(solution)/shard_map/mul | solution.py:88
  442.2 40.5 %copy.28 = f32[16,2,9,32,8,32]{5,4,3,2,1,0:T(8,128)} copy(f32[16,2,9,32,8,32]{5,1,3,2,4,0:T(2,128)} %multiply_bitcast_fusion) | data formatting | bytes 18874368 | tf_op jit(solution)/shard_map/mul | solution.py:88
  482.7 26.1 %mul.257 = f32[16,2,9,32,256]{4,3,2,1,0:T(8,128)} reshape(f32[16,2,9,32,8,32]{5,4,3,2,1,0:T(8,128)} %copy.28) | data formatting | bytes 18874368 | tf_op jit(solution)/shard_map/mul | solution.py:88
  508.8 112.4 %all_to_all.10 = f32[16,2,9,32,256]{4,3,2,1,0:T(8,128)} all-to-all(f32[16,2,9,32,256]{4,3,2,1,0:T(8,128)} %mul.257), channel_id=1, replica_groups=mesh['blk'=16,'freq'=8] {'blk'}, dimensions={0} | all-to-all | bytes 18874368 | tf_op jit(solution)/shard_map/all_to_all | solution.py:90
  621.2 23.0 %reshape.219 = f32[16,2,9,32,8,32]{5,4,3,2,1,0:T(8,128)} reshape(f32[16,2,9,32,256]{4,3,2,1,0:T(8,128)} %all_to_all.10) | data formatting | bytes 18874368 | tf_op jit(solution)/shard_map/reshape | solution.py:91
  644.2 27.8 %copy_bitcast_fusion = f32[2,9,32,32,128]{3,4,2,1,0:T(8,128)} fusion(f32[16,2,9,32,8,32]{5,4,3,2,1,0:T(8,128)} %reshape.219), kind=kLoop, calls=%fused_computation.2 | loop fusion | bytes 18874368 | tf_op jit(solution)/shard_map/reshape | solution.py:92
  672.0 23.3 %copy.30 = f32[2,9,32,32,128]{4,3,2,1,0:T(8,128)} copy(f32[2,9,32,32,128]{3,4,2,1,0:T(8,128)} %copy_bitcast_fusion) | data formatting | bytes 18874368 | tf_op jit(solution)/shard_map/reshape | solution.py:92
  (113 shorter events, 73.2 us)
Async XLA Ops:
  0.0 16.8 %copy-start = (s32[1024]{0:T(1024)S(1)}, s32[1024]{0:T(1024)}, u32[]{:S(2)}) copy-start(s32[1024]{0:T(1024)} %param.9) | copy-start | bytes 12292
  23.5 7.9 %copy-start.36 = (f32[4,2048]{1,0:T(4,128)S(1)}, f32[4,2048]{1,0:T(4,128)}, u32[]{:S(2)}) copy-start(f32[4,2048]{1,0:T(4,128)} %param.7) | copy-start | bytes 98308
  168.0 59.2 %all-to-all-start = ((bf16[128,8,4,2,256]{4,2,3,1,0:T(4,128)(2,1)}), bf16[128,8,4,2,256]{4,2,3,1,0:T(4,128)(2,1)}, u32[]{:S(2)}, u32[]{:S(2)}) async-start(bf16[128,8,4,2,256]{4,2,3,1,0:T(4,128)(2,1)} %bitcast.37), calls=%async_computation | async-start | bytes 8388608 | tf_op jit(solution)/shard_map/all_to_all | solution.py:64
  243.3 2.6 copy-start.3
  244.7 2.8 copy-start.2
  262.9 3.1 copy-start.4
  262.9 3.1 copy-start.34
  271.8 3.5 copy-start.33
  271.8 3.5 copy-start.35
  275.3 7.1 %copy-start.32 = (bf16[8,32,512]{2,1,0:T(8,128)(2,1)S(1)}, bf16[8,32,512]{2,1,0:T(8,128)(2,1)}, u32[]{:S(2)}) copy-start(bf16[8,32,512]{2,1,0:T(8,128)(2,1)} %get-tuple-element.24) | copy-start | bytes 786436
  282.4 7.2 %copy-start.31 = (bf16[8,32,512]{2,1,0:T(8,128)(2,1)S(1)}, bf16[8,32,512]{2,1,0:T(8,128)(2,1)}, u32[]{:S(2)}) copy-start(bf16[8,32,512]{2,1,0:T(8,128)(2,1)} %get-tuple-element.25) | copy-start | bytes 786436
  289.5 7.1 %copy-start.30 = (bf16[8,32,512]{2,1,0:T(8,128)(2,1)S(1)}, bf16[8,32,512]{2,1,0:T(8,128)(2,1)}, u32[]{:S(2)}) copy-start(bf16[8,32,512]{2,1,0:T(8,128)(2,1)} %get-tuple-element.26) | copy-start | bytes 786436
  296.6 7.1 %copy-start.29 = (bf16[8,32,512]{2,1,0:T(8,128)(2,1)S(1)}, bf16[8,32,512]{2,1,0:T(8,128)(2,1)}, u32[]{:S(2)}) copy-start(bf16[8,32,512]{2,1,0:T(8,128)(2,1)} %get-tuple-element.27) | copy-start | bytes 786436
  303.7 7.1 %copy-start.28 = (bf16[8,32,512]{2,1,0:T(8,128)(2,1)S(1)}, bf16[8,32,512]{2,1,0:T(8,128)(2,1)}, u32[]{:S(2)}) copy-start(bf16[8,32,512]{2,1,0:T(8,128)(2,1)} %get-tuple-element.28) | copy-start | bytes 786436
  310.8 7.1 %copy-start.27 = (bf16[8,32,512]{2,1,0:T(8,128)(2,1)S(1)}, bf16[8,32,512]{2,1,0:T(8,128)(2,1)}, u32[]{:S(2)}) copy-start(bf16[8,32,512]{2,1,0:T(8,128)(2,1)} %get-tuple-element.29) | copy-start | bytes 786436
  317.9 7.3 %copy-start.26 = (bf16[8,32,512]{2,1,0:T(8,128)(2,1)S(1)}, bf16[8,32,512]{2,1,0:T(8,128)(2,1)}, u32[]{:S(2)}) copy-start(bf16[8,32,512]{2,1,0:T(8,128)(2,1)} %get-tuple-element.31) | copy-start | bytes 786436
  325.2 7.1 %copy-start.25 = (bf16[8,32,512]{2,1,0:T(8,128)(2,1)S(1)}, bf16[8,32,512]{2,1,0:T(8,128)(2,1)}, u32[]{:S(2)}) copy-start(bf16[8,32,512]{2,1,0:T(8,128)(2,1)} %get-tuple-element.32) | copy-start | bytes 786436
  332.3 7.1 %copy-start.23 = (bf16[8,32,512]{2,1,0:T(8,128)(2,1)S(1)}, bf16[8,32,512]{2,1,0:T(8,128)(2,1)}, u32[]{:S(2)}) copy-start(bf16[8,32,512]{2,1,0:T(8,128)(2,1)} %get-tuple-element.33) | copy-start | bytes 786436
  339.5 7.1 %copy-start.22 = (bf16[8,32,512]{2,1,0:T(8,128)(2,1)S(1)}, bf16[8,32,512]{2,1,0:T(8,128)(2,1)}, u32[]{:S(2)}) copy-start(bf16[8,32,512]{2,1,0:T(8,128)(2,1)} %get-tuple-element.34) | copy-start | bytes 786436
  346.5 7.1 %copy-start.21 = (bf16[8,32,512]{2,1,0:T(8,128)(2,1)S(1)}, bf16[8,32,512]{2,1,0:T(8,128)(2,1)}, u32[]{:S(2)}) copy-start(bf16[8,32,512]{2,1,0:T(8,128)(2,1)} %get-tuple-element.35) | copy-start | bytes 786436
  353.6 7.1 %copy-start.20 = (bf16[8,32,512]{2,1,0:T(8,128)(2,1)S(1)}, bf16[8,32,512]{2,1,0:T(8,128)(2,1)}, u32[]{:S(2)}) copy-start(bf16[8,32,512]{2,1,0:T(8,128)(2,1)} %get-tuple-element.30) | copy-start | bytes 786436
  360.8 7.3 %copy-start.24 = (bf16[8,32,512]{2,1,0:T(8,128)(2,1)S(1)}, bf16[8,32,512]{2,1,0:T(8,128)(2,1)}, u32[]{:S(2)}) copy-start(bf16[8,32,512]{2,1,0:T(8,128)(2,1)} %get-tuple-element.6) | copy-start | bytes 786436
  378.6 3.7 copy-start.5
  382.3 2.5 copy-start.6
  382.3 4.2 copy-start.7
  384.9 3.5 copy-start.8
  386.6 3.4 copy-start.9
  388.3 3.4 copy-start.10
  390.0 3.4 copy-start.11
  391.7 3.4 copy-start.12
  393.4 3.5 copy-start.13
  395.1 3.5 copy-start.14
  396.9 3.5 copy-start.15
  398.6 3.5 copy-start.16
  400.4 3.4 copy-start.17
  402.1 3.4 copy-start.18
  403.8 3.3 copy-start.19
  672.0 23.3 %copy-start.1 = (s32[1024]{0:T(1024)S(1)}, s32[1024]{0:T(1024)}, u32[]{:S(2)}) copy-start(s32[1024]{0:T(1024)} %param.9) | copy-start | bytes 12292

commit v2 on v1

v2 whole, which is shorter than its diff:
```python
import math

import numpy as np
import jax
import jax.numpy as jnp
from jax import lax
from jax.sharding import PartitionSpec as P

TAPS = 4
SPECTRA = 256


def phase_table(chans, rows, period):
    sample_index = jnp.arange(rows, dtype=jnp.int32)
    product = sample_index[:, None] * chans[None, :] % period
    phase_arg = product.astype(jnp.float32) * (math.pi / (period // 2))
    return jnp.cos(phase_arg), jnp.sin(phase_arg)


def make_table(chans):
    channel_count = chans.shape[0]
    period = 2 * channel_count
    inner_rows = 64
    outer_rows = period // inner_rows
    inner_cos, inner_sin = phase_table(chans, inner_rows, period)
    outer_chans = chans * inner_rows % period
    outer_cos, outer_sin = phase_table(outer_chans, outer_rows, period)
    scale = 1.0 / math.sqrt(channel_count)
    cos = outer_cos[:, None, :] * inner_cos[None] - outer_sin[:, None, :] * inner_sin[None]
    sin = outer_sin[:, None, :] * inner_cos[None] + outer_cos[:, None, :] * inner_sin[None]
    return (cos * scale).reshape(period, channel_count), (sin * -scale).reshape(period, channel_count)


def per_device(raw_voltages, filter_taps, input_order, chan_order):
    n_blk = lax.axis_size("blk")
    n_freq = lax.axis_size("freq")
    n_dev = n_blk * n_freq
    channel_count = chan_order.shape[0]
    width = channel_count // n_freq
    chunk = width // n_blk
    steps = n_blk // 2 + 1
    tile = input_order.shape[0]
    local_inputs = raw_voltages.shape[0]
    frame = 2 * channel_count

    slot_order = lax.all_gather(input_order.astype(jnp.float32), "blk", tiled=True)

    dest_b = np.arange(n_blk)[:, None, None]
    dest_f = np.arange(n_freq)[None, :, None]
    within = np.arange(chunk)[None, None, :]
    position = (dest_f * width + dest_b * chunk + within).reshape(-1)
    cos_table, sin_table = make_table(chan_order[position])

    frames = raw_voltages.astype(jnp.float32).reshape(local_inputs, SPECTRA + TAPS - 1, frame)
    filtered = filter_taps[0] * frames[:, 0:SPECTRA]
    for tap_index in range(1, TAPS):
        filtered = filtered + filter_taps[tap_index] * frames[:, tap_index : tap_index + SPECTRA]
    filtered = filtered.reshape(local_inputs * SPECTRA, frame)
    parts = [
        jnp.einsum("mc,nm->cn", part, filtered, precision=lax.Precision.HIGH)
        for part in (cos_table, sin_table)
    ]
    spectra = jnp.stack(parts, axis=1).astype(jnp.bfloat16)
    spectra = spectra.reshape(n_dev, chunk, 2, local_inputs, SPECTRA).transpose(0, 1, 3, 2, 4)

    gathered = lax.all_to_all(spectra, ("blk", "freq"), 0, 0, tiled=True)
    total_inputs = n_dev * local_inputs
    gathered = gathered.transpose(1, 0, 2, 3, 4).reshape(chunk, total_inputs, 2, SPECTRA)

    slotted = jnp.take(gathered, slot_order.astype(jnp.int32), axis=1)
    plain = slotted.reshape(chunk, total_inputs, 2 * SPECTRA)
    rotated = jnp.concatenate([slotted[:, :, 1], -slotted[:, :, 0]], axis=2)
    both = jnp.concatenate([plain, rotated], axis=1)

    gram = jnp.einsum("kat,kpt->kap", both, plain, preferred_element_type=jnp.float32)
    gram = gram.reshape(chunk, 2, n_blk, tile, total_inputs)
    doubled = jnp.concatenate([gram, gram], axis=-1)
    rows = steps * tile
    blocks = []
    for own in range(n_blk):
        start = (own - steps + 1) % n_blk * tile
        blocks.append(doubled[:, :, own, :, start : start + rows])
    banded = jnp.stack(blocks).transpose(0, 2, 1, 3, 4) * (1.0 / SPECTRA)

    returned = lax.all_to_all(banded, "blk", 0, 0, tiled=True)
    returned = returned.reshape(n_blk, 2, chunk, tile, steps, tile)[:, :, :, :, ::-1]
    return returned.transpose(1, 4, 5, 3, 0, 2).reshape(2, steps, tile, tile, n_blk * chunk)


def solution(mesh):
    placed = (P(("blk", "freq"), None), P(), P("blk"), P())
    return jax.shard_map(
        per_device,
        mesh=mesh,
        in_specs=placed,
        out_specs=P(None, None, None, "blk", "freq"),
        check_vma=False,
    )
```

time: 709 us -> 511 us (0.72)
  local copies, waits for them, and re-layouts: 315 us -> 160 us
  blocking collectives: 126 us -> 219 us
  matrix products: 111 us -> 53.8 us
  waiting for transfers between devices: 51.2 us -> 0.01 us
  other arithmetic: 83.6 us -> 54.9 us
    reshape x5 -> x1, local copies, waits for them, and re-layouts: 111 us -> 23.3 us  [per_device(): returned.transpose(1, 4, 5, 3, 0, 2)]
    mul x2 -> x0, local copies, waits for them, and re-layouts: 66.6 us -> none  [per_device(): banded.transpose(0, 4, 2, 3, 1, 5)]
    unnamed x1, blocking collectives: 13.4 us -> 72.9 us
    another operation x17 -> x1, local copies, waits for them, and re-layouts: 60.5 us -> 1.16 us  [per_device(): banded = jnp.stack(blocks).transpose(0, 2, 1, 3, 4) * (1.0 / SPECTRA)]
    dot_general x17 -> x3, matrix products: 111 us -> 53.8 us  [the longest x2 45.7 us: per_device(): jnp.einsum('mc,nm->cn', part, filtered, precision=lax.Precision.HIGH)]
    all_to_all x1, waiting for transfers between devices: 51.2 us -> 0.01 us  [per_device(): gathered = lax.all_to_all(spectra, ('blk', 'freq'), 0, 0, tiled=True)]
    transpose x1 -> x3, local copies, waits for them, and re-layouts: 5.69 us -> 44.2 us  [the longest x2 39 us: per_device(): returned.transpose(1, 4, 5, 3, 0, 2)]
    all_to_all x1, blocking collectives: 112 us -> 146 us  [per_device(): returned = lax.all_to_all(banded, 'blk', 0, 0, tiled=True)]
  transfers between devices with their start and end apart: 1 -> 1, of which waited for: 1 -> 0; matrix products, arithmetic and copies ran while one was open for 0% -> 0% of each run, Pallas kernels for 0% -> 0%
where the time goes in v2:
time: 511 us; the launch traced here: 501 us
  blocking collectives  219 us (43%)
  local copies, waits for them, and re-layouts  160 us (31%)
  other arithmetic  54.9 us (11%)
  matrix products  53.8 us (11%)
  starting transfers between devices  11.9 us (2%)
    all_to_all x1, blocking collectives, per_device(): returned = lax.all_to_all(banded, 'blk', 0, 0, tiled=True)  146 us
    unnamed x1, blocking collectives  72.9 us
    dot_general x2, matrix products, per_device(): jnp.einsum('mc,nm->cn', part, filtered, precision=lax.Precision.HIGH)  45.7 us
    transpose x2, local copies, waits for them, and re-layouts, per_device(): returned.transpose(1, 4, 5, 3, 0, 2)  39 us
    reshape x1, local copies, waits for them, and re-layouts, per_device(): returned.transpose(1, 4, 5, 3, 0, 2)  23.3 us
    all_to_all x1, local copies, waits for them, and re-layouts, per_device(): returned = lax.all_to_all(banded, 'blk', 0, 0, tiled=True)  22.4 us
    gather x3, local copies, waits for them, and re-layouts, per_device(): slotted = jnp.take(gathered, slot_order.astype(jnp.int32), axis=1)  19.1 us
    dot_general x2, local copies, waits for them, and re-layouts, per_device(): jnp.einsum('mc,nm->cn', part, filtered, precision=lax.Precision.HIGH)  18.4 us
  transfers between devices with their start and end apart: 1, of which 0 were waited for; matrix products, arithmetic and copies ran while one was open for 0% of the time, Pallas kernels for 0%

profile of v2, /device:TPU:1, one launch (start us, length us, event | category | flops | bytes accessed | tf_op | source)
XLA Modules:
  0.0 500.9 jit_solution(6906827211873966020)
XLA Ops:
  0.0 0.7 broadcast_clamp_fusion
  0.7 4.5 gather_fusion
  5.3 1.0 fusion.47
  6.3 0.9 fusion.55
  7.2 0.5 fusion.52
  7.8 7.9 %reshape.201 = f32[4,259,2048]{2,1,0:T(8,128)} reshape(bf16[4,530432]{1,0:T(4,128)(2,1)} %param.6) | data formatting | bytes 12730368 | tf_op jit(solution)/shard_map/reshape | solution.py:54
  15.6 6.9 %subtract_multiply_fusion = (f32[32,64,1024]{2,1,0:T(8,128)}, f32[32,64,1024]{2,1,0:T(8,128)}) fusion(f32[64,1024]{1,0:T(8,128)S(1)} %get-tuple-element.16, f32[32,1024]{1,0:T(8,128)S(1)} %get-tuple-element.14, f32[64,1024]{1,0:T(8,128)S(1)} %get-tuple-element.15, f32[32,1024]{1,0:T(8,128)S(1)} %get-tuple-element.13), kind=kLoop, calls=%fused_computation.25 | loop fusion | flops 16777216 | bytes 17563648 | tf_op jit(solution)/shard_map/mul | solution.py:31
  22.6 9.2 %copy.55 = f32[1024,2048]{1,0:T(8,128)} copy(f32[1024,2048]{0,1:T(8,128)} %bitcast.132) | data formatting | bytes 16777216 | tf_op jit(solution)/shard_map/mc,nm->cn/dot_general | solution.py:60
  31.8 9.2 %copy.57 = f32[1024,2048]{1,0:T(8,128)} copy(f32[1024,2048]{0,1:T(8,128)} %bitcast.131) | data formatting | bytes 16777216 | tf_op jit(solution)/shard_map/mc,nm->cn/dot_general | solution.py:60
  41.0 17.3 %fusion.2 = f32[4,256,2048,1]{2,1,0,3:T(8,128)} fusion(f32[4,259,2048]{2,1,0:T(8,128)} %reshape.201, f32[2048]{0:T(1024)S(1)} %bitcast.139, f32[2048]{0:T(1024)S(1)} %bitcast.140, f32[2048]{0:T(1024)S(1)} %bitcast.138, f32[2048]{0:T(1024)S(1)} %bitcast.137), kind=kLoop, calls=%fused_computation.8 | loop fusion | flops 14680064 | bytes 41975808 | tf_op jit(solution)/shard_map/add | solution.py:57
  58.3 22.8 %convert_bitcast_fusion.1 = bf16[128,8,1,4,256]{4,0,3,1,2:T(8,128)(2,1)S(1)} fusion(f32[4,256,2048,1]{2,1,0,3:T(8,128)} %fusion.2, f32[128,8,2048,1]{2,1,0,3:T(8,128)S(1)} %bitcast.135), kind=kOutput, calls=%fused_computation.33 | convolution fusion | flops 12885950464 | bytes 18874368 | tf_op jit(solution)/shard_map/mc,nm->cn/dot_general | solution.py:60
  81.2 22.8 %convert_bitcast_fusion = bf16[128,8,1,4,256]{4,0,3,1,2:T(8,128)(2,1)S(1)} fusion(f32[4,256,2048,1]{2,1,0,3:T(8,128)} %fusion.2, f32[128,8,2048,1]{2,1,0,3:T(8,128)S(1)} %bitcast.136), kind=kOutput, calls=%fused_computation.32 | convolution fusion | flops 12885950464 | bytes 18874368 | tf_op jit(solution)/shard_map/mc,nm->cn/dot_general | solution.py:60
  104.0 0.4 maximum_bitcast_fusion
  104.4 5.3 %copy.59 = bf16[128,8,4,2,256]{4,2,1,3,0:T(4,128)(2,1)} copy(bf16[128,8,4,2,256]{4,0,2,1,3:T(8,128)(2,1)S(1)} %maximum_bitcast_fusion) | data formatting | bytes 8388608 | tf_op jit(solution)/shard_map/transpose | solution.py:64
  109.7 11.9 %all-to-all-start = ((bf16[128,8,4,2,256]{4,2,1,3,0:T(4,128)(2,1)}), bf16[128,8,4,2,256]{4,2,1,3,0:T(4,128)(2,1)}, u32[]{:S(2)}, u32[]{:S(2)}) async-start(bf16[128,8,4,2,256]{4,2,1,3,0:T(4,128)(2,1)} %copy.59), calls=%async_computation | async-start | bytes 8388608 | tf_op jit(solution)/shard_map/all_to_all | solution.py:66
  121.6 0.7 dynamic-slice
  123.1 72.9 %all-reduce = f32[512]{0:T(512)S(1)} all-reduce(f32[512]{0:T(512)S(1)} %convert_dynamic-update-slice_fusion), channel_id=1, replica_groups=mesh['blk'=16,'freq'=8] {'blk'}, use_global_device_ids=true, to_apply=%add | all-reduce | flops 512 | bytes 4096
  196.1 5.3 %copy.60 = bf16[128,8,4,2,256]{4,1,3,2,0:T(8,128)(2,1)} copy(bf16[128,8,4,2,256]{4,2,1,3,0:T(4,128)(2,1)} %all-to-all-done) | data formatting | bytes 8388608 | tf_op jit(solution)/shard_map/all_to_all | solution.py:66
  201.4 5.1 %gather_fusion.1 = bf16[512,8,2,256]{3,1,2,0:T(8,128)(2,1)} fusion(bf16[8,512,2,256]{3,0,2,1:T(8,128)(2,1)} %bitcast.133, s32[1024]{0:T(1024)S(1)} %pad_clamp_fusion), kind=kCustom, calls=%fused_computation.1 | custom fusion | bytes 8390656 | tf_op jit(solution)/shard_map/jit(_take)/gather | solution.py:70
  206.5 7.5 %copy.62 = bf16[8,512,2,256]{1,3,2,0:T(8,128)(2,1)} copy(bf16[8,512,2,256]{3,0,2,1:T(8,128)(2,1)} %bitcast.130) | data formatting | bytes 8388608 | tf_op jit(solution)/shard_map/jit(_take)/gather | solution.py:70
  214.0 6.5 %copy.63 = bf16[8,512,512]{2,1,0:T(8,128)(2,1)} copy(bf16[8,512,512]{1,2,0:T(8,128)(2,1)} %bitcast.134) | data formatting | bytes 8388608 | tf_op jit(solution)/shard_map/jit(_take)/gather | solution.py:70
  220.5 5.2 %bitcast_select_fusion = bf16[8,512,2,256]{3,1,0,2:T(8,128)(2,1)S(1)} fusion(bf16[512,8,2,256]{3,1,2,0:T(8,128)(2,1)} %gather_fusion.1, pred[512]{0:T(512)(128)(4,1)S(1)} %compare_and_fusion), kind=kLoop, calls=%fused_computation.27 | loop fusion | flops 2097152 | bytes 8389120 | tf_op jit(solution)/shard_map/jit(_take)/select_n | solution.py:70
  225.6 0.5 broadcast_select_fusion
  226.1 0.3 slice_bitcast_fusion
  226.4 8.1 %fusion.5 = f32[8,1024,512]{2,1,0:T(8,128)} fusion(bf16[8,512,512]{2,1,0:T(8,128)(2,1)S(1)} %broadcast_select_fusion, bf16[8,512,256]{2,1,0:T(8,128)(2,1)S(1)} %get-tuple-element.6, bf16[8,512,256]{2,1,0:T(8,128)(2,1)S(1)} %get-tuple-element.5), kind=kOutput, calls=%fused_computation.14 | convolution fusion | flops 4320133120 | bytes 25165824 | tf_op jit(solution)/shard_map/kat,kpt->kap/dot_general | solution.py:75
  234.5 2.2 fusion.36
  236.8 4.1 copy-done.2
  240.8 1.2 fusion.35
  242.1 1.2 fusion.34
  243.3 1.2 fusion.33
  244.5 1.0 fusion.32
  245.5 1.2 fusion.31
  246.7 1.3 fusion.30
  248.0 1.2 fusion.29
  249.2 1.0 fusion.27
  250.2 1.2 fusion.26
  251.3 1.2 fusion.25
  252.6 1.2 fusion.24
  253.8 1.0 fusion.23
  254.8 1.2 fusion.22
  256.0 1.1 fusion.21
  257.1 1.2 fusion.20
  258.3 11.4 %fusion = f32[16,2,8,32,288]{4,3,2,1,0:T(8,128)} fusion(f32[16,8,2,32,288]{4,3,2,1,0:T(8,128)} %fusion.20), kind=kLoop, calls=%fused_computation.5 | loop fusion | flops 2359296 | bytes 18874368 | tf_op jit(solution)/shard_map/mul | solution.py:83
  269.6 146.4 %all_to_all.10 = f32[16,2,8,32,288]{4,3,2,1,0:T(8,128)} all-to-all(f32[16,2,8,32,288]{4,3,2,1,0:T(8,128)} %fusion), channel_id=1, replica_groups=mesh['blk'=16,'freq'=8] {'blk'}, dimensions={0} | all-to-all | bytes 18874368 | tf_op jit(solution)/shard_map/all_to_all | solution.py:85
  416.0 22.4 %copy.65 = f32[16,2,8,32,288]{3,4,2,1,0:T(8,128)} copy(f32[16,2,8,32,288]{4,3,2,1,0:T(8,128)} %all_to_all.10) | data formatting | bytes 18874368 | tf_op jit(solution)/shard_map/all_to_all | solution.py:85
  438.4 14.9 %reverse_bitcast_fusion = f32[2,9,32,32,16,8]{3,2,1,5,0,4:T(8,128)S(1)} fusion(f32[16,2,8,32,9,32]{3,5,4,2,1,0:T(8,128)} %bitcast.128), kind=kLoop, calls=%fused_computation.3 | loop fusion | bytes 18874368 | tf_op jit(solution)/shard_map/transpose | solution.py:87
  453.4 24.0 %copy.88 = f32[2,9,32,32,16,8]{3,5,4,2,1,0:T(8,128)} copy(f32[2,9,32,32,16,8]{3,2,1,5,0,4:T(8,128)S(1)} %reverse_bitcast_fusion) | data formatting | bytes 18874368 | tf_op jit(solution)/shard_map/transpose | solution.py:87
  477.4 23.3 %copy.67 = f32[2,9,32,32,128]{4,3,2,1,0:T(8,128)} copy(f32[2,9,32,32,128]{3,4,2,1,0:T(8,128)} %bitcast.129) | data formatting | bytes 18874368 | tf_op jit(solution)/shard_map/reshape | solution.py:87
  (22 shorter events, 0.2 us)
Async XLA Ops:
  0.0 0.7 copy-start
  41.0 17.3 %copy-start.4 = (f32[1024,2048]{1,0:T(8,128)S(1)}, f32[1024,2048]{1,0:T(8,128)}, u32[]{:S(2)}) copy-start(f32[1024,2048]{1,0:T(8,128)} %copy.55) | copy-start | bytes 25165828
  58.3 22.9 %copy-start.5 = (f32[1024,2048]{1,0:T(8,128)S(1)}, f32[1024,2048]{1,0:T(8,128)}, u32[]{:S(2)}) copy-start(f32[1024,2048]{1,0:T(8,128)} %copy.57) | copy-start | bytes 25165828
  104.4 17.2 %copy-start.7 = (u32[128]{0:T(128)S(1)}, u32[128]{0:T(128)}, u32[]{:S(2)}) copy-start(u32[128]{0:T(128)} %constant.70) | copy-start | bytes 1540
  104.4 18.6 %copy-start.6 = (s32[32]{0:T(128)S(1)}, s32[32]{0:T(128)}, u32[]{:S(2)}) copy-start(s32[32]{0:T(128)} %param.8) | copy-start | bytes 388
  109.7 86.4 %all-to-all-start = ((bf16[128,8,4,2,256]{4,2,1,3,0:T(4,128)(2,1)}), bf16[128,8,4,2,256]{4,2,1,3,0:T(4,128)(2,1)}, u32[]{:S(2)}, u32[]{:S(2)}) async-start(bf16[128,8,4,2,256]{4,2,1,3,0:T(4,128)(2,1)} %copy.59), calls=%async_computation | async-start | bytes 8388608 | tf_op jit(solution)/shard_map/all_to_all | solution.py:66
  220.5 5.2 %copy-start.3 = (bf16[8,512,512]{2,1,0:T(8,128)(2,1)S(1)}, bf16[8,512,512]{2,1,0:T(8,128)(2,1)}, u32[]{:S(2)}) copy-start(bf16[8,512,512]{2,1,0:T(8,128)(2,1)} %copy.63) | copy-start | bytes 12582916
  234.5 6.3 %copy-start.2 = (f32[8,1024,512]{2,1,0:T(8,128)S(1)}, f32[8,1024,512]{2,1,0:T(8,128)}, u32[]{:S(2)}) copy-start(f32[8,1024,512]{2,1,0:T(8,128)} %fusion.5) | copy-start | bytes 50331652
  477.4 23.3 %copy-start.1 = (s32[1024]{0:T(1024)S(1)}, s32[1024]{0:T(1024)}, u32[]{:S(2)}) copy-start(s32[1024]{0:T(1024)} %param.9) | copy-start | bytes 12292

commit v3 on v2

--- a/solution.py
+++ b/solution.py
@@ -44,6 +44,7 @@
     frame = 2 * channel_count
 
     slot_order = lax.all_gather(input_order.astype(jnp.float32), "blk", tiled=True)
+    slot_order, chan_order = lax.optimization_barrier((slot_order, chan_order))
 
     dest_b = np.arange(n_blk)[:, None, None]
     dest_f = np.arange(n_freq)[None, :, None]
@@ -80,11 +81,12 @@
     for own in range(n_blk):
         start = (own - steps + 1) % n_blk * tile
         blocks.append(doubled[:, :, own, :, start : start + rows])
-    banded = jnp.stack(blocks).transpose(0, 2, 1, 3, 4) * (1.0 / SPECTRA)
+    banded = jnp.stack(blocks).transpose(0, 2, 3, 1, 4) * (1.0 / SPECTRA)
 
     returned = lax.all_to_all(banded, "blk", 0, 0, tiled=True)
-    returned = returned.reshape(n_blk, 2, chunk, tile, steps, tile)[:, :, :, :, ::-1]
-    return returned.transpose(1, 4, 5, 3, 0, 2).reshape(2, steps, tile, tile, n_blk * chunk)
+    returned = returned.transpose(1, 2, 0, 3, 4).reshape(2, tile, n_blk * chunk, steps, tile)
+    returned = returned[:, :, :, ::-1].transpose(0, 1, 3, 4, 2)
+    return returned.transpose(0, 2, 3, 1, 4)
 
 
 def solution(mesh):

time: 511 us -> 528 us (1.033)
  waiting for transfers between devices: 0.01 us -> 51.2 us
  blocking collectives: 219 us -> 182 us
  other arithmetic: 54.9 us -> 65.3 us
    unnamed x1 -> x0, blocking collectives: 72.9 us -> none
    another operation x1 -> x3, local copies, waits for them, and re-layouts: 1.16 us -> 57.5 us  [the longest x2 56.3 us: per_device(): return returned.transpose(0, 2, 3, 1, 4)]
    all_to_all x1, waiting for transfers between devices: 0.01 us -> 51.2 us  [per_device(): gathered = lax.all_to_all(spectra, ('blk', 'freq'), 0, 0, tiled=True)]
    optimization_barrier x0 -> x1, blocking collectives: none -> 35.1 us  [per_device(): slot_order, chan_order = lax.optimization_barrier((slot_order, chan_order))]
    reshape x1 -> x0, local copies, waits for them, and re-layouts: 23.3 us -> none  [per_device(): returned.transpose(1, 4, 5, 3, 0, 2)]
    all_to_all x1 -> x0, local copies, waits for them, and re-layouts: 22.4 us -> none  [per_device(): returned = lax.all_to_all(banded, 'blk', 0, 0, tiled=True)]
    transpose x2 -> x1, local copies, waits for them, and re-layouts: 39 us -> 22.6 us  [per_device(): returned.transpose(1, 2, 0, 3, 4)]
    mul x1, other arithmetic: 11.4 us -> 21.2 us  [per_device(): banded = jnp.stack(blocks).transpose(0, 2, 3, 1, 4) * (1.0 / SPECTRA)]
  transfers between devices with their start and end apart: 1 -> 1, of which waited for: 0 -> 1; matrix products, arithmetic and copies ran while one was open for 0% -> 0% of each run, Pallas kernels for 0% -> 0%
where the time goes in v3:
time: 528 us; the launch traced here: 519 us
  blocking collectives  182 us (34%)
  local copies, waits for them, and re-layouts  155 us (29%)
  other arithmetic  65.3 us (12%)
  matrix products  54.1 us (10%)
  waiting for transfers between devices  51.2 us (10%)
  starting transfers between devices  10.1 us (2%)
    all_to_all x1, blocking collectives, per_device(): returned = lax.all_to_all(banded, 'blk', 0, 0, tiled=True)  147 us
    another operation x2, local copies, waits for them, and re-layouts, per_device(): return returned.transpose(0, 2, 3, 1, 4)  56.3 us
    all_to_all x1, waiting for transfers between devices, per_device(): gathered = lax.all_to_all(spectra, ('blk', 'freq'), 0, 0, tiled=True)  51.2 us
    dot_general x2, matrix products, per_device(): jnp.einsum('mc,nm->cn', part, filtered, precision=lax.Precision.HIGH)  45.8 us
    optimization_barrier x1, blocking collectives, per_device(): slot_order, chan_order = lax.optimization_barrier((slot_order, chan_order))  35.1 us
    transpose x1, local copies, waits for them, and re-layouts, per_device(): returned.transpose(1, 2, 0, 3, 4)  22.6 us
    mul x1, other arithmetic, per_device(): banded = jnp.stack(blocks).transpose(0, 2, 3, 1, 4) * (1.0 / SPECTRA)  21.2 us
    gather x3, local copies, waits for them, and re-layouts, per_device(): slotted = jnp.take(gathered, slot_order.astype(jnp.int32), axis=1)  19.1 us
  transfers between devices with their start and end apart: 1, of which 1 were waited for; matrix products, arithmetic and copies ran while one was open for 0% of the time, Pallas kernels for 0%

profile of v3, /device:TPU:1, one launch (start us, length us, event | category | flops | bytes accessed | tf_op | source)
XLA Modules:
  0.0 518.8 jit_solution(15906352861903801345)
XLA Ops:
  0.0 1.2 dynamic-slice
  1.9 0.8 convert_dynamic-update-slice_fusion
  2.7 35.1 %all-reduce = f32[512]{0:T(512)S(1)} all-reduce(f32[512]{0:T(512)S(1)} %convert_dynamic-update-slice_fusion), channel_id=1, replica_groups=mesh['blk'=16,'freq'=8] {'blk'}, use_global_device_ids=true, to_apply=%add | all-reduce | flops 512 | bytes 4096 | tf_op jit(solution)/shard_map/optimization_barrier | solution.py:47
  37.7 0.7 broadcast_clamp_fusion
  38.4 4.5 gather_fusion
  43.0 1.0 fusion.47
  44.0 0.9 fusion.55
  45.0 0.5 fusion.52
  45.5 7.9 %reshape.197 = f32[4,259,2048]{2,1,0:T(8,128)} reshape(bf16[4,530432]{1,0:T(4,128)(2,1)} %param.6) | data formatting | bytes 12730368 | tf_op jit(solution)/shard_map/reshape | solution.py:55
  53.4 6.9 %subtract_multiply_fusion = (f32[32,64,1024]{2,1,0:T(8,128)}, f32[32,64,1024]{2,1,0:T(8,128)}) fusion(f32[64,1024]{1,0:T(8,128)S(1)} %get-tuple-element.20, f32[32,1024]{1,0:T(8,128)S(1)} %get-tuple-element.18, f32[64,1024]{1,0:T(8,128)S(1)} %get-tuple-element.19, f32[32,1024]{1,0:T(8,128)S(1)} %get-tuple-element.17), kind=kLoop, calls=%fused_computation.24 | loop fusion | flops 16777216 | bytes 17563648 | tf_op jit(solution)/shard_map/mul | solution.py:31
  60.3 9.3 %copy.67 = f32[1024,2048]{1,0:T(8,128)} copy(f32[1024,2048]{0,1:T(8,128)} %bitcast.130) | data formatting | bytes 16777216 | tf_op jit(solution)/shard_map/mc,nm->cn/dot_general | solution.py:61
  69.6 9.2 %copy.69 = f32[1024,2048]{1,0:T(8,128)} copy(f32[1024,2048]{0,1:T(8,128)} %bitcast.129) | data formatting | bytes 16777216 | tf_op jit(solution)/shard_map/mc,nm->cn/dot_general | solution.py:61
  78.8 17.3 %fusion.2 = f32[4,256,2048,1]{2,1,0,3:T(8,128)} fusion(f32[4,259,2048]{2,1,0:T(8,128)} %reshape.197, f32[2048]{0:T(1024)S(1)} %bitcast.137, f32[2048]{0:T(1024)S(1)} %bitcast.138, f32[2048]{0:T(1024)S(1)} %bitcast.136, f32[2048]{0:T(1024)S(1)} %bitcast.135), kind=kLoop, calls=%fused_computation.7 | loop fusion | flops 14680064 | bytes 41975808 | tf_op jit(solution)/shard_map/add | solution.py:58
  96.1 22.8 %convert_bitcast_fusion.1 = bf16[128,8,1,4,256]{4,0,3,1,2:T(8,128)(2,1)S(1)} fusion(f32[4,256,2048,1]{2,1,0,3:T(8,128)} %fusion.2, f32[128,8,2048,1]{2,1,0,3:T(8,128)S(1)} %bitcast.133), kind=kOutput, calls=%fused_computation.32 | convolution fusion | flops 12885950464 | bytes 18874368 | tf_op jit(solution)/shard_map/mc,nm->cn/dot_general | solution.py:61
  119.0 23.0 %convert_bitcast_fusion = bf16[128,8,1,4,256]{4,0,3,1,2:T(8,128)(2,1)S(1)} fusion(f32[4,256,2048,1]{2,1,0,3:T(8,128)} %fusion.2, f32[128,8,2048,1]{2,1,0,3:T(8,128)S(1)} %bitcast.134), kind=kOutput, calls=%fused_computation.31 | convolution fusion | flops 12885950464 | bytes 18874368 | tf_op jit(solution)/shard_map/mc,nm->cn/dot_general | solution.py:61
  142.0 0.4 maximum_bitcast_fusion
  142.4 5.3 %copy.71 = bf16[128,8,4,2,256]{4,2,1,3,0:T(4,128)(2,1)} copy(bf16[128,8,4,2,256]{4,0,2,1,3:T(8,128)(2,1)S(1)} %maximum_bitcast_fusion) | data formatting | bytes 8388608 | tf_op jit(solution)/shard_map/transpose | solution.py:65
  147.6 10.1 %all-to-all-start = ((bf16[128,8,4,2,256]{4,2,1,3,0:T(4,128)(2,1)}), bf16[128,8,4,2,256]{4,2,1,3,0:T(4,128)(2,1)}, u32[]{:S(2)}, u32[]{:S(2)}) async-start(bf16[128,8,4,2,256]{4,2,1,3,0:T(4,128)(2,1)} %copy.71), calls=%async_computation | async-start | bytes 8388608 | tf_op jit(solution)/shard_map/all_to_all | solution.py:67
  157.8 51.2 %all-to-all-done = bf16[128,8,4,2,256]{4,2,1,3,0:T(4,128)(2,1)} async-done(((bf16[128,8,4,2,256]{4,2,1,3,0:T(4,128)(2,1)}), bf16[128,8,4,2,256]{4,2,1,3,0:T(4,128)(2,1)}, u32[]{:S(2)}, u32[]{:S(2)}) %all-to-all-start) | async-done | bytes 4194336 | tf_op jit(solution)/shard_map/all_to_all | solution.py:67
  209.0 5.3 %copy.72 = bf16[128,8,4,2,256]{4,1,3,2,0:T(8,128)(2,1)} copy(bf16[128,8,4,2,256]{4,2,1,3,0:T(4,128)(2,1)} %all-to-all-done) | data formatting | bytes 8388608 | tf_op jit(solution)/shard_map/all_to_all | solution.py:67
  214.2 5.1 gather_fusion.1
  219.4 7.5 %copy.74 = bf16[8,512,2,256]{1,3,2,0:T(8,128)(2,1)} copy(bf16[8,512,2,256]{3,0,2,1:T(8,128)(2,1)} %bitcast.128) | data formatting | bytes 8388608 | tf_op jit(solution)/shard_map/jit(_take)/gather | solution.py:71
  226.8 6.5 %copy.75 = bf16[8,512,512]{2,1,0:T(8,128)(2,1)} copy(bf16[8,512,512]{1,2,0:T(8,128)(2,1)} %bitcast.132) | data formatting | bytes 8388608 | tf_op jit(solution)/shard_map/jit(_take)/gather | solution.py:71
  233.3 5.2 bitcast_select_fusion
  238.5 0.5 broadcast_select_fusion
  239.2 8.3 %fusion.5 = f32[8,1024,512]{2,1,0:T(8,128)} fusion(bf16[8,512,512]{2,1,0:T(8,128)(2,1)S(1)} %broadcast_select_fusion, bf16[8,512,256]{2,1,0:T(8,128)(2,1)S(1)} %get-tuple-element.10, bf16[8,512,256]{2,1,0:T(8,128)(2,1)S(1)} %get-tuple-element.9), kind=kOutput, calls=%fused_computation.13 | convolution fusion | flops 4320133120 | bytes 25165824 | tf_op jit(solution)/shard_map/kat,kpt->kap/dot_general | solution.py:76
  247.6 2.2 fusion.36
  249.8 4.1 copy-done.2
  253.9 1.3 fusion.35
  255.1 1.2 fusion.34
  256.3 1.2 fusion.33
  257.6 1.0 fusion.32
  258.6 1.2 fusion.31
  259.8 1.2 fusion.30
  261.0 1.2 fusion.29
  262.3 1.0 fusion.27
  263.2 1.2 fusion.26
  264.4 1.3 fusion.25
  265.7 1.3 fusion.24
  266.9 1.0 fusion.23
  267.9 1.2 fusion.22
  269.1 1.2 fusion.21
  270.2 1.2 fusion.20
  271.4 21.2 %fusion = f32[16,2,32,8,288]{4,3,2,1,0:T(8,128)} fusion(f32[16,8,2,32,288]{4,3,2,1,0:T(8,128)} %fusion.20), kind=kLoop, calls=%fused_computation.4 | loop fusion | flops 2359296 | bytes 18874368 | tf_op jit(solution)/shard_map/mul | solution.py:84
  292.6 146.9 %all_to_all.10 = f32[16,2,32,8,288]{4,3,2,1,0:T(8,128)} all-to-all(f32[16,2,32,8,288]{4,3,2,1,0:T(8,128)} %fusion), channel_id=1, replica_groups=mesh['blk'=16,'freq'=8] {'blk'}, dimensions={0} | all-to-all | bytes 18874368 | tf_op jit(solution)/shard_map/all_to_all | solution.py:86
  439.5 22.6 %copy.77 = f32[2,32,16,8,288]{1,4,3,2,0:T(8,128)} copy(f32[2,32,16,8,288]{4,3,1,0,2:T(8,128)} %bitcast.127) | data formatting | bytes 18874368 | tf_op jit(solution)/shard_map/transpose | solution.py:87
  462.1 27.7 %reverse_bitcast_fusion = f32[2,9,32,32,128]{3,2,1,4,0:T(8,128)} fusion(f32[2,32,128,9,32]{1,4,3,2,0:T(8,128)} %bitcast.126), kind=kLoop, calls=%fused_computation.2 | loop fusion | bytes 18874368 | tf_op jit(solution)/shard_map/transpose;transpose | solution.py:89
  489.8 28.6 %copy.78 = f32[2,9,32,32,128]{4,3,2,1,0:T(8,128)} copy(f32[2,9,32,32,128]{3,2,1,4,0:T(8,128)} %reverse_bitcast_fusion) | data formatting | bytes 18874368 | tf_op jit(solution)/shard_map/transpose;transpose | solution.py:89
  (17 shorter events, 0.3 us)
Async XLA Ops:
  0.0 38.4 %copy-start = (s32[1024]{0:T(1024)S(1)}, s32[1024]{0:T(1024)}, u32[]{:S(2)}) copy-start(s32[1024]{0:T(1024)} %param.9) | copy-start | bytes 12292
  78.8 17.3 %copy-start.4 = (f32[1024,2048]{1,0:T(8,128)S(1)}, f32[1024,2048]{1,0:T(8,128)}, u32[]{:S(2)}) copy-start(f32[1024,2048]{1,0:T(8,128)} %copy.67) | copy-start | bytes 25165828
  96.1 22.9 %copy-start.5 = (f32[1024,2048]{1,0:T(8,128)S(1)}, f32[1024,2048]{1,0:T(8,128)}, u32[]{:S(2)}) copy-start(f32[1024,2048]{1,0:T(8,128)} %copy.69) | copy-start | bytes 25165828
  147.6 61.4 %all-to-all-start = ((bf16[128,8,4,2,256]{4,2,1,3,0:T(4,128)(2,1)}), bf16[128,8,4,2,256]{4,2,1,3,0:T(4,128)(2,1)}, u32[]{:S(2)}, u32[]{:S(2)}) async-start(bf16[128,8,4,2,256]{4,2,1,3,0:T(4,128)(2,1)} %copy.71), calls=%async_computation | async-start | bytes 8388608 | tf_op jit(solution)/shard_map/all_to_all | solution.py:67
  233.3 5.2 copy-start.3
  247.6 6.3 %copy-start.2 = (f32[8,1024,512]{2,1,0:T(8,128)S(1)}, f32[8,1024,512]{2,1,0:T(8,128)}, u32[]{:S(2)}) copy-start(f32[8,1024,512]{2,1,0:T(8,128)} %fusion.5) | copy-start | bytes 50331652
  489.8 28.6 %copy-start.1 = (s32[1024]{0:T(1024)S(1)}, s32[1024]{0:T(1024)}, u32[]{:S(2)}) copy-start(s32[1024]{0:T(1024)} %param.9) | copy-start | bytes 12292

commit v4 on v3

--- a/solution.py
+++ b/solution.py
@@ -84,9 +84,10 @@
     banded = jnp.stack(blocks).transpose(0, 2, 3, 1, 4) * (1.0 / SPECTRA)
 
     returned = lax.all_to_all(banded, "blk", 0, 0, tiled=True)
-    returned = returned.transpose(1, 2, 0, 3, 4).reshape(2, tile, n_blk * chunk, steps, tile)
-    returned = returned[:, :, :, ::-1].transpose(0, 1, 3, 4, 2)
-    return returned.transpose(0, 2, 3, 1, 4)
+    eye = jnp.eye(n_blk * chunk, dtype=jnp.float32).reshape(n_blk, chunk, n_blk * chunk)
+    turned = jnp.einsum("brikq,bkc->riqc", returned, eye, precision=lax.Precision.HIGHEST)
+    turned = turned.reshape(2, tile, steps, tile, n_blk * chunk)[:, :, ::-1]
+    return turned.transpose(0, 2, 3, 1, 4)
 
 
 def solution(mesh):

time: 528 us -> 535 us (1.013)
  waiting for transfers between devices: 51.2 us -> 219 us
  blocking collectives: 182 us -> 35.1 us
  local copies, waits for them, and re-layouts: 155 us -> 107 us
  matrix products: 54.1 us -> 81.6 us
  starting transfers between devices: 10.1 us -> 16.6 us
    all_to_all x0 -> x1, waiting for transfers between devices: none -> 168 us  [per_device(): returned = lax.all_to_all(banded, 'blk', 0, 0, tiled=True)]
    all_to_all x1 -> x0, blocking collectives: 147 us -> none  [per_device(): returned = lax.all_to_all(banded, 'blk', 0, 0, tiled=True)]
    another operation x2 -> x0, local copies, waits for them, and re-layouts: 56.3 us -> none  [per_device(): return returned.transpose(0, 2, 3, 1, 4)]
    dot_general x0 -> x1, matrix products: none -> 33.8 us  [per_device(): jnp.einsum('brikq,bkc->riqc', returned, eye, precision=lax.Precision.HIGH...]
    all_to_all x0 -> x1, local copies, waits for them, and re-layouts: none -> 26.8 us  [per_device(): returned = lax.all_to_all(banded, 'blk', 0, 0, tiled=True)]
    transpose x1, local copies, waits for them, and re-layouts: 22.6 us -> 5.25 us  [per_device(): return turned.transpose(0, 2, 3, 1, 4)]
    dot_general x2, matrix products: 45.8 us -> 39.6 us  [per_device(): jnp.einsum('mc,nm->cn', part, filtered, precision=lax.Precision.HIGH)]
    all_to_all x0 -> x1, starting transfers between devices: none -> 5.9 us  [per_device(): returned = lax.all_to_all(banded, 'blk', 0, 0, tiled=True)]
  transfers between devices with their start and end apart: 1 -> 2, of which waited for: 1 -> 2; matrix products, arithmetic and copies ran while one was open for 0% -> 0% of each run, Pallas kernels for 0% -> 0%
where the time goes in v4:
time: 535 us; the launch traced here: 526 us
  waiting for transfers between devices  219 us (41%)
  local copies, waits for them, and re-layouts  107 us (20%)
  matrix products  81.6 us (15%)
  other arithmetic  65.7 us (12%)
  blocking collectives  35.1 us (7%)
  starting transfers between devices  16.6 us (3%)
    all_to_all x1, waiting for transfers between devices, per_device(): returned = lax.all_to_all(banded, 'blk', 0, 0, tiled=True)  168 us
    all_to_all x1, waiting for transfers between devices, per_device(): gathered = lax.all_to_all(spectra, ('blk', 'freq'), 0, 0, tiled=True)  51 us
    dot_general x2, matrix products, per_device(): jnp.einsum('mc,nm->cn', part, filtered, precision=lax.Precision.HIGH)  39.6 us
    optimization_barrier x1, blocking collectives, per_device(): slot_order, chan_order = lax.optimization_barrier((slot_order, chan_order))  35.1 us
    dot_general x1, matrix products, per_device(): jnp.einsum('brikq,bkc->riqc', returned, eye, precision=lax.Precision.HIGH...  33.8 us
    all_to_all x1, local copies, waits for them, and re-layouts, per_device(): returned = lax.all_to_all(banded, 'blk', 0, 0, tiled=True)  26.8 us
    mul x1, other arithmetic, per_device(): banded = jnp.stack(blocks).transpose(0, 2, 3, 1, 4) * (1.0 / SPECTRA)  21.1 us
    gather x3, local copies, waits for them, and re-layouts, per_device(): slotted = jnp.take(gathered, slot_order.astype(jnp.int32), axis=1)  19.1 us
  transfers between devices with their start and end apart: 2, of which 2 were waited for; matrix products, arithmetic and copies ran while one was open for 0% of the time, Pallas kernels for 0%

profile of v4, /device:TPU:1, one launch (start us, length us, event | category | flops | bytes accessed | tf_op | source)
XLA Modules:
  0.0 526.3 jit_solution(6521348147084006417)
XLA Ops:
  0.0 1.2 dynamic-slice
  1.9 0.8 convert_dynamic-update-slice_fusion
  2.7 35.1 %all-reduce = f32[512]{0:T(512)S(1)} all-reduce(f32[512]{0:T(512)S(1)} %convert_dynamic-update-slice_fusion), channel_id=1, replica_groups=mesh['blk'=16,'freq'=8] {'blk'}, use_global_device_ids=true, to_apply=%add | all-reduce | flops 512 | bytes 4096 | tf_op jit(solution)/shard_map/optimization_barrier | solution.py:47
  37.7 0.7 broadcast_clamp_fusion
  38.4 4.5 gather_fusion
  43.0 1.0 fusion.47
  44.0 0.5 fusion.52
  44.5 7.1 %subtract_multiply_fusion = (f32[32,64,1024]{2,1,0:T(8,128)}, f32[32,64,1024]{2,1,0:T(8,128)}) fusion(f32[64,1024]{1,0:T(8,128)S(1)} %get-tuple-element.20, f32[32,1024]{1,0:T(8,128)S(1)} %get-tuple-element.18, f32[64,1024]{1,0:T(8,128)S(1)} %get-tuple-element.19, f32[32,1024]{1,0:T(8,128)S(1)} %get-tuple-element.17), kind=kLoop, calls=%fused_computation.24 | loop fusion | flops 16777216 | bytes 17563648 | tf_op jit(solution)/shard_map/mul | solution.py:31
  51.7 9.2 %copy.67 = f32[1024,2048]{1,0:T(8,128)} copy(f32[1024,2048]{0,1:T(8,128)} %bitcast.141) | data formatting | bytes 16777216 | tf_op jit(solution)/shard_map/mc,nm->cn/dot_general | solution.py:61
  60.9 7.9 %reshape.221 = f32[4,259,2048]{2,1,0:T(8,128)} reshape(bf16[4,530432]{1,0:T(4,128)(2,1)} %param.6) | data formatting | bytes 12730368 | tf_op jit(solution)/shard_map/reshape | solution.py:55
  68.8 9.2 %copy.69 = f32[1024,2048]{1,0:T(8,128)} copy(f32[1024,2048]{0,1:T(8,128)} %bitcast.140) | data formatting | bytes 16777216 | tf_op jit(solution)/shard_map/mc,nm->cn/dot_general | solution.py:61
  78.0 14.1 %fusion.2 = f32[4,256,2048,1]{2,1,0,3:T(8,128)S(1)} fusion(f32[4,259,2048]{2,1,0:T(8,128)} %reshape.221, f32[2048]{0:T(1024)S(1)} %bitcast.148, f32[2048]{0:T(1024)S(1)} %bitcast.149, f32[2048]{0:T(1024)S(1)} %bitcast.147, f32[2048]{0:T(1024)S(1)} %bitcast.146), kind=kLoop, calls=%fused_computation.7 | loop fusion | flops 14680064 | bytes 41975808 | tf_op jit(solution)/shard_map/add | solution.py:58
  92.1 21.8 %convert_bitcast_fusion.1 = bf16[128,8,1,4,256]{4,0,3,1,2:T(8,128)(2,1)S(1)} fusion(f32[4,256,2048,1]{2,1,0,3:T(8,128)S(1)} %fusion.2, f32[128,8,2048,1]{2,1,0,3:T(8,128)} %bitcast.144), kind=kOutput, calls=%fused_computation.33 | convolution fusion | flops 12885950464 | bytes 18874368 | tf_op jit(solution)/shard_map/mc,nm->cn/dot_general | solution.py:61
  113.9 17.8 %convert_bitcast_fusion = bf16[128,8,1,4,256]{4,0,3,1,2:T(8,128)(2,1)S(1)} fusion(f32[4,256,2048,1]{2,1,0,3:T(8,128)S(1)} %fusion.2, f32[128,8,2048,1]{2,1,0,3:T(8,128)S(1)} %bitcast.145), kind=kOutput, calls=%fused_computation.32 | convolution fusion | flops 12885950464 | bytes 18874368 | tf_op jit(solution)/shard_map/mc,nm->cn/dot_general | solution.py:61
  132.1 5.3 copy.71
  137.4 10.7 %all-to-all-start = ((bf16[128,8,4,2,256]{4,2,1,3,0:T(4,128)(2,1)}), bf16[128,8,4,2,256]{4,2,1,3,0:T(4,128)(2,1)}, u32[]{:S(2)}, u32[]{:S(2)}) async-start(bf16[128,8,4,2,256]{4,2,1,3,0:T(4,128)(2,1)} %copy.71), calls=%async_computation | async-start | bytes 8388608 | tf_op jit(solution)/shard_map/all_to_all | solution.py:67
  148.1 51.0 %all-to-all-done = bf16[128,8,4,2,256]{4,2,1,3,0:T(4,128)(2,1)} async-done(((bf16[128,8,4,2,256]{4,2,1,3,0:T(4,128)(2,1)}), bf16[128,8,4,2,256]{4,2,1,3,0:T(4,128)(2,1)}, u32[]{:S(2)}, u32[]{:S(2)}) %all-to-all-start) | async-done | bytes 4194336 | tf_op jit(solution)/shard_map/all_to_all | solution.py:67
  199.1 5.3 copy.72
  204.4 5.1 gather_fusion.1
  209.5 5.0 bitcast_select_fusion
  214.5 1.6 slice_bitcast_fusion
  216.1 7.5 %copy.74 = bf16[8,512,2,256]{1,3,2,0:T(8,128)(2,1)} copy(bf16[8,512,2,256]{3,0,2,1:T(8,128)(2,1)} %bitcast.138) | data formatting | bytes 8388608 | tf_op jit(solution)/shard_map/jit(_take)/gather | solution.py:71
  223.6 6.5 %copy.75 = bf16[8,512,512]{2,1,0:T(8,128)(2,1)} copy(bf16[8,512,512]{1,2,0:T(8,128)(2,1)} %bitcast.143) | data formatting | bytes 8388608 | tf_op jit(solution)/shard_map/jit(_take)/gather | solution.py:71
  230.0 2.8 broadcast_select_fusion
  232.9 8.3 %fusion.5 = f32[8,1024,512]{2,1,0:T(8,128)} fusion(bf16[8,512,512]{2,1,0:T(8,128)(2,1)S(1)} %broadcast_select_fusion, bf16[8,512,256]{2,1,0:T(8,128)(2,1)S(1)} %copy-done.4, bf16[8,512,256]{2,1,0:T(8,128)(2,1)S(1)} %get-tuple-element.9), kind=kOutput, calls=%fused_computation.13 | convolution fusion | flops 4320133120 | bytes 25165824 | tf_op jit(solution)/shard_map/kat,kpt->kap/dot_general | solution.py:76
  241.2 2.2 fusion.36
  243.4 4.1 copy-done.2
  247.4 1.2 fusion.35
  248.7 1.2 fusion.34
  249.9 1.2 fusion.33
  251.1 1.0 fusion.32
  252.1 1.2 fusion.31
  253.3 1.3 fusion.30
  254.6 1.2 fusion.29
  255.8 1.0 fusion.27
  256.8 1.2 fusion.26
  258.0 1.2 fusion.25
  259.2 1.2 fusion.24
  260.5 1.0 fusion.23
  261.4 1.2 fusion.22
  262.6 1.1 fusion.21
  263.7 1.2 fusion.20
  264.9 21.1 %fusion = f32[16,2,32,8,288]{4,3,2,1,0:T(8,128)} fusion(f32[16,8,2,32,288]{4,3,2,1,0:T(8,128)} %fusion.20), kind=kLoop, calls=%fused_computation.3 | loop fusion | flops 2359296 | bytes 18874368 | tf_op jit(solution)/shard_map/mul | solution.py:84
  286.0 5.9 %all-to-all-start.1 = ((f32[16,2,32,8,288]{4,3,2,1,0:T(8,128)}), f32[16,2,32,8,288]{4,3,2,1,0:T(8,128)}, u32[]{:S(2)}, u32[]{:S(2)}) async-start(f32[16,2,32,8,288]{4,3,2,1,0:T(8,128)} %fusion), calls=%async_computation.1 | async-start | bytes 25165824 | tf_op jit(solution)/shard_map/all_to_all | solution.py:86
  291.9 168.3 %all-to-all-done.1 = f32[16,2,32,8,288]{4,3,2,1,0:T(8,128)} async-done(((f32[16,2,32,8,288]{4,3,2,1,0:T(8,128)}), f32[16,2,32,8,288]{4,3,2,1,0:T(8,128)}, u32[]{:S(2)}, u32[]{:S(2)}) %all-to-all-start.1) | async-done | bytes 9437216 | tf_op jit(solution)/shard_map/all_to_all | solution.py:86
  460.2 26.8 %copy.77 = f32[16,2,32,8,288]{2,3,0,4,1:T(8,128)} copy(f32[16,2,32,8,288]{4,3,2,1,0:T(8,128)} %all-to-all-done.1) | data formatting | bytes 18874368 | tf_op jit(solution)/shard_map/all_to_all | solution.py:86
  487.0 33.8 %convolution_bitcast_fusion = f32[2,32,9,32,128]{4,1,3,2,0:T(8,128)S(1)} fusion(f32[2,32,9,32,16,8]{1,5,4,3,2,0:T(8,128)} %bitcast.139, s32[16,8]{1,0:T(8,128)S(1)} %multiply_add_fusion), kind=kOutput, calls=%fused_computation.28 | convolution fusion | flops 3623895040 | bytes 18874880 | tf_op jit(solution)/shard_map/brikq,bkc->riqc/dot_general | solution.py:88
  520.8 5.3 reverse_bitcast_fusion
  (19 shorter events, 0.5 us)
Async XLA Ops:
  0.0 38.4 %copy-start = (s32[1024]{0:T(1024)S(1)}, s32[1024]{0:T(1024)}, u32[]{:S(2)}) copy-start(s32[1024]{0:T(1024)} %param.9) | copy-start | bytes 12292
  51.7 9.2 %copy-start.5 = (f32[4,2048]{1,0:T(4,128)S(1)}, f32[4,2048]{1,0:T(4,128)}, u32[]{:S(2)}) copy-start(f32[4,2048]{1,0:T(4,128)} %param.7) | copy-start | bytes 98308
  92.1 21.8 %copy-start.3 = (f32[1024,2048]{1,0:T(8,128)S(1)}, f32[1024,2048]{1,0:T(8,128)}, u32[]{:S(2)}) copy-start(f32[1024,2048]{1,0:T(8,128)} %copy.69) | copy-start | bytes 25165828
  137.4 61.7 %all-to-all-start = ((bf16[128,8,4,2,256]{4,2,1,3,0:T(4,128)(2,1)}), bf16[128,8,4,2,256]{4,2,1,3,0:T(4,128)(2,1)}, u32[]{:S(2)}, u32[]{:S(2)}) async-start(bf16[128,8,4,2,256]{4,2,1,3,0:T(4,128)(2,1)} %copy.71), calls=%async_computation | async-start | bytes 8388608 | tf_op jit(solution)/shard_map/all_to_all | solution.py:67
  230.0 2.9 copy-start.4
  241.1 6.3 %copy-start.2 = (f32[8,1024,512]{2,1,0:T(8,128)S(1)}, f32[8,1024,512]{2,1,0:T(8,128)}, u32[]{:S(2)}) copy-start(f32[8,1024,512]{2,1,0:T(8,128)} %fusion.5) | copy-start | bytes 50331652
  286.0 174.2 %all-to-all-start.1 = ((f32[16,2,32,8,288]{4,3,2,1,0:T(8,128)}), f32[16,2,32,8,288]{4,3,2,1,0:T(8,128)}, u32[]{:S(2)}, u32[]{:S(2)}) async-start(f32[16,2,32,8,288]{4,3,2,1,0:T(8,128)} %fusion), calls=%async_computation.1 | async-start | bytes 25165824 | tf_op jit(solution)/shard_map/all_to_all | solution.py:86
  487.0 39.1 %copy-start.1 = (s32[1024]{0:T(1024)S(1)}, s32[1024]{0:T(1024)}, u32[]{:S(2)}) copy-start(s32[1024]{0:T(1024)} %param.9) | copy-start | bytes 12292

commit v5 on v4

v5 whole, which is shorter than its diff:
```python
import math

import numpy as np
import jax
import jax.numpy as jnp
from jax import lax
from jax.sharding import PartitionSpec as P

TAPS = 4
SPECTRA = 256


def phase_table(chans, rows, period):
    sample_index = jnp.arange(rows, dtype=jnp.int32)
    product = sample_index[:, None] * chans[None, :] % period
    phase_arg = product.astype(jnp.float32) * (math.pi / (period // 2))
    return jnp.cos(phase_arg), jnp.sin(phase_arg)


def make_table(chans, channel_count):
    period = 2 * channel_count
    inner_rows = 64
    outer_rows = period // inner_rows
    inner_cos, inner_sin = phase_table(chans, inner_rows, period)
    outer_chans = chans * inner_rows % period
    outer_cos, outer_sin = phase_table(outer_chans, outer_rows, period)
    scale = 1.0 / math.sqrt(channel_count)
    cos = outer_cos[:, None, :] * inner_cos[None] - outer_sin[:, None, :] * inner_sin[None]
    sin = outer_sin[:, None, :] * inner_cos[None] + outer_cos[:, None, :] * inner_sin[None]
    columns = chans.shape[0]
    return (cos * scale).reshape(period, columns), (sin * -scale).reshape(period, columns)


def per_device(raw_voltages, filter_taps, input_order, chan_order):
    n_blk = lax.axis_size("blk")
    n_freq = lax.axis_size("freq")
    n_dev = n_blk * n_freq
    channel_count = chan_order.shape[0]
    width = channel_count // n_freq
    chunk = width // n_blk
    halves = 2
    part_chunk = chunk // halves
    steps = n_blk // 2 + 1
    tile = input_order.shape[0]
    local_inputs = raw_voltages.shape[0]
    total_inputs = n_dev * local_inputs
    frame = 2 * channel_count
    rows = steps * tile

    slot_order = lax.all_gather(input_order.astype(jnp.float32), "blk", tiled=True)
    slot_order, chan_order = lax.optimization_barrier((slot_order, chan_order))
    slot_order = slot_order.astype(jnp.int32)

    frames = raw_voltages.astype(jnp.float32).reshape(local_inputs, SPECTRA + TAPS - 1, frame)
    filtered = filter_taps[0] * frames[:, 0:SPECTRA]
    for tap_index in range(1, TAPS):
        filtered = filtered + filter_taps[tap_index] * frames[:, tap_index : tap_index + SPECTRA]
    filtered = filtered.reshape(local_inputs * SPECTRA, frame)

    dest_b = np.arange(n_blk)[:, None, None]
    dest_f = np.arange(n_freq)[None, :, None]

    def half_spectra(half):
        within = np.arange(half * part_chunk, (half + 1) * part_chunk)[None, None, :]
        position = (dest_f * width + dest_b * chunk + within).reshape(-1)
        cos_table, sin_table = make_table(chan_order[position], channel_count)
        parts = [
            jnp.einsum("mc,nm->cn", part, filtered, precision=lax.Precision.HIGH)
            for part in (cos_table, sin_table)
        ]
        spectra = jnp.stack(parts, axis=1).astype(jnp.bfloat16)
        spectra = spectra.reshape(n_dev, part_chunk, 2, local_inputs, SPECTRA)
        return spectra.transpose(0, 1, 3, 2, 4)

    def half_band(spectra):
        gathered = lax.all_to_all(spectra, ("blk", "freq"), 0, 0, tiled=True)
        gathered = gathered.transpose(1, 0, 2, 3, 4).reshape(part_chunk, total_inputs, 2, SPECTRA)
        slotted = jnp.take(gathered, slot_order, axis=1)
        plain = slotted.reshape(part_chunk, total_inputs, 2 * SPECTRA)
        rotated = jnp.concatenate([slotted[:, :, 1], -slotted[:, :, 0]], axis=2)
        both = jnp.concatenate([plain, rotated], axis=1)
        gram = jnp.einsum("kat,kpt->kap", both, plain, preferred_element_type=jnp.float32)
        gram = gram.reshape(part_chunk, 2, n_blk, tile, total_inputs)
        doubled = jnp.concatenate([gram, gram], axis=-1)
        blocks = []
        for own in range(n_blk):
            start = (own - steps + 1) % n_blk * tile
            blocks.append(doubled[:, :, own, :, start : start + rows])
        return jnp.stack(blocks) * (1.0 / SPECTRA)

    def half_output(banded, half):
        returned = lax.all_to_all(banded, "blk", 0, 0, tiled=True)
        returned = returned.reshape(n_blk * part_chunk, 2 * tile * rows)
        source = np.arange(n_blk)[:, None] * chunk + half * part_chunk + np.arange(part_chunk)[None, :]
        select = (source.reshape(-1, 1) == np.arange(n_blk * chunk)[None, :]).astype(np.float32)
        return jnp.einsum("ax,ac->xc", returned, jnp.asarray(select), precision=lax.Precision.HIGHEST)

    spectra_parts = [half_spectra(half) for half in range(halves)]
    band_parts = [half_band(spectra) for spectra in spectra_parts]
    turned = half_output(band_parts[0], 0)
    for half in range(1, halves):
        turned = turned + half_output(band_parts[half], half)
    turned = turned.reshape(2, tile, steps, tile, n_blk * chunk)[:, :, ::-1]
    return turned.transpose(0, 2, 3, 1, 4)


def solution(mesh):
    placed = (P(("blk", "freq"), None), P(), P("blk"), P())
    return jax.shard_map(
        per_device,
        mesh=mesh,
        in_specs=placed,
        out_specs=P(None, None, None, "blk", "freq"),
        check_vma=False,
    )
```

time: 535 us -> 497 us (0.929)
  waiting for transfers between devices: 219 us -> 156 us
  other arithmetic: 65.7 us -> 44.2 us
  local copies, waits for them, and re-layouts: 107 us -> 127 us
  starting transfers between devices: 16.6 us -> 33.5 us
  matrix products: 81.6 us -> 92 us
    all_to_all x2 -> x4, waiting for transfers between devices: 219 us -> 156 us  [the longest x2 132 us: half_output(): returned = lax.all_to_all(banded, 'blk', 0, 0, tiled=True)]
    reshape x0 -> x7, local copies, waits for them, and re-layouts: none -> 36.5 us  [the longest x2 13.9 us: half_output(): returned = returned.reshape(n_blk * part_chunk, 2 * tile * rows)]
    all_to_all x2 -> x0, local copies, waits for them, and re-layouts: 32.1 us -> none  [the longest x1 26.8 us: per_device(): returned = lax.all_to_all(banded, 'blk', 0, 0, tiled=True)]
    dot_general x2 -> x8, local copies, waits for them, and re-layouts: 18.4 us -> 42.3 us  [half_spectra(): jnp.einsum('mc,nm->cn', part, filtered, precision=lax.Precision.HIGH)]
    all_to_all x2 -> x4, starting transfers between devices: 16.6 us -> 33.5 us  [the longest x2 20.5 us: half_band(): gathered = lax.all_to_all(spectra, ('blk', 'freq'), 0, 0, tiled=True)]
    mul x1 -> x2, other arithmetic: 21.1 us -> 6.67 us  [half_band(): return jnp.stack(blocks) * (1.0 / SPECTRA)]
    dot_general x4 -> x8, matrix products: 81.6 us -> 92 us  [the longest x4 46.1 us: half_spectra(): jnp.einsum('mc,nm->cn', part, filtered, precision=lax.Precision.HIGH)]
    unnamed x21 -> x36, local copies, waits for them, and re-layouts: 13.3 us -> 3.09 us
  transfers between devices with their start and end apart: 2 -> 4, of which waited for: 2 -> 3; matrix products, arithmetic and copies ran while one was open for 0% -> 20% of each run, Pallas kernels for 0% -> 0%
where the time goes in v5:
time: 497 us; the launch traced here: 489 us
  waiting for transfers between devices  156 us (31%)
  local copies, waits for them, and re-layouts  127 us (26%)
  matrix products  92 us (19%)
  other arithmetic  44.2 us (9%)
  blocking collectives  35.1 us (7%)
  starting transfers between devices  33.5 us (7%)
    all_to_all x2, waiting for transfers between devices, half_output(): returned = lax.all_to_all(banded, 'blk', 0, 0, tiled=True)  132 us
    dot_general x4, matrix products, half_spectra(): jnp.einsum('mc,nm->cn', part, filtered, precision=lax.Precision.HIGH)  46.1 us
    dot_general x8, local copies, waits for them, and re-layouts, half_spectra(): jnp.einsum('mc,nm->cn', part, filtered, precision=lax.Precision.HIGH)  42.3 us
    dot_general x2, matrix products, half_output(): jnp.einsum('ax,ac->xc', returned, jnp.asarray(select), precision=lax.Prec...  36.4 us
    optimization_barrier x1, blocking collectives, per_device(): slot_order, chan_order = lax.optimization_barrier((slot_order, chan_order))  35.1 us
    all_to_all x2, waiting for transfers between devices, half_band(): gathered = lax.all_to_all(spectra, ('blk', 'freq'), 0, 0, tiled=True)  23.8 us
    all_to_all x2, starting transfers between devices, half_band(): gathered = lax.all_to_all(spectra, ('blk', 'freq'), 0, 0, tiled=True)  20.5 us
    add x1, other arithmetic, per_device(): filtered + filter_taps[tap_index] * frames[:, tap_index:tap_index + SPECTRA]  14.2 us
  transfers between devices with their start and end apart: 4, of which 3 were waited for; matrix products, arithmetic and copies ran while one was open for 20% of the time, Pallas kernels for 0%

profile of v5, /device:TPU:1, one launch (start us, length us, event | category | flops | bytes accessed | tf_op | source)
XLA Modules:
  0.0 489.5 jit_solution(6401983878258471883)
XLA Ops:
  2.7 35.1 %all-reduce = f32[512]{0:T(512)S(1)} all-reduce(f32[512]{0:T(512)S(1)} %convert_dynamic-update-slice_fusion), channel_id=1, replica_groups=mesh['blk'=16,'freq'=8] {'blk'}, use_global_device_ids=true, to_apply=%add | all-reduce | flops 512 | bytes 4096 | tf_op jit(solution)/shard_map/optimization_barrier | solution.py:51
  41.6 4.7 subtract_multiply_fusion
  46.2 5.4 %copy.127 = f32[512,2048]{1,0:T(8,128)} copy(f32[512,2048]{0,1:T(8,128)} %bitcast.297) | data formatting | bytes 8388608 | tf_op jit(solution)/shard_map/mc,nm->cn/dot_general | solution.py:68
  51.6 5.2 %dot_general.59 = f32[128,4,2048]{2,1,0:T(4,128)} reshape(f32[512,2048]{1,0:T(8,128)} %copy.127) | data formatting | bytes 8388608 | tf_op jit(solution)/shard_map/mc,nm->cn/dot_general | solution.py:68
  56.8 7.9 %reshape.383 = f32[4,259,2048]{2,1,0:T(8,128)} reshape(bf16[4,530432]{1,0:T(4,128)(2,1)} %param.12) | data formatting | bytes 12730368 | tf_op jit(solution)/shard_map/reshape | solution.py:54
  64.7 5.4 %copy.129 = f32[512,2048]{1,0:T(8,128)} copy(f32[512,2048]{0,1:T(8,128)} %bitcast.295) | data formatting | bytes 8388608 | tf_op jit(solution)/shard_map/mc,nm->cn/dot_general | solution.py:68
  70.0 5.3 %dot_general.63 = f32[128,4,2048]{2,1,0:T(4,128)} reshape(f32[512,2048]{1,0:T(8,128)} %copy.129) | data formatting | bytes 8388608 | tf_op jit(solution)/shard_map/mc,nm->cn/dot_general | solution.py:68
  75.3 14.2 %fusion.1 = f32[4,256,2048,1]{2,1,0,3:T(8,128)S(1)} fusion(f32[4,259,2048]{2,1,0:T(8,128)} %reshape.383, f32[2048]{0:T(1024)S(1)} %bitcast.312, f32[2048]{0:T(1024)S(1)} %bitcast.313, f32[2048]{0:T(1024)S(1)} %bitcast.311, f32[2048]{0:T(1024)S(1)} %bitcast.310), kind=kLoop, calls=%fused_computation.8 | loop fusion | flops 14680064 | bytes 41975808 | tf_op jit(solution)/shard_map/add | solution.py:57
  89.6 9.2 %fusion.41 = bf16[128,4,1,4,256]{4,0,3,1,2:T(8,128)(2,1)S(1)} fusion(f32[4,256,2048,1]{2,1,0,3:T(8,128)S(1)} %fusion.1, f32[128,4,2048,1]{2,1,0,3:T(4,128)S(1)} %bitcast.306), kind=kOutput, calls=%fused_computation.51 | convolution fusion | flops 6442975232 | bytes 13631488 | tf_op jit(solution)/shard_map/mc,nm->cn/dot_general | solution.py:68
  98.8 9.5 %fusion.38 = bf16[128,4,1,4,256]{4,0,3,1,2:T(8,128)(2,1)S(1)} fusion(f32[4,256,2048,1]{2,1,0,3:T(8,128)S(1)} %fusion.1, f32[128,4,2048,1]{2,1,0,3:T(4,128)S(1)} %bitcast.307), kind=kOutput, calls=%fused_computation.50 | convolution fusion | flops 6442975232 | bytes 13631488 | tf_op jit(solution)/shard_map/mc,nm->cn/dot_general | solution.py:68
  108.5 2.9 copy.131
  111.4 9.7 %all-to-all-start.2 = ((bf16[128,4,4,2,256]{4,2,1,3,0:T(4,128)(2,1)}), bf16[128,4,4,2,256]{4,2,1,3,0:T(4,128)(2,1)S(1)}, u32[]{:S(2)}, u32[]{:S(2)}) async-start(bf16[128,4,4,2,256]{4,2,1,3,0:T(4,128)(2,1)} %copy.131), calls=%async_computation.2 | async-start | bytes 4194304 | tf_op jit(solution)/shard_map/all_to_all | solution.py:76
  121.1 2.3 gather_fusion
  124.3 4.6 subtract_multiply_fusion.1
  128.8 5.4 %copy.109 = f32[512,2048]{1,0:T(8,128)} copy(f32[512,2048]{0,1:T(8,128)} %bitcast.298) | data formatting | bytes 8388608 | tf_op jit(solution)/shard_map/mc,nm->cn/dot_general | solution.py:68
  134.2 5.3 %dot_general.53 = f32[128,4,2048]{2,1,0:T(4,128)} reshape(f32[512,2048]{1,0:T(8,128)} %copy.109) | data formatting | bytes 8388608 | tf_op jit(solution)/shard_map/mc,nm->cn/dot_general | solution.py:68
  139.4 5.4 %copy.107 = f32[512,2048]{1,0:T(8,128)} copy(f32[512,2048]{0,1:T(8,128)} %bitcast.296) | data formatting | bytes 8388608 | tf_op jit(solution)/shard_map/mc,nm->cn/dot_general | solution.py:68
  144.8 5.2 %dot_general.49 = f32[128,4,2048]{2,1,0:T(4,128)} reshape(f32[512,2048]{1,0:T(8,128)} %copy.107) | data formatting | bytes 8388608 | tf_op jit(solution)/shard_map/mc,nm->cn/dot_general | solution.py:68
  150.0 14.2 %fusion.44 = bf16[128,4,1,4,256]{4,0,3,1,2:T(8,128)(2,1)S(1)} fusion(f32[4,256,2048,1]{2,1,0,3:T(8,128)} %copy-done.2, f32[128,4,2048,1]{2,1,0,3:T(4,128)} %bitcast.308), kind=kOutput, calls=%fused_computation.52 | convolution fusion | flops 6442975232 | bytes 13631488 | tf_op jit(solution)/shard_map/mc,nm->cn/dot_general | solution.py:68
  164.1 13.2 %fusion.47 = bf16[128,4,1,4,256]{4,0,3,1,2:T(8,128)(2,1)S(1)} fusion(f32[4,256,2048,1]{2,1,0,3:T(8,128)} %copy-done.2, f32[128,4,2048,1]{2,1,0,3:T(4,128)S(1)} %bitcast.309), kind=kOutput, calls=%fused_computation.53 | convolution fusion | flops 6442975232 | bytes 13631488 | tf_op jit(solution)/shard_map/mc,nm->cn/dot_general | solution.py:68
  177.6 2.9 copy.111
  180.5 10.8 %all-to-all-start = ((bf16[128,4,4,2,256]{4,2,1,3,0:T(4,128)(2,1)}), bf16[128,4,4,2,256]{4,2,1,3,0:T(4,128)(2,1)}, u32[]{:S(2)}, u32[]{:S(2)}) async-start(bf16[128,4,4,2,256]{4,2,1,3,0:T(4,128)(2,1)} %copy.111), calls=%async_computation | async-start | bytes 4194304 | tf_op jit(solution)/shard_map/all_to_all | solution.py:76
  193.5 2.7 copy.133
  196.2 23.8 %all-to-all-done = bf16[128,4,4,2,256]{4,2,1,3,0:T(4,128)(2,1)} async-done(((bf16[128,4,4,2,256]{4,2,1,3,0:T(4,128)(2,1)}), bf16[128,4,4,2,256]{4,2,1,3,0:T(4,128)(2,1)}, u32[]{:S(2)}, u32[]{:S(2)}) %all-to-all-start) | async-done | bytes 2097184 | tf_op jit(solution)/shard_map/all_to_all | solution.py:76
  220.1 3.7 copy.112
  223.8 4.0 copy.113
  227.8 3.9 gather_fusion.3
  231.8 5.4 %gather_fusion.2 = bf16[512,4,2,256]{3,1,2,0:T(4,128)(2,1)} fusion(bf16[4,512,2,256]{3,0,2,1:T(4,128)(2,1)} %copy.113, s32[1024]{0:T(1024)S(1)} %get-tuple-element.33), kind=kCustom, calls=%fused_computation.clone | custom fusion | bytes 4196352 | tf_op jit(solution)/shard_map/jit(_take)/gather | solution.py:78
  237.2 5.2 %fusion.24 = (bf16[4,512,2,256]{3,1,0,2:T(8,128)(2,1)S(1)}, bf16[4,512,2,256]{3,1,0,2:T(8,128)(2,1)}) fusion(bf16[512,4,2,256]{3,1,2,0:T(4,128)(2,1)} %gather_fusion.3, pred[512]{0:T(512)(128)(4,1)S(1)} %compare_and_fusion, bf16[512,4,2,256]{3,1,2,0:T(4,128)(2,1)} %gather_fusion.2), kind=kLoop, calls=%fused_computation.43 | loop fusion | flops 2097152 | bytes 8389120 | tf_op jit(solution)/shard_map/jit(_take)/select_n | solution.py:78
  242.3 4.1 copy.115
  246.5 2.7 slice_bitcast_fusion.1
  249.2 2.4 copy.135
  251.6 4.2 copy.136
  255.8 4.1 copy.116
  260.0 4.9 fusion.4
  267.3 3.4 broadcast_multiply_fusion.1
  270.7 6.4 %all-to-all-start.1 = ((f32[16,4,2,32,288]{4,3,2,1,0:T(8,128)}), f32[16,4,2,32,288]{4,3,2,1,0:T(8,128)}, u32[]{:S(2)}, u32[]{:S(2)}) async-start(f32[16,4,2,32,288]{4,3,2,1,0:T(8,128)} %broadcast_multiply_fusion.1), calls=%async_computation.1 | async-start | bytes 12582912 | tf_op jit(solution)/shard_map/all_to_all | solution.py:92
  277.3 4.6 fusion.10
  284.3 3.3 broadcast_multiply_fusion
  287.5 73.4 %all-to-all-done.1 = f32[16,4,2,32,288]{4,3,2,1,0:T(8,128)} async-done(((f32[16,4,2,32,288]{4,3,2,1,0:T(8,128)}), f32[16,4,2,32,288]{4,3,2,1,0:T(8,128)}, u32[]{:S(2)}, u32[]{:S(2)}) %all-to-all-start.1) | async-done | bytes 4718624 | tf_op jit(solution)/shard_map/all_to_all | solution.py:92
  360.9 6.6 %all-to-all-start.3 = ((f32[16,4,2,32,288]{4,3,2,1,0:T(8,128)}), f32[16,4,2,32,288]{4,3,2,1,0:T(8,128)}, u32[]{:S(2)}, u32[]{:S(2)}) async-start(f32[16,4,2,32,288]{4,3,2,1,0:T(8,128)} %broadcast_multiply_fusion), calls=%async_computation.3 | async-start | bytes 12582912 | tf_op jit(solution)/shard_map/all_to_all | solution.py:92
  367.5 6.9 %reshape.376 = f32[64,18432]{1,0:T(8,128)} reshape(f32[16,4,2,32,288]{4,3,2,1,0:T(8,128)} %all-to-all-done.1) | data formatting | bytes 9437184 | tf_op jit(solution)/shard_map/reshape | solution.py:93
  374.5 18.3 %fusion.123 = f32[18432,128]{1,0:T(8,128)} fusion(f32[64,18432]{1,0:T(8,128)} %reshape.376, f32[64,128]{1,0:T(8,128)S(1)} %copy-done.7), kind=kOutput, calls=%fused_computation.187 | convolution fusion | flops 1811939328 | bytes 14188544 | tf_op jit(solution)/shard_map/ax,ac->xc/dot_general | solution.py:96
  392.7 58.8 %all-to-all-done.3 = f32[16,4,2,32,288]{4,3,2,1,0:T(8,128)} async-done(((f32[16,4,2,32,288]{4,3,2,1,0:T(8,128)}), f32[16,4,2,32,288]{4,3,2,1,0:T(8,128)}, u32[]{:S(2)}, u32[]{:S(2)}) %all-to-all-start.3) | async-done | bytes 4718624 | tf_op jit(solution)/shard_map/all_to_all | solution.py:92
  451.6 6.9 %reshape.380 = f32[64,18432]{1,0:T(8,128)} reshape(f32[16,4,2,32,288]{4,3,2,1,0:T(8,128)} %all-to-all-done.3) | data formatting | bytes 9437184 | tf_op jit(solution)/shard_map/reshape | solution.py:93
  458.5 18.1 %convolution_add_fusion = f32[18432,128]{1,0:T(8,128)S(1)} fusion(f32[18432,128]{1,0:T(8,128)} %fusion.123, f32[64,18432]{1,0:T(8,128)} %reshape.380, f32[64,128]{1,0:T(8,128)S(1)} %copy-done.6), kind=kOutput, calls=%fused_computation.4 | convolution fusion | flops 1814298624 | bytes 23625728 | tf_op jit(solution)/shard_map/ax,ac->xc/dot_general | solution.py:96
  476.6 7.6 %copy.148 = f32[2,32,9,32,128]{4,1,3,2,0:T(8,128)S(1)} copy(f32[2,32,9,32,128]{4,3,2,1,0:T(8,128)S(1)} %bitcast.294) | data formatting | bytes 18874368 | tf_op jit(solution)/shard_map/reshape | solution.py:103
  484.2 4.9 reverse_bitcast_fusion
  (72 shorter events, 14.1 us)
Async XLA Ops:
  0.0 38.4 %copy-start = (s32[1024]{0:T(1024)S(1)}, s32[1024]{0:T(1024)}, u32[]{:S(2)}) copy-start(s32[1024]{0:T(1024)} %param.15) | copy-start | bytes 12292
  46.2 10.5 %copy-start.8 = (f32[4,2048]{1,0:T(4,128)S(1)}, f32[4,2048]{1,0:T(4,128)}, u32[]{:S(2)}) copy-start(f32[4,2048]{1,0:T(4,128)} %param.13) | copy-start | bytes 98308
  75.3 14.3 %copy-start.3 = (f32[128,4,2048]{2,1,0:T(4,128)S(1)}, f32[128,4,2048]{2,1,0:T(4,128)}, u32[]{:S(2)}) copy-start(f32[128,4,2048]{2,1,0:T(4,128)} %dot_general.59) | copy-start | bytes 12582916
  89.5 9.2 %copy-start.2 = (f32[4,256,2048,1]{2,1,0,3:T(8,128)}, f32[4,256,2048,1]{2,1,0,3:T(8,128)S(1)}, u32[]{:S(2)}) copy-start(f32[4,256,2048,1]{2,1,0,3:T(8,128)S(1)} %fusion.1) | copy-start | bytes 25165828
  89.6 9.2 %copy-start.4 = (f32[128,4,2048]{2,1,0:T(4,128)S(1)}, f32[128,4,2048]{2,1,0:T(4,128)}, u32[]{:S(2)}) copy-start(f32[128,4,2048]{2,1,0:T(4,128)} %dot_general.63) | copy-start | bytes 12582916
  108.3 12.8 %copy-start.9 = (s32[512]{0:T(512)S(1)}, s32[512]{0:T(512)}, u32[]{:S(2)}) copy-start(s32[512]{0:T(512)} %constant.87) | copy-start | bytes 6148
  111.4 69.1 %all-to-all-start.2 = ((bf16[128,4,4,2,256]{4,2,1,3,0:T(4,128)(2,1)}), bf16[128,4,4,2,256]{4,2,1,3,0:T(4,128)(2,1)S(1)}, u32[]{:S(2)}, u32[]{:S(2)}) async-start(bf16[128,4,4,2,256]{4,2,1,3,0:T(4,128)(2,1)} %copy.131), calls=%async_computation.2 | async-start | bytes 4194304 | tf_op jit(solution)/shard_map/all_to_all | solution.py:76
  150.0 14.2 %copy-start.5 = (f32[128,4,2048]{2,1,0:T(4,128)S(1)}, f32[128,4,2048]{2,1,0:T(4,128)}, u32[]{:S(2)}) copy-start(f32[128,4,2048]{2,1,0:T(4,128)} %dot_general.49) | copy-start | bytes 12582916
  180.5 39.5 %all-to-all-start = ((bf16[128,4,4,2,256]{4,2,1,3,0:T(4,128)(2,1)}), bf16[128,4,4,2,256]{4,2,1,3,0:T(4,128)(2,1)}, u32[]{:S(2)}, u32[]{:S(2)}) async-start(bf16[128,4,4,2,256]{4,2,1,3,0:T(4,128)(2,1)} %copy.111), calls=%async_computation | async-start | bytes 4194304 | tf_op jit(solution)/shard_map/all_to_all | solution.py:76
  270.7 90.2 %all-to-all-start.1 = ((f32[16,4,2,32,288]{4,3,2,1,0:T(8,128)}), f32[16,4,2,32,288]{4,3,2,1,0:T(8,128)}, u32[]{:S(2)}, u32[]{:S(2)}) async-start(f32[16,4,2,32,288]{4,3,2,1,0:T(8,128)} %broadcast_multiply_fusion.1), calls=%async_computation.1 | async-start | bytes 12582912 | tf_op jit(solution)/shard_map/all_to_all | solution.py:92
  360.9 90.6 %all-to-all-start.3 = ((f32[16,4,2,32,288]{4,3,2,1,0:T(8,128)}), f32[16,4,2,32,288]{4,3,2,1,0:T(8,128)}, u32[]{:S(2)}, u32[]{:S(2)}) async-start(f32[16,4,2,32,288]{4,3,2,1,0:T(8,128)} %broadcast_multiply_fusion), calls=%async_computation.3 | async-start | bytes 12582912 | tf_op jit(solution)/shard_map/all_to_all | solution.py:92
  367.5 7.0 %copy-start.7 = (f32[64,128]{1,0:T(8,128)S(1)}, f32[64,128]{1,0:T(8,128)}, u32[]{:S(2)}) copy-start(f32[64,128]{1,0:T(8,128)} %constant.82.clone) | copy-start | bytes 98308
  392.7 65.7 %copy-start.6 = (f32[64,128]{1,0:T(8,128)S(1)}, f32[64,128]{1,0:T(8,128)}, u32[]{:S(2)}) copy-start(f32[64,128]{1,0:T(8,128)} %constant.83.clone) | copy-start | bytes 98308
  476.6 12.4 %copy-start.1 = (s32[1024]{0:T(1024)S(1)}, s32[1024]{0:T(1024)}, u32[]{:S(2)}) copy-start(s32[1024]{0:T(1024)} %param.15) | copy-start | bytes 12292

commit v6 on v5

--- a/solution.py
+++ b/solution.py
@@ -86,14 +86,14 @@
         for own in range(n_blk):
             start = (own - steps + 1) % n_blk * tile
             blocks.append(doubled[:, :, own, :, start : start + rows])
-        return jnp.stack(blocks) * (1.0 / SPECTRA)
+        return (jnp.stack(blocks) * (1.0 / SPECTRA)).reshape(n_blk, -1)
 
     def half_output(banded, half):
         returned = lax.all_to_all(banded, "blk", 0, 0, tiled=True)
-        returned = returned.reshape(n_blk * part_chunk, 2 * tile * rows)
+        returned = returned.reshape(n_blk, part_chunk, 2 * tile * rows)
         source = np.arange(n_blk)[:, None] * chunk + half * part_chunk + np.arange(part_chunk)[None, :]
-        select = (source.reshape(-1, 1) == np.arange(n_blk * chunk)[None, :]).astype(np.float32)
-        return jnp.einsum("ax,ac->xc", returned, jnp.asarray(select), precision=lax.Precision.HIGHEST)
+        select = (source[:, :, None] == np.arange(n_blk * chunk)[None, None, :]).astype(np.float32)
+        return jnp.einsum("bkx,bkc->xc", returned, jnp.asarray(select), precision=lax.Precision.HIGHEST)
 
     spectra_parts = [half_spectra(half) for half in range(halves)]
     band_parts = [half_band(spectra) for spectra in spectra_parts]

time: 497 us -> 558 us (1.12)
  local copies, waits for them, and re-layouts: 127 us -> 196 us
  waiting for transfers between devices: 156 us -> 95 us
  other arithmetic: 44.2 us -> 94.5 us
    all_to_all x2, waiting for transfers between devices: 132 us -> 71.1 us  [half_output(): returned = lax.all_to_all(banded, 'blk', 0, 0, tiled=True)]
    another operation x2 -> x34, local copies, waits for them, and re-layouts: 0.33 us -> 56.6 us  [half_band(): return (jnp.stack(blocks) * (1.0 / SPECTRA)).reshape(n_blk, -1)]
    all_to_all x0 -> x2, other arithmetic: none -> 30.5 us  [half_output(): returned = lax.all_to_all(banded, 'blk', 0, 0, tiled=True)]
    unnamed x36 -> x100, local copies, waits for them, and re-layouts: 3.09 us -> 31.1 us
    reshape x2 -> x0, local copies, waits for them, and re-layouts: 13.9 us -> none  [half_output(): returned = returned.reshape(n_blk * part_chunk, 2 * tile * rows)]
    mul x2, other arithmetic: 6.67 us -> 19.6 us  [half_band(): return (jnp.stack(blocks) * (1.0 / SPECTRA)).reshape(n_blk, -1)]
    slice x0 -> x4, other arithmetic: none -> 8.07 us  [half_band(): blocks.append(doubled[:, :, own, :, start:start + rows])]
  transfers between devices with their start and end apart: 4 -> 4, of which waited for: 3 -> 3; matrix products, arithmetic and copies ran while one was open for 20% -> 22% of each run, Pallas kernels for 0% -> 0%
where the time goes in v6:
time: 558 us; the launch traced here: 549 us
  local copies, waits for them, and re-layouts  196 us (35%)
  waiting for transfers between devices  95 us (17%)
  other arithmetic  94.5 us (17%)
  matrix products  92.6 us (17%)
  blocking collectives  35.1 us (6%)
  starting transfers between devices  33.6 us (6%)
    all_to_all x2, waiting for transfers between devices, half_output(): returned = lax.all_to_all(banded, 'blk', 0, 0, tiled=True)  71.1 us
    another operation x34, local copies, waits for them, and re-layouts, half_band(): return (jnp.stack(blocks) * (1.0 / SPECTRA)).reshape(n_blk, -1)  56.6 us
    dot_general x4, matrix products, half_spectra(): jnp.einsum('mc,nm->cn', part, filtered, precision=lax.Precision.HIGH)  46.1 us
    dot_general x8, local copies, waits for them, and re-layouts, half_spectra(): jnp.einsum('mc,nm->cn', part, filtered, precision=lax.Precision.HIGH)  42.6 us
    dot_general x2, matrix products, half_output(): jnp.einsum('bkx,bkc->xc', returned, jnp.asarray(select), precision=lax.Pr...  36.7 us
    optimization_barrier x1, blocking collectives, per_device(): slot_order, chan_order = lax.optimization_barrier((slot_order, chan_order))  35.1 us
    unnamed x100, local copies, waits for them, and re-layouts  31.1 us
    all_to_all x2, other arithmetic, half_output(): returned = lax.all_to_all(banded, 'blk', 0, 0, tiled=True)  30.5 us
  transfers between devices with their start and end apart: 4, of which 3 were waited for; matrix products, arithmetic and copies ran while one was open for 22% of the time, Pallas kernels for 0%

profile of v6, /device:TPU:1, one launch (start us, length us, event | category | flops | bytes accessed | tf_op | source)
XLA Modules:
  0.0 548.8 jit_solution(16755965261043680664)
XLA Ops:
  2.7 35.1 %all-reduce = f32[512]{0:T(512)S(1)} all-reduce(f32[512]{0:T(512)S(1)} %convert_dynamic-update-slice_fusion), channel_id=1, replica_groups=mesh['blk'=16,'freq'=8] {'blk'}, use_global_device_ids=true, to_apply=%add | all-reduce | flops 512 | bytes 4096 | tf_op jit(solution)/shard_map/optimization_barrier | solution.py:51
  41.6 4.7 subtract_multiply_fusion
  46.2 5.4 copy.68
  51.7 5.2 dot_general.63
  56.9 7.9 %reshape.909 = f32[4,259,2048]{2,1,0:T(8,128)} reshape(bf16[4,530432]{1,0:T(4,128)(2,1)} %param.12) | data formatting | bytes 12730368 | tf_op jit(solution)/shard_map/reshape | solution.py:54
  64.7 5.4 copy.66
  70.2 5.2 dot_general.59
  75.4 14.2 %fusion.2 = f32[4,256,2048,1]{2,1,0,3:T(8,128)S(1)} fusion(f32[4,259,2048]{2,1,0:T(8,128)} %reshape.909, f32[2048]{0:T(1024)S(1)} %bitcast.168, f32[2048]{0:T(1024)S(1)} %bitcast.169, f32[2048]{0:T(1024)S(1)} %bitcast.167, f32[2048]{0:T(1024)S(1)} %bitcast.166), kind=kLoop, calls=%fused_computation.10 | loop fusion | flops 14680064 | bytes 41975808 | tf_op jit(solution)/shard_map/add | solution.py:57
  89.7 9.2 %fusion.43 = bf16[128,4,1,4,256]{4,0,3,1,2:T(8,128)(2,1)S(1)} fusion(f32[4,256,2048,1]{2,1,0,3:T(8,128)S(1)} %fusion.2, f32[128,4,2048,1]{2,1,0,3:T(4,128)S(1)} %bitcast.162), kind=kOutput, calls=%fused_computation.56 | convolution fusion | flops 6442975232 | bytes 13631488 | tf_op jit(solution)/shard_map/mc,nm->cn/dot_general | solution.py:68
  98.9 9.5 %fusion.46 = bf16[128,4,1,4,256]{4,0,3,1,2:T(8,128)(2,1)S(1)} fusion(f32[4,256,2048,1]{2,1,0,3:T(8,128)S(1)} %fusion.2, f32[128,4,2048,1]{2,1,0,3:T(4,128)S(1)} %bitcast.163), kind=kOutput, calls=%fused_computation.57 | convolution fusion | flops 6442975232 | bytes 13631488 | tf_op jit(solution)/shard_map/mc,nm->cn/dot_general | solution.py:68
  108.6 2.9 copy.70
  111.6 9.7 %all-to-all-start.2 = ((bf16[128,4,4,2,256]{4,2,1,3,0:T(4,128)(2,1)}), bf16[128,4,4,2,256]{4,2,1,3,0:T(4,128)(2,1)S(1)}, u32[]{:S(2)}, u32[]{:S(2)}) async-start(bf16[128,4,4,2,256]{4,2,1,3,0:T(4,128)(2,1)} %copy.70), calls=%async_computation.2 | async-start | bytes 4194304 | tf_op jit(solution)/shard_map/all_to_all | solution.py:76
  124.4 4.6 subtract_multiply_fusion.1
  129.0 5.4 copy.54
  134.4 5.2 dot_general.49
  139.7 5.4 copy.56
  145.1 5.2 dot_general.53
  150.3 14.2 %fusion.52 = bf16[128,4,1,4,256]{4,0,3,1,2:T(8,128)(2,1)S(1)} fusion(f32[4,256,2048,1]{2,1,0,3:T(8,128)} %copy-done.2, f32[128,4,2048,1]{2,1,0,3:T(4,128)} %bitcast.164), kind=kOutput, calls=%fused_computation.59 | convolution fusion | flops 6442975232 | bytes 13631488 | tf_op jit(solution)/shard_map/mc,nm->cn/dot_general | solution.py:68
  164.4 13.2 %fusion.49 = bf16[128,4,1,4,256]{4,0,3,1,2:T(8,128)(2,1)S(1)} fusion(f32[4,256,2048,1]{2,1,0,3:T(8,128)} %copy-done.2, f32[128,4,2048,1]{2,1,0,3:T(4,128)S(1)} %bitcast.165), kind=kOutput, calls=%fused_computation.58 | convolution fusion | flops 6442975232 | bytes 13631488 | tf_op jit(solution)/shard_map/mc,nm->cn/dot_general | solution.py:68
  177.9 2.9 copy.58
  180.8 10.8 %all-to-all-start = ((bf16[128,4,4,2,256]{4,2,1,3,0:T(4,128)(2,1)}), bf16[128,4,4,2,256]{4,2,1,3,0:T(4,128)(2,1)}, u32[]{:S(2)}, u32[]{:S(2)}) async-start(bf16[128,4,4,2,256]{4,2,1,3,0:T(4,128)(2,1)} %copy.58), calls=%async_computation | async-start | bytes 4194304 | tf_op jit(solution)/shard_map/all_to_all | solution.py:76
  193.9 2.7 copy.72
  196.6 23.8 %all-to-all-done = bf16[128,4,4,2,256]{4,2,1,3,0:T(4,128)(2,1)} async-done(((bf16[128,4,4,2,256]{4,2,1,3,0:T(4,128)(2,1)}), bf16[128,4,4,2,256]{4,2,1,3,0:T(4,128)(2,1)}, u32[]{:S(2)}, u32[]{:S(2)}) %all-to-all-start) | async-done | bytes 2097184 | tf_op jit(solution)/shard_map/all_to_all | solution.py:76
  220.4 3.7 copy.59
  224.2 4.0 copy.60
  228.2 3.9 gather_fusion.3
  232.1 5.4 gather_fusion.2
  237.5 5.2 fusion.30
  242.7 4.2 copy.62
  246.9 2.6 slice_bitcast_fusion.1
  249.5 4.1 copy.63
  253.7 4.9 fusion.9
  258.6 3.2 fusion.93
  266.8 2.8 copy.75
  269.5 4.9 fusion.15
  274.5 3.3 fusion.95
  353.6 9.8 %broadcast_multiply_fusion = f32[16,1,73728]{2,1,0:T(1,128)} fusion(f32[16,1,73728]{2,1,0:T(1,128)} %constant_dynamic-update-slice_fusion.16), kind=kLoop, calls=%fused_computation.44 | loop fusion | flops 1179648 | bytes 9437184 | tf_op jit(solution)/shard_map/mul | solution.py:89
  363.5 6.2 %all-to-all-start.3 = ((f32[16,1,73728]{2,1,0:T(1,128)}), f32[16,1,73728]{2,1,0:T(1,128)}, u32[]{:S(2)}, u32[]{:S(2)}) async-start(f32[16,1,73728]{2,1,0:T(1,128)} %broadcast_multiply_fusion), calls=%async_computation.3 | async-start | bytes 9437184 | tf_op jit(solution)/shard_map/all_to_all | solution.py:92
  380.8 9.7 %broadcast_multiply_fusion.1 = f32[16,1,73728]{2,1,0:T(1,128)} fusion(f32[16,1,73728]{2,1,0:T(1,128)} %constant_dynamic-update-slice_fusion), kind=kLoop, calls=%fused_computation.45 | loop fusion | flops 1179648 | bytes 9437184 | tf_op jit(solution)/shard_map/mul | solution.py:89
  390.6 41.9 %all-to-all-done.3 = f32[16,1,73728]{2,1,0:T(1,128)} async-done(((f32[16,1,73728]{2,1,0:T(1,128)}), f32[16,1,73728]{2,1,0:T(1,128)}, u32[]{:S(2)}, u32[]{:S(2)}) %all-to-all-start.3) | async-done | bytes 4718624 | tf_op jit(solution)/shard_map/all_to_all | solution.py:92
  432.4 6.9 %all-to-all-start.1 = ((f32[16,1,73728]{2,1,0:T(1,128)}), f32[16,1,73728]{2,1,0:T(1,128)}, u32[]{:S(2)}, u32[]{:S(2)}) async-start(f32[16,1,73728]{2,1,0:T(1,128)} %broadcast_multiply_fusion.1), calls=%async_computation.1 | async-start | bytes 9437184 | tf_op jit(solution)/shard_map/all_to_all | solution.py:92
  439.4 15.2 %reduce.1 = f32[16,73728]{1,0:T(8,128)} reduce(f32[16,1,73728]{2,1,0:T(1,128)} %all-to-all-done.3, f32[]{:T(128)} %constant.95), dimensions={1}, to_apply=%all_to_all.17.reduce_sub_computation | reduce | bytes 9437188 | tf_op jit(solution)/shard_map/all_to_all | solution.py:92
  454.6 18.3 %convolution_bitcast_fusion = f32[18432,128]{1,0:T(8,128)} fusion(f32[16,4,128]{2,0,1:T(8,128)S(1)} %copy-done.33, f32[2,4,8,18432]{3,2,1,0:T(8,128)} %bitcast.161), kind=kOutput, calls=%fused_computation.4 | convolution fusion | flops 1811939328 | bytes 14188544 | tf_op jit(solution)/shard_map/bkx,bkc->xc/dot_general | solution.py:96
  472.9 29.3 %all-to-all-done.1 = f32[16,1,73728]{2,1,0:T(1,128)} async-done(((f32[16,1,73728]{2,1,0:T(1,128)}), f32[16,1,73728]{2,1,0:T(1,128)}, u32[]{:S(2)}, u32[]{:S(2)}) %all-to-all-start.1) | async-done | bytes 4718624 | tf_op jit(solution)/shard_map/all_to_all | solution.py:92
  502.2 15.3 %reduce = f32[16,73728]{1,0:T(8,128)} reduce(f32[16,1,73728]{2,1,0:T(1,128)} %all-to-all-done.1, f32[]{:T(128)} %constant.95), dimensions={1}, to_apply=%all_to_all.15.reduce_sub_computation | reduce | bytes 9437188 | tf_op jit(solution)/shard_map/all_to_all | solution.py:92
  517.5 18.4 %fusion = f32[18432,128]{1,0:T(8,128)S(1)} fusion(f32[18432,128]{1,0:T(8,128)} %convolution_bitcast_fusion, f32[16,4,128]{2,0,1:T(8,128)S(1)} %copy-done.30, f32[2,4,8,18432]{3,2,1,0:T(8,128)} %bitcast.149), kind=kOutput, calls=%fused_computation.6 | convolution fusion | flops 1814298624 | bytes 23625728 | tf_op jit(solution)/shard_map/bkx,bkc->xc/dot_general | solution.py:96
  535.9 7.6 %copy.78 = f32[2,32,9,32,128]{4,1,3,2,0:T(8,128)S(1)} copy(f32[2,32,9,32,128]{4,3,2,1,0:T(8,128)S(1)} %bitcast.144) | data formatting | bytes 18874368 | tf_op jit(solution)/shard_map/reshape | solution.py:103
  543.5 4.9 reverse_bitcast_fusion
  (156 shorter events, 103.3 us)
Async XLA Ops:
  0.0 38.4 %copy-start = (s32[1024]{0:T(1024)S(1)}, s32[1024]{0:T(1024)}, u32[]{:S(2)}) copy-start(s32[1024]{0:T(1024)} %param.15) | copy-start | bytes 12292
  51.7 5.2 copy-start.31
  75.4 14.3 %copy-start.3 = (f32[128,4,2048]{2,1,0:T(4,128)S(1)}, f32[128,4,2048]{2,1,0:T(4,128)}, u32[]{:S(2)}) copy-start(f32[128,4,2048]{2,1,0:T(4,128)} %dot_general.63) | copy-start | bytes 12582916
  89.7 9.2 %copy-start.2 = (f32[4,256,2048,1]{2,1,0,3:T(8,128)}, f32[4,256,2048,1]{2,1,0,3:T(8,128)S(1)}, u32[]{:S(2)}) copy-start(f32[4,256,2048,1]{2,1,0,3:T(8,128)S(1)} %fusion.2) | copy-start | bytes 25165828
  89.7 9.2 %copy-start.4 = (f32[128,4,2048]{2,1,0:T(4,128)S(1)}, f32[128,4,2048]{2,1,0:T(4,128)}, u32[]{:S(2)}) copy-start(f32[128,4,2048]{2,1,0:T(4,128)} %dot_general.59) | copy-start | bytes 12582916
  108.6 12.6 %copy-start.32 = (s32[512]{0:T(512)S(1)}, s32[512]{0:T(512)}, u32[]{:S(2)}) copy-start(s32[512]{0:T(512)} %constant.87) | copy-start | bytes 6148
  111.6 69.3 %all-to-all-start.2 = ((bf16[128,4,4,2,256]{4,2,1,3,0:T(4,128)(2,1)}), bf16[128,4,4,2,256]{4,2,1,3,0:T(4,128)(2,1)S(1)}, u32[]{:S(2)}, u32[]{:S(2)}) async-start(bf16[128,4,4,2,256]{4,2,1,3,0:T(4,128)(2,1)} %copy.70), calls=%async_computation.2 | async-start | bytes 4194304 | tf_op jit(solution)/shard_map/all_to_all | solution.py:76
  150.3 14.2 %copy-start.5 = (f32[128,4,2048]{2,1,0:T(4,128)S(1)}, f32[128,4,2048]{2,1,0:T(4,128)}, u32[]{:S(2)}) copy-start(f32[128,4,2048]{2,1,0:T(4,128)} %dot_general.53) | copy-start | bytes 12582916
  180.8 39.6 %all-to-all-start = ((bf16[128,4,4,2,256]{4,2,1,3,0:T(4,128)(2,1)}), bf16[128,4,4,2,256]{4,2,1,3,0:T(4,128)(2,1)}, u32[]{:S(2)}, u32[]{:S(2)}) async-start(bf16[128,4,4,2,256]{4,2,1,3,0:T(4,128)(2,1)} %copy.58), calls=%async_computation | async-start | bytes 4194304 | tf_op jit(solution)/shard_map/all_to_all | solution.py:76
  278.2 17.4 %copy-start.6 = (f32[4,2,1,32,288]{4,3,2,1,0:T(8,128)S(1)}, f32[4,2,1,32,288]{4,3,2,1,0:T(8,128)}, u32[]{:S(2)}) copy-start(f32[4,2,1,32,288]{4,3,2,1,0:T(8,128)} %get-tuple-element.25) | copy-start | bytes 884740
  307.3 25.8 %copy-start.11 = (f32[4,2,1,32,288]{4,3,2,1,0:T(8,128)S(1)}, f32[4,2,1,32,288]{4,3,2,1,0:T(8,128)}, u32[]{:S(2)}) copy-start(f32[4,2,1,32,288]{4,3,2,1,0:T(8,128)} %get-tuple-element.37) | copy-start | bytes 884740
  309.6 24.1 %copy-start.10 = (f32[4,2,1,32,288]{4,3,2,1,0:T(8,128)S(1)}, f32[4,2,1,32,288]{4,3,2,1,0:T(8,128)}, u32[]{:S(2)}) copy-start(f32[4,2,1,32,288]{4,3,2,1,0:T(8,128)} %get-tuple-element.36) | copy-start | bytes 884740
  311.8 22.4 %copy-start.9 = (f32[4,2,1,32,288]{4,3,2,1,0:T(8,128)S(1)}, f32[4,2,1,32,288]{4,3,2,1,0:T(8,128)}, u32[]{:S(2)}) copy-start(f32[4,2,1,32,288]{4,3,2,1,0:T(8,128)} %get-tuple-element.35) | copy-start | bytes 884740
  313.4 21.4 %copy-start.8 = (f32[4,2,1,32,288]{4,3,2,1,0:T(8,128)S(1)}, f32[4,2,1,32,288]{4,3,2,1,0:T(8,128)}, u32[]{:S(2)}) copy-start(f32[4,2,1,32,288]{4,3,2,1,0:T(8,128)} %get-tuple-element.34) | copy-start | bytes 884740
  314.1 21.2 %copy-start.7 = (f32[4,2,1,32,288]{4,3,2,1,0:T(8,128)S(1)}, f32[4,2,1,32,288]{4,3,2,1,0:T(8,128)}, u32[]{:S(2)}) copy-start(f32[4,2,1,32,288]{4,3,2,1,0:T(8,128)} %get-tuple-element.26) | copy-start | bytes 884740
  333.6 14.8 %copy-start.27 = (f32[1,1,73728]{2,1,0:T(1,128)S(1)}, f32[1,1,73728]{2,1,0:T(1,128)}, u32[]{:S(2)}) copy-start(f32[1,1,73728]{2,1,0:T(1,128)} %stack.108) | copy-start | bytes 884740
  334.2 15.0 %copy-start.28 = (f32[1,1,73728]{2,1,0:T(1,128)S(1)}, f32[1,1,73728]{2,1,0:T(1,128)}, u32[]{:S(2)}) copy-start(f32[1,1,73728]{2,1,0:T(1,128)} %stack.109) | copy-start | bytes 884740
  334.7 13.0 %copy-start.29 = (f32[1,1,73728]{2,1,0:T(1,128)S(1)}, f32[1,1,73728]{2,1,0:T(1,128)}, u32[]{:S(2)}) copy-start(f32[1,1,73728]{2,1,0:T(1,128)} %stack.107) | copy-start | bytes 884740
  363.4 6.2 %copy-start.25 = (f32[1,1,73728]{2,1,0:T(1,128)S(1)}, f32[1,1,73728]{2,1,0:T(1,128)}, u32[]{:S(2)}) copy-start(f32[1,1,73728]{2,1,0:T(1,128)} %stack.82) | copy-start | bytes 884740
  363.4 7.0 %copy-start.26 = (f32[1,1,73728]{2,1,0:T(1,128)S(1)}, f32[1,1,73728]{2,1,0:T(1,128)}, u32[]{:S(2)}) copy-start(f32[1,1,73728]{2,1,0:T(1,128)} %stack.83) | copy-start | bytes 884740
  363.4 7.8 %copy-start.24 = (f32[1,1,73728]{2,1,0:T(1,128)S(1)}, f32[1,1,73728]{2,1,0:T(1,128)}, u32[]{:S(2)}) copy-start(f32[1,1,73728]{2,1,0:T(1,128)} %stack.84) | copy-start | bytes 884740
  363.4 8.5 %copy-start.23 = (f32[1,1,73728]{2,1,0:T(1,128)S(1)}, f32[1,1,73728]{2,1,0:T(1,128)}, u32[]{:S(2)}) copy-start(f32[1,1,73728]{2,1,0:T(1,128)} %stack.85) | copy-start | bytes 884740
  363.4 9.2 %copy-start.22 = (f32[1,1,73728]{2,1,0:T(1,128)S(1)}, f32[1,1,73728]{2,1,0:T(1,128)}, u32[]{:S(2)}) copy-start(f32[1,1,73728]{2,1,0:T(1,128)} %stack.86) | copy-start | bytes 884740
  363.4 10.0 %copy-start.21 = (f32[1,1,73728]{2,1,0:T(1,128)S(1)}, f32[1,1,73728]{2,1,0:T(1,128)}, u32[]{:S(2)}) copy-start(f32[1,1,73728]{2,1,0:T(1,128)} %stack.87) | copy-start | bytes 884740
  363.5 10.7 %copy-start.20 = (f32[1,1,73728]{2,1,0:T(1,128)S(1)}, f32[1,1,73728]{2,1,0:T(1,128)}, u32[]{:S(2)}) copy-start(f32[1,1,73728]{2,1,0:T(1,128)} %stack.88) | copy-start | bytes 884740
  363.5 11.4 %copy-start.19 = (f32[1,1,73728]{2,1,0:T(1,128)S(1)}, f32[1,1,73728]{2,1,0:T(1,128)}, u32[]{:S(2)}) copy-start(f32[1,1,73728]{2,1,0:T(1,128)} %stack.89) | copy-start | bytes 884740
  363.5 69.0 %all-to-all-start.3 = ((f32[16,1,73728]{2,1,0:T(1,128)}), f32[16,1,73728]{2,1,0:T(1,128)}, u32[]{:S(2)}, u32[]{:S(2)}) async-start(f32[16,1,73728]{2,1,0:T(1,128)} %broadcast_multiply_fusion), calls=%async_computation.3 | async-start | bytes 9437184 | tf_op jit(solution)/shard_map/all_to_all | solution.py:92
  369.7 6.0 %copy-start.17 = (f32[1,1,73728]{2,1,0:T(1,128)S(1)}, f32[1,1,73728]{2,1,0:T(1,128)}, u32[]{:S(2)}) copy-start(f32[1,1,73728]{2,1,0:T(1,128)} %stack.90) | copy-start | bytes 884740
  369.7 6.7 %copy-start.18 = (f32[1,1,73728]{2,1,0:T(1,128)S(1)}, f32[1,1,73728]{2,1,0:T(1,128)}, u32[]{:S(2)}) copy-start(f32[1,1,73728]{2,1,0:T(1,128)} %stack.91) | copy-start | bytes 884740
  369.7 7.4 %copy-start.16 = (f32[1,1,73728]{2,1,0:T(1,128)S(1)}, f32[1,1,73728]{2,1,0:T(1,128)}, u32[]{:S(2)}) copy-start(f32[1,1,73728]{2,1,0:T(1,128)} %stack.92) | copy-start | bytes 884740
  369.7 8.2 %copy-start.15 = (f32[1,1,73728]{2,1,0:T(1,128)S(1)}, f32[1,1,73728]{2,1,0:T(1,128)}, u32[]{:S(2)}) copy-start(f32[1,1,73728]{2,1,0:T(1,128)} %stack.93) | copy-start | bytes 884740
  369.7 8.9 %copy-start.14 = (f32[1,1,73728]{2,1,0:T(1,128)S(1)}, f32[1,1,73728]{2,1,0:T(1,128)}, u32[]{:S(2)}) copy-start(f32[1,1,73728]{2,1,0:T(1,128)} %stack.94) | copy-start | bytes 884740
  369.7 9.6 %copy-start.12 = (f32[1,1,73728]{2,1,0:T(1,128)S(1)}, f32[1,1,73728]{2,1,0:T(1,128)}, u32[]{:S(2)}) copy-start(f32[1,1,73728]{2,1,0:T(1,128)} %stack.95) | copy-start | bytes 884740
  369.7 10.4 %copy-start.13 = (f32[1,1,73728]{2,1,0:T(1,128)S(1)}, f32[1,1,73728]{2,1,0:T(1,128)}, u32[]{:S(2)}) copy-start(f32[1,1,73728]{2,1,0:T(1,128)} %stack.96) | copy-start | bytes 884740
  432.4 69.7 %all-to-all-start.1 = ((f32[16,1,73728]{2,1,0:T(1,128)}), f32[16,1,73728]{2,1,0:T(1,128)}, u32[]{:S(2)}, u32[]{:S(2)}) async-start(f32[16,1,73728]{2,1,0:T(1,128)} %broadcast_multiply_fusion.1), calls=%async_computation.1 | async-start | bytes 9437184 | tf_op jit(solution)/shard_map/all_to_all | solution.py:92
  439.3 15.3 %copy-start.33 = (f32[16,4,128]{2,0,1:T(8,128)S(1)}, f32[16,4,128]{2,0,1:T(8,128)}, u32[]{:S(2)}) copy-start(f32[16,4,128]{2,0,1:T(8,128)} %constant.83.clone) | copy-start | bytes 98308
  472.9 44.6 %copy-start.30 = (f32[16,4,128]{2,0,1:T(8,128)S(1)}, f32[16,4,128]{2,0,1:T(8,128)}, u32[]{:S(2)}) copy-start(f32[16,4,128]{2,0,1:T(8,128)} %constant.82.clone) | copy-start | bytes 98308
  543.4 4.9 copy-start.1

commit v7 on v5

--- a/solution.py
+++ b/solution.py
@@ -38,7 +38,7 @@
     channel_count = chan_order.shape[0]
     width = channel_count // n_freq
     chunk = width // n_blk
-    halves = 2
+    halves = 4
     part_chunk = chunk // halves
     steps = n_blk // 2 + 1
     tile = input_order.shape[0]
@@ -47,9 +47,9 @@
     frame = 2 * channel_count
     rows = steps * tile
 
-    slot_order = lax.all_gather(input_order.astype(jnp.float32), "blk", tiled=True)
-    slot_order, chan_order = lax.optimization_barrier((slot_order, chan_order))
-    slot_order = slot_order.astype(jnp.int32)
+    spread = jnp.broadcast_to(input_order.astype(jnp.float32)[None], (n_dev, tile))
+    slot_order = lax.all_to_all(spread, ("blk", "freq"), 0, 0, tiled=True)
+    slot_order = slot_order.reshape(n_blk, n_freq, tile)[:, 0].reshape(-1).astype(jnp.int32)
 
     frames = raw_voltages.astype(jnp.float32).reshape(local_inputs, SPECTRA + TAPS - 1, frame)
     filtered = filter_taps[0] * frames[:, 0:SPECTRA]

time: 497 us -> 519 us (1.044)
  waiting for transfers between devices: 156 us -> 75.1 us
  local copies, waits for them, and re-layouts: 127 us -> 179 us
  matrix products: 92 us -> 134 us
  starting transfers between devices: 33.5 us -> 70.2 us
  blocking collectives: 35.1 us -> 0 us
  other arithmetic: 44.2 us -> 50.6 us
    all_to_all x2 -> x4, waiting for transfers between devices: 132 us -> 61.4 us  [half_output(): returned = lax.all_to_all(banded, 'blk', 0, 0, tiled=True)]
    unnamed x36 -> x90, local copies, waits for them, and re-layouts: 3.09 us -> 44.4 us
    optimization_barrier x1 -> x0, blocking collectives: 35.1 us -> none  [per_device(): slot_order, chan_order = lax.optimization_barrier((slot_order, chan_order))]
    dot_general x2 -> x4, matrix products: 36.4 us -> 67.7 us  [half_output(): jnp.einsum('ax,ac->xc', returned, jnp.asarray(select), precision=lax.Prec...]
    all_to_all x2 -> x4, starting transfers between devices: 13 us -> 26 us  [half_output(): returned = lax.all_to_all(banded, 'blk', 0, 0, tiled=True)]
    all_to_all x2 -> x4, starting transfers between devices: 20.5 us -> 32.7 us  [half_band(): gathered = lax.all_to_all(spectra, ('blk', 'freq'), 0, 0, tiled=True)]
    dot_general x4 -> x8, matrix products: 46.1 us -> 57.8 us  [half_spectra(): jnp.einsum('mc,nm->cn', part, filtered, precision=lax.Precision.HIGH)]
    all_to_all x0 -> x1, starting transfers between devices: none -> 11.5 us  [per_device(): slot_order = lax.all_to_all(spread, ('blk', 'freq'), 0, 0, tiled=True)]
  transfers between devices with their start and end apart: 4 -> 9, of which waited for: 3 -> 6; matrix products, arithmetic and copies ran while one was open for 20% -> 56% of each run, Pallas kernels for 0% -> 0%
where the time goes in v7:
time: 519 us; the launch traced here: 510 us
  local copies, waits for them, and re-layouts  179 us (34%)
  matrix products  134 us (26%)
  waiting for transfers between devices  75.1 us (14%)
  starting transfers between devices  70.2 us (14%)
  other arithmetic  50.6 us (10%)
    dot_general x4, matrix products, half_output(): jnp.einsum('ax,ac->xc', returned, jnp.asarray(select), precision=lax.Prec...  67.7 us
    all_to_all x4, waiting for transfers between devices, half_output(): returned = lax.all_to_all(banded, 'blk', 0, 0, tiled=True)  61.4 us
    dot_general x8, matrix products, half_spectra(): jnp.einsum('mc,nm->cn', part, filtered, precision=lax.Precision.HIGH)  57.8 us
    dot_general x16, local copies, waits for them, and re-layouts, half_spectra(): jnp.einsum('mc,nm->cn', part, filtered, precision=lax.Precision.HIGH)  44.5 us
    unnamed x90, local copies, waits for them, and re-layouts  44.4 us
    all_to_all x4, starting transfers between devices, half_band(): gathered = lax.all_to_all(spectra, ('blk', 'freq'), 0, 0, tiled=True)  32.7 us
    all_to_all x4, starting transfers between devices, half_output(): returned = lax.all_to_all(banded, 'blk', 0, 0, tiled=True)  26 us
    gather x4, local copies, waits for them, and re-layouts, half_band(): slotted = jnp.take(gathered, slot_order, axis=1)  16.5 us
  transfers between devices with their start and end apart: 9, of which 6 were waited for; matrix products, arithmetic and copies ran while one was open for 56% of the time, Pallas kernels for 0%

profile of v7, /device:TPU:1, one launch (start us, length us, event | category | flops | bytes accessed | tf_op | source)
XLA Modules:
  0.0 509.9 jit_solution(13992007160743969511)
XLA Ops:
  1.3 11.5 %all-to-all-start.1 = ((f32[128,1,32]{2,1,0:T(1,128)}), f32[128,1,32]{2,1,0:T(1,128)S(1)}, u32[]{:S(2)}, u32[]{:S(2)}) async-start(f32[128,1,32]{2,1,0:T(1,128)} %broadcast_in_dim.17), calls=%async_computation.1 | async-start | bytes 131072 | tf_op jit(solution)/shard_map/all_to_all | solution.py:51
  19.3 7.9 %reshape.755 = f32[4,259,2048]{2,1,0:T(8,128)} reshape(bf16[4,530432]{1,0:T(4,128)(2,1)} %param.18) | data formatting | bytes 12730368 | tf_op jit(solution)/shard_map/reshape | solution.py:54
  29.3 2.9 copy.242
  32.2 3.5 dot_general.121
  40.0 14.0 %fusion.1 = f32[4,256,2048,1]{2,1,0,3:T(8,128)S(1)} fusion(f32[4,259,2048]{2,1,0:T(8,128)} %reshape.755, f32[2048]{0:T(1024)S(1)} %bitcast.613, f32[2048]{0:T(1024)S(1)} %bitcast.614, f32[2048]{0:T(1024)S(1)} %bitcast.612, f32[2048]{0:T(1024)S(1)} %bitcast.611), kind=kLoop, calls=%fused_computation.14 | loop fusion | flops 14680064 | bytes 41975808 | tf_op jit(solution)/shard_map/add | solution.py:57
  54.0 5.9 %fusion.74 = bf16[128,2,1,4,256]{4,0,3,1,2:T(8,128)(2,1)} fusion(f32[4,256,2048,1]{2,1,0,3:T(8,128)S(1)} %fusion.1, f32[128,2,2048,1]{2,1,0,3:T(2,128)S(1)} %bitcast.591), kind=kOutput, calls=%fused_computation.82 | convolution fusion | flops 3221487616 | bytes 11010048 | tf_op jit(solution)/shard_map/mc,nm->cn/dot_general | solution.py:68
  59.9 5.9 %fusion.77 = bf16[128,2,1,4,256]{4,0,3,1,2:T(8,128)(2,1)} fusion(f32[4,256,2048,1]{2,1,0,3:T(8,128)S(1)} %fusion.1, f32[128,2,2048,1]{2,1,0,3:T(2,128)S(1)} %bitcast.593), kind=kOutput, calls=%fused_computation.83 | convolution fusion | flops 3221487616 | bytes 11010048 | tf_op jit(solution)/shard_map/mc,nm->cn/dot_general | solution.py:68
  70.9 3.6 dot_general.127
  74.5 8.6 %fusion.71 = bf16[128,2,1,4,256]{4,0,3,1,2:T(8,128)(2,1)S(1)} fusion(f32[4,256,2048,1]{2,1,0,3:T(8,128)} %copy-done.2, f32[128,2,2048,1]{2,1,0,3:T(2,128)} %bitcast.594), kind=kOutput, calls=%fused_computation.81 | convolution fusion | flops 3221487616 | bytes 11010048 | tf_op jit(solution)/shard_map/mc,nm->cn/dot_general | solution.py:68
  87.5 6.9 %fusion.68 = bf16[128,2,1,4,256]{4,0,3,1,2:T(8,128)(2,1)S(1)} fusion(f32[4,256,2048,1]{2,1,0,3:T(8,128)} %copy-done.2, f32[128,2,2048,1]{2,1,0,3:T(2,128)S(1)} %bitcast.595), kind=kOutput, calls=%fused_computation.80 | convolution fusion | flops 3221487616 | bytes 11010048 | tf_op jit(solution)/shard_map/mc,nm->cn/dot_general | solution.py:68
  99.4 3.8 dot_general.101
  103.3 9.5 %fusion.86 = bf16[128,2,1,4,256]{4,0,3,1,2:T(8,128)(2,1)} fusion(f32[4,256,2048,1]{2,1,0,3:T(8,128)} %copy-done.2, f32[128,2,2048,1]{2,1,0,3:T(2,128)} %bitcast.596), kind=kOutput, calls=%fused_computation.86 | convolution fusion | flops 3221487616 | bytes 11010048 | tf_op jit(solution)/shard_map/mc,nm->cn/dot_general | solution.py:68
  121.0 9.8 %all-to-all-start.5 = ((bf16[128,2,4,2,256]{4,2,1,3,0:T(4,128)(2,1)}), bf16[128,2,4,2,256]{4,2,1,3,0:T(4,128)(2,1)S(1)}, u32[]{:S(2)}, u32[]{:S(2)}) async-start(bf16[128,2,4,2,256]{4,2,1,3,0:T(4,128)(2,1)} %copy.244), calls=%async_computation.5 | async-start | bytes 2097152 | tf_op jit(solution)/shard_map/all_to_all | solution.py:76
  130.8 7.0 %fusion.89 = bf16[128,2,1,4,256]{4,0,3,1,2:T(8,128)(2,1)S(1)} fusion(f32[4,256,2048,1]{2,1,0,3:T(8,128)} %copy-done.2, f32[128,2,2048,1]{2,1,0,3:T(2,128)S(1)} %bitcast.592), kind=kOutput, calls=%fused_computation.87 | convolution fusion | flops 3221487616 | bytes 11010048 | tf_op jit(solution)/shard_map/mc,nm->cn/dot_general | solution.py:68
  139.8 9.3 %all-to-all-done.5 = bf16[128,2,4,2,256]{4,2,1,3,0:T(4,128)(2,1)S(1)} async-done(((bf16[128,2,4,2,256]{4,2,1,3,0:T(4,128)(2,1)}), bf16[128,2,4,2,256]{4,2,1,3,0:T(4,128)(2,1)S(1)}, u32[]{:S(2)}, u32[]{:S(2)}) %all-to-all-start.5) | async-done | bytes 1048608 | tf_op jit(solution)/shard_map/all_to_all | solution.py:76
  149.0 6.3 %all-to-all-start.7 = ((bf16[128,2,4,2,256]{4,2,1,3,0:T(4,128)(2,1)}), bf16[128,2,4,2,256]{4,2,1,3,0:T(4,128)(2,1)}, u32[]{:S(2)}, u32[]{:S(2)}) async-start(bf16[128,2,4,2,256]{4,2,1,3,0:T(4,128)(2,1)} %copy.264), calls=%async_computation.7 | async-start | bytes 2097152 | tf_op jit(solution)/shard_map/all_to_all | solution.py:76
  162.1 3.5 dot_general.111
  167.4 3.6 dot_general.107
  173.4 8.0 %all-to-all-start = ((bf16[128,2,4,2,256]{4,2,1,3,0:T(4,128)(2,1)}), bf16[128,2,4,2,256]{4,2,1,3,0:T(4,128)(2,1)}, u32[]{:S(2)}, u32[]{:S(2)}) async-start(bf16[128,2,4,2,256]{4,2,1,3,0:T(4,128)(2,1)} %copy.205), calls=%async_computation | async-start | bytes 2097152 | tf_op jit(solution)/shard_map/all_to_all | solution.py:76
  181.4 7.1 %fusion.80 = bf16[128,2,1,4,256]{4,0,3,1,2:T(8,128)(2,1)S(1)} fusion(f32[4,256,2048,1]{2,1,0,3:T(8,128)} %copy-done.2, f32[128,2,2048,1]{2,1,0,3:T(2,128)S(1)} %bitcast.589), kind=kOutput, calls=%fused_computation.84 | convolution fusion | flops 3221487616 | bytes 11010048 | tf_op jit(solution)/shard_map/mc,nm->cn/dot_general | solution.py:68
  188.5 6.9 %fusion.83 = bf16[128,2,1,4,256]{4,0,3,1,2:T(8,128)(2,1)S(1)} fusion(f32[4,256,2048,1]{2,1,0,3:T(8,128)} %copy-done.2, f32[128,2,2048,1]{2,1,0,3:T(2,128)S(1)} %bitcast.590), kind=kOutput, calls=%fused_computation.85 | convolution fusion | flops 3221487616 | bytes 11010048 | tf_op jit(solution)/shard_map/mc,nm->cn/dot_general | solution.py:68
  199.3 8.7 %all-to-all-start.3 = ((bf16[128,2,4,2,256]{4,2,1,3,0:T(4,128)(2,1)}), bf16[128,2,4,2,256]{4,2,1,3,0:T(4,128)(2,1)}, u32[]{:S(2)}, u32[]{:S(2)}) async-start(bf16[128,2,4,2,256]{4,2,1,3,0:T(4,128)(2,1)} %copy.224), calls=%async_computation.3 | async-start | bytes 2097152 | tf_op jit(solution)/shard_map/all_to_all | solution.py:76
  211.4 4.1 gather_fusion.6
  215.5 4.1 gather_fusion.7
  221.9 4.1 gather_fusion.4
  228.3 4.1 gather_fusion.5
  232.4 3.9 fusion.92
  259.9 7.7 %all-to-all-start.6 = ((f32[16,2,2,32,288]{4,3,2,1,0:T(8,128)}), f32[16,2,2,32,288]{4,3,2,1,0:T(8,128)S(1)}, u32[]{:S(2)}, u32[]{:S(2)}) async-start(f32[16,2,2,32,288]{4,3,2,1,0:T(8,128)} %broadcast_multiply_fusion.1), calls=%async_computation.6 | async-start | bytes 6291456 | tf_op jit(solution)/shard_map/all_to_all | solution.py:92
  269.9 3.1 fusion.10
  279.1 3.1 fusion.4
  296.5 13.0 %all-to-all-done.6 = f32[16,2,2,32,288]{4,3,2,1,0:T(8,128)S(1)} async-done(((f32[16,2,2,32,288]{4,3,2,1,0:T(8,128)}), f32[16,2,2,32,288]{4,3,2,1,0:T(8,128)S(1)}, u32[]{:S(2)}, u32[]{:S(2)}) %all-to-all-start.6) | async-done | bytes 2359328 | tf_op jit(solution)/shard_map/all_to_all | solution.py:92
  311.1 6.1 %all-to-all-start.4 = ((f32[16,2,2,32,288]{4,3,2,1,0:T(8,128)}), f32[16,2,2,32,288]{4,3,2,1,0:T(8,128)}, u32[]{:S(2)}, u32[]{:S(2)}) async-start(f32[16,2,2,32,288]{4,3,2,1,0:T(8,128)} %broadcast_multiply_fusion.2), calls=%async_computation.4 | async-start | bytes 6291456 | tf_op jit(solution)/shard_map/all_to_all | solution.py:92
  330.9 4.0 broadcast_multiply_fusion.3
  334.9 24.2 %all-to-all-done.4 = f32[16,2,2,32,288]{4,3,2,1,0:T(8,128)} async-done(((f32[16,2,2,32,288]{4,3,2,1,0:T(8,128)}), f32[16,2,2,32,288]{4,3,2,1,0:T(8,128)}, u32[]{:S(2)}, u32[]{:S(2)}) %all-to-all-start.4) | async-done | bytes 2359328 | tf_op jit(solution)/shard_map/all_to_all | solution.py:92
  359.1 6.2 %all-to-all-start.2 = ((f32[16,2,2,32,288]{4,3,2,1,0:T(8,128)}), f32[16,2,2,32,288]{4,3,2,1,0:T(8,128)S(1)}, u32[]{:S(2)}, u32[]{:S(2)}) async-start(f32[16,2,2,32,288]{4,3,2,1,0:T(8,128)} %broadcast_multiply_fusion.3), calls=%async_computation.2 | async-start | bytes 6291456 | tf_op jit(solution)/shard_map/all_to_all | solution.py:92
  378.9 3.9 broadcast_multiply_fusion
  382.8 24.3 %all-to-all-done.2 = f32[16,2,2,32,288]{4,3,2,1,0:T(8,128)S(1)} async-done(((f32[16,2,2,32,288]{4,3,2,1,0:T(8,128)}), f32[16,2,2,32,288]{4,3,2,1,0:T(8,128)S(1)}, u32[]{:S(2)}, u32[]{:S(2)}) %all-to-all-start.2) | async-done | bytes 2359328 | tf_op jit(solution)/shard_map/all_to_all | solution.py:92
  408.8 6.1 %all-to-all-start.8 = ((f32[16,2,2,32,288]{4,3,2,1,0:T(8,128)}), f32[16,2,2,32,288]{4,3,2,1,0:T(8,128)}, u32[]{:S(2)}, u32[]{:S(2)}) async-start(f32[16,2,2,32,288]{4,3,2,1,0:T(8,128)} %broadcast_multiply_fusion), calls=%async_computation.8 | async-start | bytes 6291456 | tf_op jit(solution)/shard_map/all_to_all | solution.py:92
  414.8 3.1 reshape.748
  417.9 4.1 reshape.744
  422.0 4.3 reshape.740
  426.3 16.9 %fusion.242 = f32[18432,128]{1,0:T(8,128)S(1)} fusion(f32[32,18432]{1,0:T(8,128)} %reshape.740, f32[32,128]{1,0:T(8,128)S(1)} %copy-done.29), kind=kOutput, calls=%fused_computation.362 | convolution fusion | flops 905969664 | bytes 11812864 | tf_op jit(solution)/shard_map/ax,ac->xc/dot_general | solution.py:96
  443.3 15.2 %convolution_add_fusion.2 = f32[18432,128]{1,0:T(8,128)S(1)} fusion(f32[18432,128]{1,0:T(8,128)S(1)} %fusion.242, f32[32,18432]{1,0:T(8,128)S(1)} %copy-done.6, f32[32,128]{1,0:T(8,128)S(1)} %copy-done.28), kind=kOutput, calls=%fused_computation.10 | convolution fusion | flops 908328960 | bytes 21250048 | tf_op jit(solution)/shard_map/ax,ac->xc/dot_general | solution.py:96
  458.5 17.6 %convolution_add_fusion.1 = f32[18432,128]{1,0:T(8,128)} fusion(f32[18432,128]{1,0:T(8,128)S(1)} %convolution_add_fusion.2, f32[32,18432]{1,0:T(8,128)S(1)} %reshape.748, f32[32,128]{1,0:T(8,128)S(1)} %copy-done.27), kind=kOutput, calls=%fused_computation.9 | convolution fusion | flops 908328960 | bytes 21250048 | tf_op jit(solution)/shard_map/ax,ac->xc/dot_general | solution.py:96
  476.1 3.1 reshape.752
  479.2 18.0 %convolution_add_fusion = f32[18432,128]{1,0:T(8,128)S(1)} fusion(f32[18432,128]{1,0:T(8,128)} %convolution_add_fusion.1, f32[32,18432]{1,0:T(8,128)S(1)} %reshape.752, f32[32,128]{1,0:T(8,128)S(1)} %copy-done.26), kind=kOutput, calls=%fused_computation.8 | convolution fusion | flops 908328960 | bytes 21250048 | tf_op jit(solution)/shard_map/ax,ac->xc/dot_general | solution.py:96
  497.2 7.6 %copy.280 = f32[2,32,9,32,128]{4,1,3,2,0:T(8,128)S(1)} copy(f32[2,32,9,32,128]{4,3,2,1,0:T(8,128)S(1)} %bitcast.580) | data formatting | bytes 18874368 | tf_op jit(solution)/shard_map/reshape | solution.py:103
  504.8 4.9 reverse_bitcast_fusion
  (199 shorter events, 138.1 us)
Async XLA Ops:
  0.0 13.5 %copy-start = (s32[1024]{0:T(1024)S(1)}, s32[1024]{0:T(1024)}, u32[]{:S(2)}) copy-start(s32[1024]{0:T(1024)} %param.21) | copy-start | bytes 12292
  0.0 19.2 %copy-start.25 = (f32[4,2048]{1,0:T(4,128)S(1)}, f32[4,2048]{1,0:T(4,128)}, u32[]{:S(2)}) copy-start(f32[4,2048]{1,0:T(4,128)} %param.19) | copy-start | bytes 98308
  1.3 119.6 %all-to-all-start.1 = ((f32[128,1,32]{2,1,0:T(1,128)}), f32[128,1,32]{2,1,0:T(1,128)S(1)}, u32[]{:S(2)}, u32[]{:S(2)}) async-start(f32[128,1,32]{2,1,0:T(1,128)} %broadcast_in_dim.17), calls=%async_computation.1 | async-start | bytes 131072 | tf_op jit(solution)/shard_map/all_to_all | solution.py:51
  40.0 14.0 %copy-start.11 = (f32[128,2,2048]{2,1,0:T(2,128)S(1)}, f32[128,2,2048]{2,1,0:T(2,128)}, u32[]{:S(2)}) copy-start(f32[128,2,2048]{2,1,0:T(2,128)} %dot_general.121) | copy-start | bytes 6291460
  54.0 5.9 %copy-start.2 = (f32[4,256,2048,1]{2,1,0,3:T(8,128)}, f32[4,256,2048,1]{2,1,0,3:T(8,128)S(1)}, u32[]{:S(2)}) copy-start(f32[4,256,2048,1]{2,1,0,3:T(8,128)S(1)} %fusion.1) | copy-start | bytes 25165828
  103.3 9.5 %copy-start.18 = (bf16[128,2,1,4,256]{4,0,3,1,2:T(8,128)(2,1)S(1)}, bf16[128,2,1,4,256]{4,0,3,1,2:T(8,128)(2,1)}, u32[]{:S(2)}) copy-start(bf16[128,2,1,4,256]{4,0,3,1,2:T(8,128)(2,1)} %fusion.74) | copy-start | bytes 1572868
  103.3 9.5 %copy-start.19 = (bf16[128,2,1,4,256]{4,0,3,1,2:T(8,128)(2,1)S(1)}, bf16[128,2,1,4,256]{4,0,3,1,2:T(8,128)(2,1)}, u32[]{:S(2)}) copy-start(bf16[128,2,1,4,256]{4,0,3,1,2:T(8,128)(2,1)} %fusion.77) | copy-start | bytes 1572868
  121.0 28.1 %all-to-all-start.5 = ((bf16[128,2,4,2,256]{4,2,1,3,0:T(4,128)(2,1)}), bf16[128,2,4,2,256]{4,2,1,3,0:T(4,128)(2,1)S(1)}, u32[]{:S(2)}, u32[]{:S(2)}) async-start(bf16[128,2,4,2,256]{4,2,1,3,0:T(4,128)(2,1)} %copy.244), calls=%async_computation.5 | async-start | bytes 2097152 | tf_op jit(solution)/shard_map/all_to_all | solution.py:76
  130.8 7.0 %copy-start.20 = (bf16[128,2,1,4,256]{4,0,3,1,2:T(8,128)(2,1)S(1)}, bf16[128,2,1,4,256]{4,0,3,1,2:T(8,128)(2,1)}, u32[]{:S(2)}) copy-start(bf16[128,2,1,4,256]{4,0,3,1,2:T(8,128)(2,1)} %fusion.86) | copy-start | bytes 1572868
  137.8 17.6 %copy-start.30 = (s32[256]{0:T(256)S(1)}, s32[256]{0:T(256)}, u32[]{:S(2)}) copy-start(s32[256]{0:T(256)} %constant.132) | copy-start | bytes 3076
  149.0 24.3 %all-to-all-start.7 = ((bf16[128,2,4,2,256]{4,2,1,3,0:T(4,128)(2,1)}), bf16[128,2,4,2,256]{4,2,1,3,0:T(4,128)(2,1)}, u32[]{:S(2)}, u32[]{:S(2)}) async-start(bf16[128,2,4,2,256]{4,2,1,3,0:T(4,128)(2,1)} %copy.264), calls=%async_computation.7 | async-start | bytes 2097152 | tf_op jit(solution)/shard_map/all_to_all | solution.py:76
  167.4 14.0 %copy-start.9 = (f32[128,2,2048]{2,1,0:T(2,128)S(1)}, f32[128,2,2048]{2,1,0:T(2,128)}, u32[]{:S(2)}) copy-start(f32[128,2,2048]{2,1,0:T(2,128)} %dot_general.111) | copy-start | bytes 6291460
  173.4 25.9 %all-to-all-start = ((bf16[128,2,4,2,256]{4,2,1,3,0:T(4,128)(2,1)}), bf16[128,2,4,2,256]{4,2,1,3,0:T(4,128)(2,1)}, u32[]{:S(2)}, u32[]{:S(2)}) async-start(bf16[128,2,4,2,256]{4,2,1,3,0:T(4,128)(2,1)} %copy.205), calls=%async_computation | async-start | bytes 2097152 | tf_op jit(solution)/shard_map/all_to_all | solution.py:76
  181.4 7.1 %copy-start.10 = (f32[128,2,2048]{2,1,0:T(2,128)S(1)}, f32[128,2,2048]{2,1,0:T(2,128)}, u32[]{:S(2)}) copy-start(f32[128,2,2048]{2,1,0:T(2,128)} %dot_general.107) | copy-start | bytes 6291460
  199.3 26.7 %all-to-all-start.3 = ((bf16[128,2,4,2,256]{4,2,1,3,0:T(4,128)(2,1)}), bf16[128,2,4,2,256]{4,2,1,3,0:T(4,128)(2,1)}, u32[]{:S(2)}, u32[]{:S(2)}) async-start(bf16[128,2,4,2,256]{4,2,1,3,0:T(4,128)(2,1)} %copy.224), calls=%async_computation.3 | async-start | bytes 2097152 | tf_op jit(solution)/shard_map/all_to_all | solution.py:76
  245.1 3.4 copy-start.13
  246.2 2.9 copy-start.23
  246.2 2.9 copy-start.24
  250.4 2.0 copy-start.3
  252.4 1.8 copy-start.12
  252.4 2.3 copy-start.21
  252.4 2.6 copy-start.22
  252.5 1.6 copy-start.14
  259.9 49.6 %all-to-all-start.6 = ((f32[16,2,2,32,288]{4,3,2,1,0:T(8,128)}), f32[16,2,2,32,288]{4,3,2,1,0:T(8,128)S(1)}, u32[]{:S(2)}, u32[]{:S(2)}) async-start(f32[16,2,2,32,288]{4,3,2,1,0:T(8,128)} %broadcast_multiply_fusion.1), calls=%async_computation.6 | async-start | bytes 6291456 | tf_op jit(solution)/shard_map/all_to_all | solution.py:92
  273.0 2.0 copy-start.5
  275.2 1.7 copy-start.15
  282.2 2.0 copy-start.4
  284.2 1.9 copy-start.16
  286.1 7.4 %copy-start.17 = (f32[16,2,2,32,288]{4,3,2,1,0:T(8,128)}, f32[16,2,2,32,288]{4,3,2,1,0:T(8,128)S(1)}, u32[]{:S(2)}) copy-start(f32[16,2,2,32,288]{4,3,2,1,0:T(8,128)S(1)} %fusion.160) | copy-start | bytes 7077892
  309.5 1.7 copy-start.7
  311.1 47.9 %all-to-all-start.4 = ((f32[16,2,2,32,288]{4,3,2,1,0:T(8,128)}), f32[16,2,2,32,288]{4,3,2,1,0:T(8,128)}, u32[]{:S(2)}, u32[]{:S(2)}) async-start(f32[16,2,2,32,288]{4,3,2,1,0:T(8,128)} %broadcast_multiply_fusion.2), calls=%async_computation.4 | async-start | bytes 6291456 | tf_op jit(solution)/shard_map/all_to_all | solution.py:92
  359.1 48.0 %all-to-all-start.2 = ((f32[16,2,2,32,288]{4,3,2,1,0:T(8,128)}), f32[16,2,2,32,288]{4,3,2,1,0:T(8,128)S(1)}, u32[]{:S(2)}, u32[]{:S(2)}) async-start(f32[16,2,2,32,288]{4,3,2,1,0:T(8,128)} %broadcast_multiply_fusion.3), calls=%async_computation.2 | async-start | bytes 6291456 | tf_op jit(solution)/shard_map/all_to_all | solution.py:92
  407.1 1.7 copy-start.8
  408.8 67.4 %all-to-all-start.8 = ((f32[16,2,2,32,288]{4,3,2,1,0:T(8,128)}), f32[16,2,2,32,288]{4,3,2,1,0:T(8,128)}, u32[]{:S(2)}, u32[]{:S(2)}) async-start(f32[16,2,2,32,288]{4,3,2,1,0:T(8,128)} %broadcast_multiply_fusion), calls=%async_computation.8 | async-start | bytes 6291456 | tf_op jit(solution)/shard_map/all_to_all | solution.py:92
  422.0 4.3 copy-start.29
  426.3 16.9 %copy-start.6 = (f32[32,18432]{1,0:T(8,128)S(1)}, f32[32,18432]{1,0:T(8,128)}, u32[]{:S(2)}) copy-start(f32[32,18432]{1,0:T(8,128)} %reshape.744) | copy-start | bytes 7077892
  426.3 16.9 %copy-start.28 = (f32[32,128]{1,0:T(8,128)S(1)}, f32[32,128]{1,0:T(8,128)}, u32[]{:S(2)}) copy-start(f32[32,128]{1,0:T(8,128)} %constant.123.clone) | copy-start | bytes 49156
  443.2 15.2 %copy-start.27 = (f32[32,128]{1,0:T(8,128)S(1)}, f32[32,128]{1,0:T(8,128)}, u32[]{:S(2)}) copy-start(f32[32,128]{1,0:T(8,128)} %constant.124.clone) | copy-start | bytes 49156
  476.1 3.1 copy-start.26
  504.8 4.9 copy-start.1

commit v8 on v7

--- a/solution.py
+++ b/solution.py
@@ -38,7 +38,7 @@
     channel_count = chan_order.shape[0]
     width = channel_count // n_freq
     chunk = width // n_blk
-    halves = 4
+    halves = 2
     part_chunk = chunk // halves
     steps = n_blk // 2 + 1
     tile = input_order.shape[0]

time: 519 us -> 477 us (0.919)
  waiting for transfers between devices: 75.1 us -> 152 us
  local copies, waits for them, and re-layouts: 179 us -> 125 us
  matrix products: 134 us -> 102 us
  starting transfers between devices: 70.2 us -> 44.7 us
  other arithmetic: 50.6 us -> 43.8 us
    all_to_all x4 -> x2, waiting for transfers between devices: 61.4 us -> 132 us  [half_output(): returned = lax.all_to_all(banded, 'blk', 0, 0, tiled=True)]
    unnamed x90 -> x32, local copies, waits for them, and re-layouts: 44.4 us -> 1.83 us
    dot_general x4 -> x2, matrix products: 67.7 us -> 36.4 us  [half_output(): jnp.einsum('ax,ac->xc', returned, jnp.asarray(select), precision=lax.Prec...]
    all_to_all x4 -> x2, starting transfers between devices: 26 us -> 12.6 us  [half_output(): returned = lax.all_to_all(banded, 'blk', 0, 0, tiled=True)]
    all_to_all x4 -> x2, starting transfers between devices: 32.7 us -> 20.6 us  [half_band(): gathered = lax.all_to_all(spectra, ('blk', 'freq'), 0, 0, tiled=True)]
    gather x4 -> x2, local copies, waits for them, and re-layouts: 16.5 us -> 7.71 us  [half_band(): slotted = jnp.take(gathered, slot_order, axis=1)]
    all_to_all x4 -> x2, waiting for transfers between devices: 13.6 us -> 20.1 us  [half_band(): gathered = lax.all_to_all(spectra, ('blk', 'freq'), 0, 0, tiled=True)]
    reshape x0 -> x2, local copies, waits for them, and re-layouts: none -> 5.4 us  [half_band(): gathered.transpose(1, 0, 2, 3, 4)]
  transfers between devices with their start and end apart: 9 -> 5, of which waited for: 6 -> 3; matrix products, arithmetic and copies ran while one was open for 56% -> 40% of each run, Pallas kernels for 0% -> 0%
where the time goes in v8:
time: 477 us; the launch traced here: 469 us
  waiting for transfers between devices  152 us (32%)
  local copies, waits for them, and re-layouts  125 us (26%)
  matrix products  102 us (21%)
  starting transfers between devices  44.7 us (9%)
  other arithmetic  43.8 us (9%)
    all_to_all x2, waiting for transfers between devices, half_output(): returned = lax.all_to_all(banded, 'blk', 0, 0, tiled=True)  132 us
    dot_general x4, matrix products, half_spectra(): jnp.einsum('mc,nm->cn', part, filtered, precision=lax.Precision.HIGH)  56.4 us
    dot_general x8, local copies, waits for them, and re-layouts, half_spectra(): jnp.einsum('mc,nm->cn', part, filtered, precision=lax.Precision.HIGH)  42.4 us
    dot_general x2, matrix products, half_output(): jnp.einsum('ax,ac->xc', returned, jnp.asarray(select), precision=lax.Prec...  36.4 us
    all_to_all x2, starting transfers between devices, half_band(): gathered = lax.all_to_all(spectra, ('blk', 'freq'), 0, 0, tiled=True)  20.6 us
    all_to_all x2, waiting for transfers between devices, half_band(): gathered = lax.all_to_all(spectra, ('blk', 'freq'), 0, 0, tiled=True)  20.1 us
    add x1, other arithmetic, per_device(): filtered + filter_taps[tap_index] * frames[:, tap_index:tap_index + SPECTRA]  14 us
    reshape x2, local copies, waits for them, and re-layouts, half_output(): returned = returned.reshape(n_blk * part_chunk, 2 * tile * rows)  13.9 us
  transfers between devices with their start and end apart: 5, of which 3 were waited for; matrix products, arithmetic and copies ran while one was open for 40% of the time, Pallas kernels for 0%

profile of v8, /device:TPU:1, one launch (start us, length us, event | category | flops | bytes accessed | tf_op | source)
XLA Modules:
  0.0 468.9 jit_solution(11870807128215401412)
XLA Ops:
  1.3 11.5 %all-to-all-start.1 = ((f32[128,1,32]{2,1,0:T(1,128)}), f32[128,1,32]{2,1,0:T(1,128)S(1)}, u32[]{:S(2)}, u32[]{:S(2)}) async-start(f32[128,1,32]{2,1,0:T(1,128)} %broadcast_in_dim.13), calls=%async_computation.1 | async-start | bytes 131072 | tf_op jit(solution)/shard_map/all_to_all | solution.py:51
  17.3 7.9 %reshape.395 = f32[4,259,2048]{2,1,0:T(8,128)} reshape(bf16[4,530432]{1,0:T(4,128)(2,1)} %param.12) | data formatting | bytes 12730368 | tf_op jit(solution)/shard_map/reshape | solution.py:54
  25.5 4.6 subtract_multiply_fusion.1
  30.0 5.4 %copy.109 = f32[512,2048]{1,0:T(8,128)} copy(f32[512,2048]{0,1:T(8,128)} %bitcast.297) | data formatting | bytes 8388608 | tf_op jit(solution)/shard_map/mc,nm->cn/dot_general | solution.py:68
  35.4 5.3 %dot_general.53 = f32[128,4,2048]{2,1,0:T(4,128)} reshape(f32[512,2048]{1,0:T(8,128)} %copy.109) | data formatting | bytes 8388608 | tf_op jit(solution)/shard_map/mc,nm->cn/dot_general | solution.py:68
  40.7 5.4 %copy.107 = f32[512,2048]{1,0:T(8,128)} copy(f32[512,2048]{0,1:T(8,128)} %bitcast.295) | data formatting | bytes 8388608 | tf_op jit(solution)/shard_map/mc,nm->cn/dot_general | solution.py:68
  46.1 5.2 %dot_general.49 = f32[128,4,2048]{2,1,0:T(4,128)} reshape(f32[512,2048]{1,0:T(8,128)} %copy.107) | data formatting | bytes 8388608 | tf_op jit(solution)/shard_map/mc,nm->cn/dot_general | solution.py:68
  51.2 14.0 %fusion.1 = f32[4,256,2048,1]{2,1,0,3:T(8,128)S(1)} fusion(f32[4,259,2048]{2,1,0:T(8,128)} %reshape.395, f32[2048]{0:T(1024)S(1)} %bitcast.313, f32[2048]{0:T(1024)S(1)} %bitcast.314, f32[2048]{0:T(1024)S(1)} %bitcast.312, f32[2048]{0:T(1024)S(1)} %bitcast.311), kind=kLoop, calls=%fused_computation.8 | loop fusion | flops 14680064 | bytes 41975808 | tf_op jit(solution)/shard_map/add | solution.py:57
  65.3 9.2 %fusion.44 = bf16[128,4,1,4,256]{4,0,3,1,2:T(8,128)(2,1)S(1)} fusion(f32[4,256,2048,1]{2,1,0,3:T(8,128)S(1)} %fusion.1, f32[128,4,2048,1]{2,1,0,3:T(4,128)S(1)} %bitcast.306), kind=kOutput, calls=%fused_computation.52 | convolution fusion | flops 6442975232 | bytes 13631488 | tf_op jit(solution)/shard_map/mc,nm->cn/dot_general | solution.py:68
  74.5 19.8 %fusion.47 = bf16[128,4,1,4,256]{4,0,3,1,2:T(8,128)(2,1)S(1)} fusion(f32[4,256,2048,1]{2,1,0,3:T(8,128)S(1)} %fusion.1, f32[128,4,2048,1]{2,1,0,3:T(4,128)S(1)} %bitcast.307), kind=kOutput, calls=%fused_computation.53 | convolution fusion | flops 6442975232 | bytes 13631488 | tf_op jit(solution)/shard_map/mc,nm->cn/dot_general | solution.py:68
  94.6 2.9 copy.111
  97.5 9.8 %all-to-all-start = ((bf16[128,4,4,2,256]{4,2,1,3,0:T(4,128)(2,1)}), bf16[128,4,4,2,256]{4,2,1,3,0:T(4,128)(2,1)S(1)}, u32[]{:S(2)}, u32[]{:S(2)}) async-start(bf16[128,4,4,2,256]{4,2,1,3,0:T(4,128)(2,1)} %copy.111), calls=%async_computation | async-start | bytes 4194304 | tf_op jit(solution)/shard_map/all_to_all | solution.py:76
  107.4 2.3 gather_fusion.1
  110.5 4.5 subtract_multiply_fusion
  115.0 5.4 %copy.127 = f32[512,2048]{1,0:T(8,128)} copy(f32[512,2048]{0,1:T(8,128)} %bitcast.298) | data formatting | bytes 8388608 | tf_op jit(solution)/shard_map/mc,nm->cn/dot_general | solution.py:68
  120.4 5.3 %dot_general.59 = f32[128,4,2048]{2,1,0:T(4,128)} reshape(f32[512,2048]{1,0:T(8,128)} %copy.127) | data formatting | bytes 8388608 | tf_op jit(solution)/shard_map/mc,nm->cn/dot_general | solution.py:68
  125.7 5.4 %copy.129 = f32[512,2048]{1,0:T(8,128)} copy(f32[512,2048]{0,1:T(8,128)} %bitcast.296) | data formatting | bytes 8388608 | tf_op jit(solution)/shard_map/mc,nm->cn/dot_general | solution.py:68
  131.1 5.2 %dot_general.63 = f32[128,4,2048]{2,1,0:T(4,128)} reshape(f32[512,2048]{1,0:T(8,128)} %copy.129) | data formatting | bytes 8388608 | tf_op jit(solution)/shard_map/mc,nm->cn/dot_general | solution.py:68
  136.3 14.2 %fusion.41 = bf16[128,4,1,4,256]{4,0,3,1,2:T(8,128)(2,1)S(1)} fusion(f32[4,256,2048,1]{2,1,0,3:T(8,128)} %copy-done.2, f32[128,4,2048,1]{2,1,0,3:T(4,128)} %bitcast.308), kind=kOutput, calls=%fused_computation.51 | convolution fusion | flops 6442975232 | bytes 13631488 | tf_op jit(solution)/shard_map/mc,nm->cn/dot_general | solution.py:68
  150.4 13.2 %fusion.38 = bf16[128,4,1,4,256]{4,0,3,1,2:T(8,128)(2,1)S(1)} fusion(f32[4,256,2048,1]{2,1,0,3:T(8,128)} %copy-done.2, f32[128,4,2048,1]{2,1,0,3:T(4,128)S(1)} %bitcast.309), kind=kOutput, calls=%fused_computation.50 | convolution fusion | flops 6442975232 | bytes 13631488 | tf_op jit(solution)/shard_map/mc,nm->cn/dot_general | solution.py:68
  163.9 2.9 copy.131
  166.8 10.8 %all-to-all-start.3 = ((bf16[128,4,4,2,256]{4,2,1,3,0:T(4,128)(2,1)}), bf16[128,4,4,2,256]{4,2,1,3,0:T(4,128)(2,1)}, u32[]{:S(2)}, u32[]{:S(2)}) async-start(bf16[128,4,4,2,256]{4,2,1,3,0:T(4,128)(2,1)} %copy.131), calls=%async_computation.3 | async-start | bytes 4194304 | tf_op jit(solution)/shard_map/all_to_all | solution.py:76
  179.8 2.7 copy.113
  182.5 3.8 gather_fusion.2
  186.3 20.1 %all-to-all-done.3 = bf16[128,4,4,2,256]{4,2,1,3,0:T(4,128)(2,1)} async-done(((bf16[128,4,4,2,256]{4,2,1,3,0:T(4,128)(2,1)}), bf16[128,4,4,2,256]{4,2,1,3,0:T(4,128)(2,1)}, u32[]{:S(2)}, u32[]{:S(2)}) %all-to-all-start.3) | async-done | bytes 2097184 | tf_op jit(solution)/shard_map/all_to_all | solution.py:76
  206.4 3.7 copy.132
  210.1 2.7 copy.133
  212.8 4.0 gather_fusion.3
  216.8 5.2 %fusion.24 = (bf16[4,512,2,256]{3,1,0,2:T(8,128)(2,1)S(1)}, bf16[4,512,2,256]{3,1,0,2:T(8,128)(2,1)}) fusion(bf16[512,4,2,256]{3,1,2,0:T(4,128)(2,1)} %gather_fusion.3, pred[512]{0:T(512)(128)(4,1)S(1)} %compare_and_fusion, bf16[512,4,2,256]{3,1,2,0:T(4,128)(2,1)} %gather_fusion.2), kind=kLoop, calls=%fused_computation.43 | loop fusion | flops 2097152 | bytes 8389120 | tf_op jit(solution)/shard_map/jit(_take)/select_n | solution.py:78
  222.0 4.1 copy.115
  226.1 2.7 slice_bitcast_fusion.1
  228.8 2.4 copy.135
  231.2 4.2 copy.136
  235.4 4.1 copy.116
  239.6 4.9 %fusion.4 = f32[4,1024,512]{2,1,0:T(8,128)S(1)} fusion(bf16[4,512,512]{1,2,0:T(8,128)(2,1)} %bitcast.303, bf16[4,512,256]{2,1,0:T(8,128)(2,1)} %get-tuple-element.9, bf16[4,512,256]{2,1,0:T(8,128)(2,1)S(1)} %get-tuple-element.8, bf16[4,512,512]{2,1,0:T(8,128)(2,1)} %copy.116), kind=kOutput, calls=%fused_computation.14 | convolution fusion | flops 2160066560 | bytes 14680064 | tf_op jit(solution)/shard_map/kat,kpt->kap/dot_general | solution.py:82
  246.9 3.4 broadcast_multiply_fusion.1
  250.3 6.1 %all-to-all-start.2 = ((f32[16,4,2,32,288]{4,3,2,1,0:T(8,128)}), f32[16,4,2,32,288]{4,3,2,1,0:T(8,128)}, u32[]{:S(2)}, u32[]{:S(2)}) async-start(f32[16,4,2,32,288]{4,3,2,1,0:T(8,128)} %broadcast_multiply_fusion.1), calls=%async_computation.2 | async-start | bytes 12582912 | tf_op jit(solution)/shard_map/all_to_all | solution.py:92
  256.5 4.6 fusion.10
  263.5 3.3 broadcast_multiply_fusion
  266.8 73.6 %all-to-all-done.2 = f32[16,4,2,32,288]{4,3,2,1,0:T(8,128)} async-done(((f32[16,4,2,32,288]{4,3,2,1,0:T(8,128)}), f32[16,4,2,32,288]{4,3,2,1,0:T(8,128)}, u32[]{:S(2)}, u32[]{:S(2)}) %all-to-all-start.2) | async-done | bytes 4718624 | tf_op jit(solution)/shard_map/all_to_all | solution.py:92
  340.3 6.5 %all-to-all-start.4 = ((f32[16,4,2,32,288]{4,3,2,1,0:T(8,128)}), f32[16,4,2,32,288]{4,3,2,1,0:T(8,128)}, u32[]{:S(2)}, u32[]{:S(2)}) async-start(f32[16,4,2,32,288]{4,3,2,1,0:T(8,128)} %broadcast_multiply_fusion), calls=%async_computation.4 | async-start | bytes 12582912 | tf_op jit(solution)/shard_map/all_to_all | solution.py:92
  346.9 7.0 %reshape.388 = f32[64,18432]{1,0:T(8,128)} reshape(f32[16,4,2,32,288]{4,3,2,1,0:T(8,128)} %all-to-all-done.2) | data formatting | bytes 9437184 | tf_op jit(solution)/shard_map/reshape | solution.py:93
  353.9 18.3 %fusion.124 = f32[18432,128]{1,0:T(8,128)} fusion(f32[64,18432]{1,0:T(8,128)} %reshape.388, f32[64,128]{1,0:T(8,128)S(1)} %copy-done.7), kind=kOutput, calls=%fused_computation.188 | convolution fusion | flops 1811939328 | bytes 14188544 | tf_op jit(solution)/shard_map/ax,ac->xc/dot_general | solution.py:96
  372.2 58.8 %all-to-all-done.4 = f32[16,4,2,32,288]{4,3,2,1,0:T(8,128)} async-done(((f32[16,4,2,32,288]{4,3,2,1,0:T(8,128)}), f32[16,4,2,32,288]{4,3,2,1,0:T(8,128)}, u32[]{:S(2)}, u32[]{:S(2)}) %all-to-all-start.4) | async-done | bytes 4718624 | tf_op jit(solution)/shard_map/all_to_all | solution.py:92
  430.9 6.9 %reshape.392 = f32[64,18432]{1,0:T(8,128)} reshape(f32[16,4,2,32,288]{4,3,2,1,0:T(8,128)} %all-to-all-done.4) | data formatting | bytes 9437184 | tf_op jit(solution)/shard_map/reshape | solution.py:93
  437.9 18.1 %convolution_add_fusion = f32[18432,128]{1,0:T(8,128)S(1)} fusion(f32[18432,128]{1,0:T(8,128)} %fusion.124, f32[64,18432]{1,0:T(8,128)} %reshape.392, f32[64,128]{1,0:T(8,128)S(1)} %copy-done.6), kind=kOutput, calls=%fused_computation.4 | convolution fusion | flops 1814298624 | bytes 23625728 | tf_op jit(solution)/shard_map/ax,ac->xc/dot_general | solution.py:96
  456.0 7.6 %copy.148 = f32[2,32,9,32,128]{4,1,3,2,0:T(8,128)S(1)} copy(f32[2,32,9,32,128]{4,3,2,1,0:T(8,128)S(1)} %bitcast.294) | data formatting | bytes 18874368 | tf_op jit(solution)/shard_map/reshape | solution.py:103
  463.6 4.9 %reverse_bitcast_fusion = f32[2,9,32,32,128]{4,3,2,1,0:T(8,128)} fusion(f32[2,32,9,32,128]{4,1,3,2,0:T(8,128)S(1)} %copy.148), kind=kLoop, calls=%fused_computation.5 | loop fusion | bytes 18874368 | tf_op jit(solution)/shard_map/transpose | solution.py:104
  (72 shorter events, 14.4 us)
Async XLA Ops:
  0.0 13.5 %copy-start = (s32[1024]{0:T(1024)S(1)}, s32[1024]{0:T(1024)}, u32[]{:S(2)}) copy-start(s32[1024]{0:T(1024)} %param.15) | copy-start | bytes 12292
  1.3 96.2 %all-to-all-start.1 = ((f32[128,1,32]{2,1,0:T(1,128)}), f32[128,1,32]{2,1,0:T(1,128)S(1)}, u32[]{:S(2)}, u32[]{:S(2)}) async-start(f32[128,1,32]{2,1,0:T(1,128)} %broadcast_in_dim.13), calls=%async_computation.1 | async-start | bytes 131072 | tf_op jit(solution)/shard_map/all_to_all | solution.py:51
  51.2 14.0 %copy-start.3 = (f32[128,4,2048]{2,1,0:T(4,128)S(1)}, f32[128,4,2048]{2,1,0:T(4,128)}, u32[]{:S(2)}) copy-start(f32[128,4,2048]{2,1,0:T(4,128)} %dot_general.53) | copy-start | bytes 12582916
  65.3 9.2 %copy-start.2 = (f32[4,256,2048,1]{2,1,0,3:T(8,128)}, f32[4,256,2048,1]{2,1,0,3:T(8,128)S(1)}, u32[]{:S(2)}) copy-start(f32[4,256,2048,1]{2,1,0,3:T(8,128)S(1)} %fusion.1) | copy-start | bytes 25165828
  65.3 9.2 %copy-start.4 = (f32[128,4,2048]{2,1,0:T(4,128)S(1)}, f32[128,4,2048]{2,1,0:T(4,128)}, u32[]{:S(2)}) copy-start(f32[128,4,2048]{2,1,0:T(4,128)} %dot_general.49) | copy-start | bytes 12582916
  94.3 13.0 %copy-start.8 = (s32[512]{0:T(512)S(1)}, s32[512]{0:T(512)}, u32[]{:S(2)}) copy-start(s32[512]{0:T(512)} %constant.88) | copy-start | bytes 6148
  97.5 69.3 %all-to-all-start = ((bf16[128,4,4,2,256]{4,2,1,3,0:T(4,128)(2,1)}), bf16[128,4,4,2,256]{4,2,1,3,0:T(4,128)(2,1)S(1)}, u32[]{:S(2)}, u32[]{:S(2)}) async-start(bf16[128,4,4,2,256]{4,2,1,3,0:T(4,128)(2,1)} %copy.111), calls=%async_computation | async-start | bytes 4194304 | tf_op jit(solution)/shard_map/all_to_all | solution.py:76
  136.3 14.2 %copy-start.5 = (f32[128,4,2048]{2,1,0:T(4,128)S(1)}, f32[128,4,2048]{2,1,0:T(4,128)}, u32[]{:S(2)}) copy-start(f32[128,4,2048]{2,1,0:T(4,128)} %dot_general.63) | copy-start | bytes 12582916
  166.8 39.5 %all-to-all-start.3 = ((bf16[128,4,4,2,256]{4,2,1,3,0:T(4,128)(2,1)}), bf16[128,4,4,2,256]{4,2,1,3,0:T(4,128)(2,1)}, u32[]{:S(2)}, u32[]{:S(2)}) async-start(bf16[128,4,4,2,256]{4,2,1,3,0:T(4,128)(2,1)} %copy.131), calls=%async_computation.3 | async-start | bytes 4194304 | tf_op jit(solution)/shard_map/all_to_all | solution.py:76
  250.3 90.0 %all-to-all-start.2 = ((f32[16,4,2,32,288]{4,3,2,1,0:T(8,128)}), f32[16,4,2,32,288]{4,3,2,1,0:T(8,128)}, u32[]{:S(2)}, u32[]{:S(2)}) async-start(f32[16,4,2,32,288]{4,3,2,1,0:T(8,128)} %broadcast_multiply_fusion.1), calls=%async_computation.2 | async-start | bytes 12582912 | tf_op jit(solution)/shard_map/all_to_all | solution.py:92
  340.3 90.6 %all-to-all-start.4 = ((f32[16,4,2,32,288]{4,3,2,1,0:T(8,128)}), f32[16,4,2,32,288]{4,3,2,1,0:T(8,128)}, u32[]{:S(2)}, u32[]{:S(2)}) async-start(f32[16,4,2,32,288]{4,3,2,1,0:T(8,128)} %broadcast_multiply_fusion), calls=%async_computation.4 | async-start | bytes 12582912 | tf_op jit(solution)/shard_map/all_to_all | solution.py:92
  346.9 7.0 %copy-start.7 = (f32[64,128]{1,0:T(8,128)S(1)}, f32[64,128]{1,0:T(8,128)}, u32[]{:S(2)}) copy-start(f32[64,128]{1,0:T(8,128)} %constant.82.clone) | copy-start | bytes 98308
  372.2 65.7 %copy-start.6 = (f32[64,128]{1,0:T(8,128)S(1)}, f32[64,128]{1,0:T(8,128)}, u32[]{:S(2)}) copy-start(f32[64,128]{1,0:T(8,128)} %constant.83.clone) | copy-start | bytes 98308
  456.0 12.4 %copy-start.1 = (s32[1024]{0:T(1024)S(1)}, s32[1024]{0:T(1024)}, u32[]{:S(2)}) copy-start(s32[1024]{0:T(1024)} %param.15) | copy-start | bytes 12292

commit v9 on v8

--- a/solution.py
+++ b/solution.py
@@ -82,25 +82,36 @@
         gram = jnp.einsum("kat,kpt->kap", both, plain, preferred_element_type=jnp.float32)
         gram = gram.reshape(part_chunk, 2, n_blk, tile, total_inputs)
         doubled = jnp.concatenate([gram, gram], axis=-1)
-        blocks = []
+        near, far = [], []
         for own in range(n_blk):
-            start = (own - steps + 1) % n_blk * tile
-            blocks.append(doubled[:, :, own, :, start : start + rows])
-        return jnp.stack(blocks) * (1.0 / SPECTRA)
+            far_start = (own - steps + 1) % n_blk * tile
+            near_start = far_start + tile
+            near.append(doubled[:, :, own, :, near_start : near_start + rows - tile])
+            far.append(doubled[:, :, own, :, far_start : far_start + tile])
+        near = jnp.stack(near) * (1.0 / SPECTRA)
+        far = jnp.stack(far).reshape(n_blk, part_chunk * 2, tile * tile) * (1.0 / SPECTRA)
+        return near, far
 
-    def half_output(banded, half):
-        returned = lax.all_to_all(banded, "blk", 0, 0, tiled=True)
-        returned = returned.reshape(n_blk * part_chunk, 2 * tile * rows)
+    def half_output(band, half):
+        near, far = band
         source = np.arange(n_blk)[:, None] * chunk + half * part_chunk + np.arange(part_chunk)[None, :]
-        select = (source.reshape(-1, 1) == np.arange(n_blk * chunk)[None, :]).astype(np.float32)
-        return jnp.einsum("ax,ac->xc", returned, jnp.asarray(select), precision=lax.Precision.HIGHEST)
+        select = (source[:, :, None] == np.arange(n_blk * chunk)[None, None, :]).astype(np.float32)
+        select = jnp.asarray(select)
+        near = lax.all_to_all(near, "blk", 0, 0, tiled=True)
+        near = near.reshape(n_blk, part_chunk, -1)
+        near = jnp.einsum("bkx,bkc->xc", near, select, precision=lax.Precision.HIGHEST)
+        near = near.reshape(2, tile, steps - 1, tile, n_blk * chunk)[:, :, ::-1]
+        far = lax.all_to_all(far, "blk", 0, 0, tiled=True)
+        far = far.reshape(n_blk, part_chunk, 2, tile * tile)
+        far = jnp.einsum("bkrx,bkc->rxc", far, select, precision=lax.Precision.HIGHEST)
+        far = far.reshape(2, tile, 1, tile, n_blk * chunk)
+        return jnp.concatenate([near, far], axis=2)
 
     spectra_parts = [half_spectra(half) for half in range(halves)]
     band_parts = [half_band(spectra) for spectra in spectra_parts]
     turned = half_output(band_parts[0], 0)
     for half in range(1, halves):
         turned = turned + half_output(band_parts[half], half)
-    turned = turned.reshape(2, tile, steps, tile, n_blk * chunk)[:, :, ::-1]
     return turned.transpose(0, 2, 3, 1, 4)
 
 

time: 477 us -> 593 us (1.24)
  local copies, waits for them, and re-layouts: 125 us -> 208 us
  waiting for transfers between devices: 152 us -> 102 us
  matrix products: 102 us -> 151 us
  other arithmetic: 43.8 us -> 64.2 us
  starting transfers between devices: 44.7 us -> 57.1 us
    all_to_all x2 -> x4, waiting for transfers between devices: 132 us -> 82 us  [the longest x2 77.7 us: half_output(): near = lax.all_to_all(near, 'blk', 0, 0, tiled=True)]
    dot_general x2 -> x4, matrix products: 36.4 us -> 86.8 us  [the longest x2 78.4 us: half_output(): jnp.einsum('bkx,bkc->xc', near, select, precision=lax.Precision.HIGHEST)]
    dot_general x0 -> x2, local copies, waits for them, and re-layouts: none -> 21.5 us  [half_output(): jnp.einsum('bkx,bkc->xc', near, select, precision=lax.Precision.HIGHEST)]
    unnamed x32 -> x88, local copies, waits for them, and re-layouts: 1.83 us -> 19.3 us
    another operation x2 -> x38, local copies, waits for them, and re-layouts: 0.33 us -> 16.7 us  [the longest x34 12.3 us: half_band(): jnp.stack(far).reshape(n_blk, part_chunk * 2, tile * tile) * (1.0 / SPECTRA)]
    rev x0 -> x2, local copies, waits for them, and re-layouts: none -> 15.6 us  [half_output(): near = near.reshape(2, tile, steps - 1, tile, n_blk * chunk)[:, :, ::-1]]
    all_to_all x2 -> x4, starting transfers between devices: 12.6 us -> 25.1 us  [the longest x2 12.7 us: half_output(): near = lax.all_to_all(near, 'blk', 0, 0, tiled=True)]
    unnamed x16, other arithmetic: 2.59 us -> 11.6 us
  transfers between devices with their start and end apart: 5 -> 7, of which waited for: 3 -> 4; matrix products, arithmetic and copies ran while one was open for 40% -> 36% of each run, Pallas kernels for 0% -> 0%
where the time goes in v9:
time: 593 us; the launch traced here: 584 us
  local copies, waits for them, and re-layouts  208 us (35%)
  matrix products  151 us (25%)
  waiting for transfers between devices  102 us (17%)
  other arithmetic  64.2 us (11%)
  starting transfers between devices  57.1 us (10%)
    dot_general x2, matrix products, half_output(): jnp.einsum('bkx,bkc->xc', near, select, precision=lax.Precision.HIGHEST)  78.4 us
    all_to_all x2, waiting for transfers between devices, half_output(): near = lax.all_to_all(near, 'blk', 0, 0, tiled=True)  77.7 us
    dot_general x4, matrix products, half_spectra(): jnp.einsum('mc,nm->cn', part, filtered, precision=lax.Precision.HIGH)  56.4 us
    dot_general x8, local copies, waits for them, and re-layouts, half_spectra(): jnp.einsum('mc,nm->cn', part, filtered, precision=lax.Precision.HIGH)  42.4 us
    reshape x4, local copies, waits for them, and re-layouts, half_output(): near = near.reshape(n_blk, part_chunk, -1)  25.1 us
    dot_general x2, local copies, waits for them, and re-layouts, half_output(): jnp.einsum('bkx,bkc->xc', near, select, precision=lax.Precision.HIGHEST)  21.5 us
    all_to_all x2, starting transfers between devices, half_band(): gathered = lax.all_to_all(spectra, ('blk', 'freq'), 0, 0, tiled=True)  20.6 us
    all_to_all x2, waiting for transfers between devices, half_band(): gathered = lax.all_to_all(spectra, ('blk', 'freq'), 0, 0, tiled=True)  20 us
  transfers between devices with their start and end apart: 7, of which 4 were waited for; matrix products, arithmetic and copies ran while one was open for 36% of the time, Pallas kernels for 0%

profile of v9, /device:TPU:1, one launch (start us, length us, event | category | flops | bytes accessed | tf_op | source)
XLA Modules:
  0.0 583.7 jit_solution(18198992559782146160)
XLA Ops:
  1.3 11.5 %all-to-all-start.1 = ((f32[128,1,32]{2,1,0:T(1,128)}), f32[128,1,32]{2,1,0:T(1,128)S(1)}, u32[]{:S(2)}, u32[]{:S(2)}) async-start(f32[128,1,32]{2,1,0:T(1,128)} %broadcast_in_dim.13), calls=%async_computation.1 | async-start | bytes 131072 | tf_op jit(solution)/shard_map/all_to_all | solution.py:51
  17.6 4.7 subtract_multiply_fusion.1
  22.3 5.4 copy.127
  27.7 5.2 dot_general.71
  32.8 5.3 copy.129
  38.2 5.2 dot_general.75
  43.4 7.9 %reshape.485 = f32[4,259,2048]{2,1,0:T(8,128)} reshape(bf16[4,530432]{1,0:T(4,128)(2,1)} %param.12) | data formatting | bytes 12730368 | tf_op jit(solution)/shard_map/reshape | solution.py:54
  51.3 14.0 %fusion.6 = f32[4,256,2048,1]{2,1,0,3:T(8,128)S(1)} fusion(f32[4,259,2048]{2,1,0:T(8,128)} %reshape.485, f32[2048]{0:T(1024)S(1)} %bitcast.435, f32[2048]{0:T(1024)S(1)} %bitcast.436, f32[2048]{0:T(1024)S(1)} %bitcast.434, f32[2048]{0:T(1024)S(1)} %bitcast.433), kind=kLoop, calls=%fused_computation.12 | loop fusion | flops 14680064 | bytes 41975808 | tf_op jit(solution)/shard_map/add | solution.py:57
  65.4 9.2 %fusion.59 = bf16[128,4,1,4,256]{4,0,3,1,2:T(8,128)(2,1)S(1)} fusion(f32[4,256,2048,1]{2,1,0,3:T(8,128)S(1)} %fusion.6, f32[128,4,2048,1]{2,1,0,3:T(4,128)S(1)} %bitcast.427), kind=kOutput, calls=%fused_computation.64 | convolution fusion | flops 6442975232 | bytes 13631488 | tf_op jit(solution)/shard_map/mc,nm->cn/dot_general | solution.py:68
  74.6 19.8 %fusion.62 = bf16[128,4,1,4,256]{4,0,3,1,2:T(8,128)(2,1)S(1)} fusion(f32[4,256,2048,1]{2,1,0,3:T(8,128)S(1)} %fusion.6, f32[128,4,2048,1]{2,1,0,3:T(4,128)S(1)} %bitcast.426), kind=kOutput, calls=%fused_computation.65 | convolution fusion | flops 6442975232 | bytes 13631488 | tf_op jit(solution)/shard_map/mc,nm->cn/dot_general | solution.py:68
  97.6 9.8 %all-to-all-start = ((bf16[128,4,4,2,256]{4,2,1,3,0:T(4,128)(2,1)}), bf16[128,4,4,2,256]{4,2,1,3,0:T(4,128)(2,1)S(1)}, u32[]{:S(2)}, u32[]{:S(2)}) async-start(bf16[128,4,4,2,256]{4,2,1,3,0:T(4,128)(2,1)} %copy.131), calls=%async_computation | async-start | bytes 4194304 | tf_op jit(solution)/shard_map/all_to_all | solution.py:76
  110.6 4.6 subtract_multiply_fusion
  115.2 5.4 copy.153
  120.6 5.2 dot_general.86
  125.7 5.4 copy.155
  131.2 5.2 dot_general.90
  136.4 14.2 %fusion.53 = bf16[128,4,1,4,256]{4,0,3,1,2:T(8,128)(2,1)S(1)} fusion(f32[4,256,2048,1]{2,1,0,3:T(8,128)} %copy-done.7, f32[128,4,2048,1]{2,1,0,3:T(4,128)} %bitcast.429), kind=kOutput, calls=%fused_computation.62 | convolution fusion | flops 6442975232 | bytes 13631488 | tf_op jit(solution)/shard_map/mc,nm->cn/dot_general | solution.py:68
  150.6 13.2 %fusion.56 = bf16[128,4,1,4,256]{4,0,3,1,2:T(8,128)(2,1)S(1)} fusion(f32[4,256,2048,1]{2,1,0,3:T(8,128)} %copy-done.7, f32[128,4,2048,1]{2,1,0,3:T(4,128)S(1)} %bitcast.428), kind=kOutput, calls=%fused_computation.63 | convolution fusion | flops 6442975232 | bytes 13631488 | tf_op jit(solution)/shard_map/mc,nm->cn/dot_general | solution.py:68
  167.0 10.8 %all-to-all-start.4 = ((bf16[128,4,4,2,256]{4,2,1,3,0:T(4,128)(2,1)}), bf16[128,4,4,2,256]{4,2,1,3,0:T(4,128)(2,1)}, u32[]{:S(2)}, u32[]{:S(2)}) async-start(bf16[128,4,4,2,256]{4,2,1,3,0:T(4,128)(2,1)} %copy.157), calls=%async_computation.4 | async-start | bytes 4194304 | tf_op jit(solution)/shard_map/all_to_all | solution.py:76
  186.5 20.0 %all-to-all-done.4 = bf16[128,4,4,2,256]{4,2,1,3,0:T(4,128)(2,1)} async-done(((bf16[128,4,4,2,256]{4,2,1,3,0:T(4,128)(2,1)}), bf16[128,4,4,2,256]{4,2,1,3,0:T(4,128)(2,1)}, u32[]{:S(2)}, u32[]{:S(2)}) %all-to-all-start.4) | async-done | bytes 2097184 | tf_op jit(solution)/shard_map/all_to_all | solution.py:76
  213.0 4.0 gather_fusion.3
  216.9 5.2 fusion.39
  222.1 4.2 copy.161
  232.8 4.3 copy.136
  237.1 3.9 fusion.9
  263.5 5.1 all-to-all-start.3
  268.6 4.1 fusion.15
  293.6 7.3 %all-to-all-start.6 = ((f32[16,8,1024]{2,1,0:T(8,128)}), f32[16,8,1024]{2,1,0:T(8,128)S(1)}, u32[]{:S(2)}, u32[]{:S(2)}) async-start(f32[16,8,1024]{2,1,0:T(8,128)} %broadcast_multiply_fusion.2), calls=%async_computation.6 | async-start | bytes 1048576 | tf_op jit(solution)/shard_map/all_to_all | solution.py:104
  302.6 5.0 broadcast_multiply_fusion.1
  307.6 4.3 all-to-all-done.6
  312.7 6.1 %all-to-all-start.2 = ((f32[16,4,2,32,256]{4,3,2,1,0:T(8,128)}), f32[16,4,2,32,256]{4,3,2,1,0:T(8,128)}, u32[]{:S(2)}, u32[]{:S(2)}) async-start(f32[16,4,2,32,256]{4,3,2,1,0:T(8,128)} %broadcast_multiply_fusion.1), calls=%async_computation.2 | async-start | bytes 8388608 | tf_op jit(solution)/shard_map/all_to_all | solution.py:100
  326.8 47.5 %all-to-all-done.2 = f32[16,4,2,32,256]{4,3,2,1,0:T(8,128)} async-done(((f32[16,4,2,32,256]{4,3,2,1,0:T(8,128)}), f32[16,4,2,32,256]{4,3,2,1,0:T(8,128)}, u32[]{:S(2)}, u32[]{:S(2)}) %all-to-all-start.2) | async-done | bytes 4194336 | tf_op jit(solution)/shard_map/all_to_all | solution.py:100
  374.3 6.6 %all-to-all-start.5 = ((f32[16,4,2,32,256]{4,3,2,1,0:T(8,128)}), f32[16,4,2,32,256]{4,3,2,1,0:T(8,128)}, u32[]{:S(2)}, u32[]{:S(2)}) async-start(f32[16,4,2,32,256]{4,3,2,1,0:T(8,128)} %broadcast_multiply_fusion), calls=%async_computation.5 | async-start | bytes 8388608 | tf_op jit(solution)/shard_map/all_to_all | solution.py:100
  385.3 4.2 fusion.65
  389.5 4.2 fusion.68
  393.7 6.1 %reshape.537 = f32[16,4,16384]{2,1,0:T(4,128)} reshape(f32[16,4,2,32,256]{4,3,2,1,0:T(8,128)} %all-to-all-done.2) | data formatting | bytes 8388608 | tf_op jit(solution)/shard_map/reshape | solution.py:101
  399.8 6.7 %copy.291 = f32[16,4,16384]{2,0,1:T(8,128)} copy(f32[16,4,16384]{2,1,0:T(4,128)} %reshape.537) | data formatting | bytes 8388608 | tf_op jit(solution)/shard_map/reshape | solution.py:101
  406.5 30.3 %all-to-all-done.5 = f32[16,4,2,32,256]{4,3,2,1,0:T(8,128)} async-done(((f32[16,4,2,32,256]{4,3,2,1,0:T(8,128)}), f32[16,4,2,32,256]{4,3,2,1,0:T(8,128)}, u32[]{:S(2)}, u32[]{:S(2)}) %all-to-all-start.5) | async-done | bytes 4194336 | tf_op jit(solution)/shard_map/all_to_all | solution.py:100
  436.8 5.8 reshape.539
  442.5 6.6 %copy.290 = f32[16,4,16384]{2,0,1:T(8,128)} copy(f32[16,4,16384]{2,1,0:T(4,128)} %reshape.539) | data formatting | bytes 8388608 | tf_op jit(solution)/shard_map/reshape | solution.py:101
  449.1 10.7 %dot_general.95 = f32[2,32,8,32,16,4]{3,2,1,0,4,5:T(8,128)} reshape(f32[16384,16,4]{0,1,2:T(8,128)} %bitcast.414) | data formatting | bytes 8388608 | tf_op jit(solution)/shard_map/bkx,bkc->xc/dot_general | solution.py:102
  459.8 39.2 %fusion.32 = f32[2,32,8,32,128]{4,3,2,1,0:T(8,128)} fusion(f32[16,4,128,1,1,1]{2,0,1,5,4,3:T(8,128)S(1)} %copy-done.13, f32[2,32,8,32,16,4]{3,2,1,0,4,5:T(8,128)} %dot_general.95), kind=kOutput, calls=%fused_computation.45 | convolution fusion | flops 1610612736 | bytes 12615680 | tf_op jit(solution)/shard_map/bkx,bkc->xc/dot_general | solution.py:102
  499.0 7.8 %rev.7 = f32[2,32,8,32,128]{4,3,2,1,0:T(8,128)} reverse(f32[2,32,8,32,128]{4,3,2,1,0:T(8,128)} %fusion.32), dimensions={2} | reverse | bytes 16777216 | tf_op jit(solution)/shard_map/rev | solution.py:103
  506.8 10.7 %dot_general.80 = f32[2,32,8,32,16,4]{3,2,1,0,4,5:T(8,128)} reshape(f32[16384,16,4]{0,1,2:T(8,128)} %bitcast.413) | data formatting | bytes 8388608 | tf_op jit(solution)/shard_map/bkx,bkc->xc/dot_general | solution.py:102
  517.6 39.2 %fusion.29 = f32[2,32,8,32,128]{4,3,2,1,0:T(8,128)} fusion(f32[16,4,128,1,1,1]{2,0,1,5,4,3:T(8,128)S(1)} %copy-done.12, f32[2,32,8,32,16,4]{3,2,1,0,4,5:T(8,128)} %dot_general.80), kind=kOutput, calls=%fused_computation.44 | convolution fusion | flops 1610612736 | bytes 12615680 | tf_op jit(solution)/shard_map/bkx,bkc->xc/dot_general | solution.py:102
  556.8 7.8 %rev.6 = f32[2,32,8,32,128]{4,3,2,1,0:T(8,128)} reverse(f32[2,32,8,32,128]{4,3,2,1,0:T(8,128)} %fusion.29), dimensions={2} | reverse | bytes 16777216 | tf_op jit(solution)/shard_map/rev | solution.py:103
  564.6 7.3 %fusion.4 = f32[2,9,32,32,128]{4,2,1,3,0:T(8,128)S(1)} fusion(f32[2,32,1,32,128]{4,3,2,1,0:T(8,128)S(1)} %fusion.65, f32[2,32,8,32,128]{4,3,2,1,0:T(8,128)} %rev.6, f32[2,32,1,32,128]{4,3,2,1,0:T(8,128)S(1)} %fusion.68, f32[2,32,8,32,128]{4,3,2,1,0:T(8,128)} %rev.7), kind=kLoop, calls=%fused_computation.9 | loop fusion | flops 7077888 | bytes 28311552 | tf_op jit(solution)/shard_map/transpose | solution.py:115
  571.9 11.3 %copy.180 = f32[2,9,32,32,128]{4,3,2,1,0:T(8,128)} copy(f32[2,9,32,32,128]{4,2,1,3,0:T(8,128)S(1)} %fusion.4) | data formatting | bytes 18874368 | tf_op jit(solution)/shard_map/transpose | solution.py:115
  (182 shorter events, 95.1 us)
Async XLA Ops:
  0.0 13.5 %copy-start = (s32[1024]{0:T(1024)S(1)}, s32[1024]{0:T(1024)}, u32[]{:S(2)}) copy-start(s32[1024]{0:T(1024)} %param.15) | copy-start | bytes 12292
  1.3 96.2 %all-to-all-start.1 = ((f32[128,1,32]{2,1,0:T(1,128)}), f32[128,1,32]{2,1,0:T(1,128)S(1)}, u32[]{:S(2)}, u32[]{:S(2)}) async-start(f32[128,1,32]{2,1,0:T(1,128)} %broadcast_in_dim.13), calls=%async_computation.1 | async-start | bytes 131072 | tf_op jit(solution)/shard_map/all_to_all | solution.py:51
  51.3 14.1 %copy-start.9 = (f32[128,4,2048]{2,1,0:T(4,128)S(1)}, f32[128,4,2048]{2,1,0:T(4,128)}, u32[]{:S(2)}) copy-start(f32[128,4,2048]{2,1,0:T(4,128)} %dot_general.75) | copy-start | bytes 12582916
  65.3 9.2 %copy-start.7 = (f32[4,256,2048,1]{2,1,0,3:T(8,128)}, f32[4,256,2048,1]{2,1,0,3:T(8,128)S(1)}, u32[]{:S(2)}) copy-start(f32[4,256,2048,1]{2,1,0,3:T(8,128)S(1)} %fusion.6) | copy-start | bytes 25165828
  65.4 9.2 %copy-start.8 = (f32[128,4,2048]{2,1,0:T(4,128)S(1)}, f32[128,4,2048]{2,1,0:T(4,128)}, u32[]{:S(2)}) copy-start(f32[128,4,2048]{2,1,0:T(4,128)} %dot_general.71) | copy-start | bytes 12582916
  94.6 12.8 %copy-start.16 = (s32[512]{0:T(512)S(1)}, s32[512]{0:T(512)}, u32[]{:S(2)}) copy-start(s32[512]{0:T(512)} %constant.89) | copy-start | bytes 6148
  97.6 69.4 %all-to-all-start = ((bf16[128,4,4,2,256]{4,2,1,3,0:T(4,128)(2,1)}), bf16[128,4,4,2,256]{4,2,1,3,0:T(4,128)(2,1)S(1)}, u32[]{:S(2)}, u32[]{:S(2)}) async-start(bf16[128,4,4,2,256]{4,2,1,3,0:T(4,128)(2,1)} %copy.131), calls=%async_computation | async-start | bytes 4194304 | tf_op jit(solution)/shard_map/all_to_all | solution.py:76
  136.4 14.2 %copy-start.10 = (f32[128,4,2048]{2,1,0:T(4,128)S(1)}, f32[128,4,2048]{2,1,0:T(4,128)}, u32[]{:S(2)}) copy-start(f32[128,4,2048]{2,1,0:T(4,128)} %dot_general.86) | copy-start | bytes 12582916
  167.0 39.5 %all-to-all-start.4 = ((bf16[128,4,4,2,256]{4,2,1,3,0:T(4,128)(2,1)}), bf16[128,4,4,2,256]{4,2,1,3,0:T(4,128)(2,1)}, u32[]{:S(2)}, u32[]{:S(2)}) async-start(bf16[128,4,4,2,256]{4,2,1,3,0:T(4,128)(2,1)} %copy.157), calls=%async_computation.4 | async-start | bytes 4194304 | tf_op jit(solution)/shard_map/all_to_all | solution.py:76
  232.8 4.3 copy-start.6
  241.0 3.8 copy-start.2
  242.7 3.1 copy-start.5
  263.5 30.0 %all-to-all-start.3 = ((f32[16,8,1024]{2,1,0:T(8,128)}), f32[16,8,1024]{2,1,0:T(8,128)S(1)}, u32[]{:S(2)}, u32[]{:S(2)}) async-start(f32[16,8,1024]{2,1,0:T(8,128)} %broadcast_multiply_fusion.3), calls=%async_computation.3 | async-start | bytes 1048576 | tf_op jit(solution)/shard_map/all_to_all | solution.py:104
  272.7 3.3 copy-start.3
  278.2 4.1 slice-start
  280.2 2.5 slice-start.1
  293.6 18.3 %all-to-all-start.6 = ((f32[16,8,1024]{2,1,0:T(8,128)}), f32[16,8,1024]{2,1,0:T(8,128)S(1)}, u32[]{:S(2)}, u32[]{:S(2)}) async-start(f32[16,8,1024]{2,1,0:T(8,128)} %broadcast_multiply_fusion.2), calls=%async_computation.6 | async-start | bytes 1048576 | tf_op jit(solution)/shard_map/all_to_all | solution.py:104
  311.9 0.8 copy-start.11
  312.7 61.6 %all-to-all-start.2 = ((f32[16,4,2,32,256]{4,3,2,1,0:T(8,128)}), f32[16,4,2,32,256]{4,3,2,1,0:T(8,128)}, u32[]{:S(2)}, u32[]{:S(2)}) async-start(f32[16,4,2,32,256]{4,3,2,1,0:T(8,128)} %broadcast_multiply_fusion.1), calls=%async_computation.2 | async-start | bytes 8388608 | tf_op jit(solution)/shard_map/all_to_all | solution.py:100
  318.8 2.7 slice-start.2
  320.1 2.7 slice-start.3
  374.3 62.5 %all-to-all-start.5 = ((f32[16,4,2,32,256]{4,3,2,1,0:T(8,128)}), f32[16,4,2,32,256]{4,3,2,1,0:T(8,128)}, u32[]{:S(2)}, u32[]{:S(2)}) async-start(f32[16,4,2,32,256]{4,3,2,1,0:T(8,128)} %broadcast_multiply_fusion), calls=%async_computation.5 | async-start | bytes 8388608 | tf_op jit(solution)/shard_map/all_to_all | solution.py:100
  380.9 4.4 copy-start.15
  381.2 8.2 %copy-start.14 = (f32[16,4,128,1,1]{2,0,1,4,3:T(8,128)S(1)}, f32[16,4,128,1,1]{2,0,1,4,3:T(8,128)}, u32[]{:S(2)}) copy-start(f32[16,4,128,1,1]{2,0,1,4,3:T(8,128)} %constant.93) | copy-start | bytes 98308
  385.3 4.2 copy-start.4
  449.1 10.7 %copy-start.13 = (f32[16,4,128,1,1,1]{2,0,1,5,4,3:T(8,128)S(1)}, f32[16,4,128,1,1,1]{2,0,1,5,4,3:T(8,128)}, u32[]{:S(2)}) copy-start(f32[16,4,128,1,1,1]{2,0,1,5,4,3:T(8,128)} %constant.92) | copy-start | bytes 98308
  506.8 10.7 %copy-start.12 = (f32[16,4,128,1,1,1]{2,0,1,5,4,3:T(8,128)S(1)}, f32[16,4,128,1,1,1]{2,0,1,5,4,3:T(8,128)}, u32[]{:S(2)}) copy-start(f32[16,4,128,1,1,1]{2,0,1,5,4,3:T(8,128)} %constant.90) | copy-start | bytes 98308
  571.9 11.3 %copy-start.1 = (s32[1024]{0:T(1024)S(1)}, s32[1024]{0:T(1024)}, u32[]{:S(2)}) copy-start(s32[1024]{0:T(1024)} %param.15) | copy-start | bytes 12292

commit v10 on v9

--- a/solution.py
+++ b/solution.py
@@ -46,6 +46,9 @@
     total_inputs = n_dev * local_inputs
     frame = 2 * channel_count
     rows = steps * tile
+    reverse_tiles = (
+        (n_blk - 1 - np.arange(n_blk))[:, None] * tile + np.arange(tile)[None, :]
+    ).reshape(-1)
 
     spread = jnp.broadcast_to(input_order.astype(jnp.float32)[None], (n_dev, tile))
     slot_order = lax.all_to_all(spread, ("blk", "freq"), 0, 0, tiled=True)
@@ -79,14 +82,16 @@
         plain = slotted.reshape(part_chunk, total_inputs, 2 * SPECTRA)
         rotated = jnp.concatenate([slotted[:, :, 1], -slotted[:, :, 0]], axis=2)
         both = jnp.concatenate([plain, rotated], axis=1)
-        gram = jnp.einsum("kat,kpt->kap", both, plain, preferred_element_type=jnp.float32)
+        partners = jnp.take(gathered, slot_order[reverse_tiles], axis=1)
+        partners = partners.reshape(part_chunk, total_inputs, 2 * SPECTRA)
+        gram = jnp.einsum("kat,kpt->kap", both, partners, preferred_element_type=jnp.float32)
         gram = gram.reshape(part_chunk, 2, n_blk, tile, total_inputs)
         doubled = jnp.concatenate([gram, gram], axis=-1)
         near, far = [], []
         for own in range(n_blk):
-            far_start = (own - steps + 1) % n_blk * tile
-            near_start = far_start + tile
-            near.append(doubled[:, :, own, :, near_start : near_start + rows - tile])
+            near_start = (n_blk - 1 - own) * tile
+            far_start = near_start + rows - tile
+            near.append(doubled[:, :, own, :, near_start:far_start])
             far.append(doubled[:, :, own, :, far_start : far_start + tile])
         near = jnp.stack(near) * (1.0 / SPECTRA)
         far = jnp.stack(far).reshape(n_blk, part_chunk * 2, tile * tile) * (1.0 / SPECTRA)
@@ -100,19 +105,20 @@
         near = lax.all_to_all(near, "blk", 0, 0, tiled=True)
         near = near.reshape(n_blk, part_chunk, -1)
         near = jnp.einsum("bkx,bkc->xc", near, select, precision=lax.Precision.HIGHEST)
-        near = near.reshape(2, tile, steps - 1, tile, n_blk * chunk)[:, :, ::-1]
+        near = near.reshape(2, tile, steps - 1, tile, n_blk * chunk)
         far = lax.all_to_all(far, "blk", 0, 0, tiled=True)
         far = far.reshape(n_blk, part_chunk, 2, tile * tile)
         far = jnp.einsum("bkrx,bkc->rxc", far, select, precision=lax.Precision.HIGHEST)
-        far = far.reshape(2, tile, 1, tile, n_blk * chunk)
-        return jnp.concatenate([near, far], axis=2)
+        return near, far.reshape(2, tile, 1, tile, n_blk * chunk)
 
     spectra_parts = [half_spectra(half) for half in range(halves)]
     band_parts = [half_band(spectra) for spectra in spectra_parts]
-    turned = half_output(band_parts[0], 0)
+    near, far = half_output(band_parts[0], 0)
     for half in range(1, halves):
-        turned = turned + half_output(band_parts[half], half)
-    return turned.transpose(0, 2, 3, 1, 4)
+        more_near, more_far = half_output(band_parts[half], half)
+        near = near + more_near
+        far = far + more_far
+    return jnp.concatenate([near, far], axis=2).transpose(0, 2, 3, 1, 4)
 
 
 def solution(mesh):

time: 593 us -> 610 us (1.029)
  local copies, waits for them, and re-layouts: 208 us -> 219 us
  matrix products: 151 us -> 142 us
    rev x2 -> x0, local copies, waits for them, and re-layouts: 15.6 us -> none  [half_output(): near = near.reshape(2, tile, steps - 1, tile, n_blk * chunk)[:, :, ::-1]]
    gather x0 -> x3, local copies, waits for them, and re-layouts: none -> 12.9 us  [half_band(): partners = jnp.take(gathered, slot_order[reverse_tiles], axis=1)]
    select_n x0 -> x2, local copies, waits for them, and re-layouts: none -> 8.88 us  [half_band(): partners = jnp.take(gathered, slot_order[reverse_tiles], axis=1)]
    dot_general x2, matrix products: 78.4 us -> 69.8 us  [half_output(): jnp.einsum('bkx,bkc->xc', near, select, precision=lax.Precision.HIGHEST)]
    unnamed x88 -> x96, local copies, waits for them, and re-layouts: 19.3 us -> 19.1 us
  transfers between devices with their start and end apart: 7 -> 7, of which waited for: 4 -> 4; matrix products, arithmetic and copies ran while one was open for 36% -> 24% of each run, Pallas kernels for 0% -> 0%
where the time goes in v10:
time: 610 us; the launch traced here: 599 us
  local copies, waits for them, and re-layouts  219 us (36%)
  matrix products  142 us (23%)
  waiting for transfers between devices  106 us (17%)
  other arithmetic  68.7 us (11%)
  starting transfers between devices  63 us (10%)
    all_to_all x2, waiting for transfers between devices, half_output(): near = lax.all_to_all(near, 'blk', 0, 0, tiled=True)  77.9 us
    dot_general x2, matrix products, half_output(): jnp.einsum('bkx,bkc->xc', near, select, precision=lax.Precision.HIGHEST)  69.8 us
    dot_general x4, matrix products, half_spectra(): jnp.einsum('mc,nm->cn', part, filtered, precision=lax.Precision.HIGH)  54.6 us
    dot_general x8, local copies, waits for them, and re-layouts, half_spectra(): jnp.einsum('mc,nm->cn', part, filtered, precision=lax.Precision.HIGH)  42.3 us
    all_to_all x2, starting transfers between devices, half_band(): gathered = lax.all_to_all(spectra, ('blk', 'freq'), 0, 0, tiled=True)  26.3 us
    reshape x4, local copies, waits for them, and re-layouts, half_output(): near = near.reshape(n_blk, part_chunk, -1)  25 us
    all_to_all x2, waiting for transfers between devices, half_band(): gathered = lax.all_to_all(spectra, ('blk', 'freq'), 0, 0, tiled=True)  23.6 us
    dot_general x2, local copies, waits for them, and re-layouts, half_output(): jnp.einsum('bkx,bkc->xc', near, select, precision=lax.Precision.HIGHEST)  21.5 us
  transfers between devices with their start and end apart: 7, of which 4 were waited for; matrix products, arithmetic and copies ran while one was open for 24% of the time, Pallas kernels for 0%

profile of v10, /device:TPU:1, one launch (start us, length us, event | category | flops | bytes accessed | tf_op | source)
XLA Modules:
  0.0 599.2 jit_solution(560702139257876479)
XLA Ops:
  1.3 11.5 %all-to-all-start.1 = ((f32[128,1,32]{2,1,0:T(1,128)}), f32[128,1,32]{2,1,0:T(1,128)S(1)}, u32[]{:S(2)}, u32[]{:S(2)}) async-start(f32[128,1,32]{2,1,0:T(1,128)} %broadcast_in_dim.17), calls=%async_computation.1 | async-start | bytes 131072 | tf_op jit(solution)/shard_map/all_to_all | solution.py:54
  13.8 7.9 %reshape.484 = f32[4,259,2048]{2,1,0:T(8,128)} reshape(bf16[4,530432]{1,0:T(4,128)(2,1)} %param.15) | data formatting | bytes 12730368 | tf_op jit(solution)/shard_map/reshape | solution.py:57
  21.6 17.1 %fusion.5 = f32[4,256,2048,1]{2,1,0,3:T(8,128)} fusion(f32[4,259,2048]{2,1,0:T(8,128)} %reshape.484, f32[2048]{0:T(1024)S(1)} %bitcast.445, f32[2048]{0:T(1024)S(1)} %bitcast.446, f32[2048]{0:T(1024)S(1)} %bitcast.444, f32[2048]{0:T(1024)S(1)} %bitcast.443), kind=kLoop, calls=%fused_computation.14 | loop fusion | flops 14680064 | bytes 41975808 | tf_op jit(solution)/shard_map/add | solution.py:60
  48.8 4.6 subtract_multiply_fusion
  53.3 5.4 copy.159
  58.7 5.3 dot_general.83
  64.0 5.3 copy.161
  69.3 5.2 dot_general.87
  74.5 14.4 %fusion.48 = bf16[128,4,1,4,256]{4,0,3,1,2:T(8,128)(2,1)S(1)} fusion(f32[4,256,2048,1]{2,1,0,3:T(8,128)} %fusion.5, f32[128,4,2048,1]{2,1,0,3:T(4,128)} %bitcast.436), kind=kOutput, calls=%fused_computation.65 | convolution fusion | flops 6442975232 | bytes 13631488 | tf_op jit(solution)/shard_map/mc,nm->cn/dot_general | solution.py:71
  88.9 13.0 %fusion.51 = bf16[128,4,1,4,256]{4,0,3,1,2:T(8,128)(2,1)S(1)} fusion(f32[4,256,2048,1]{2,1,0,3:T(8,128)} %fusion.5, f32[128,4,2048,1]{2,1,0,3:T(4,128)S(1)} %bitcast.435), kind=kOutput, calls=%fused_computation.66 | convolution fusion | flops 6442975232 | bytes 13631488 | tf_op jit(solution)/shard_map/mc,nm->cn/dot_general | solution.py:71
  105.1 15.6 %all-to-all-start.3 = ((bf16[128,4,4,2,256]{4,2,1,3,0:T(4,128)(2,1)}), bf16[128,4,4,2,256]{4,2,1,3,0:T(4,128)(2,1)S(1)}, u32[]{:S(2)}, u32[]{:S(2)}) async-start(bf16[128,4,4,2,256]{4,2,1,3,0:T(4,128)(2,1)} %copy.163), calls=%async_computation.3 | async-start | bytes 4194304 | tf_op jit(solution)/shard_map/all_to_all | solution.py:79
  120.7 4.6 subtract_multiply_fusion.1
  125.3 5.4 copy.134
  130.6 5.3 dot_general.71
  135.9 5.3 copy.136
  141.2 5.2 dot_general.75
  146.4 14.2 %fusion.54 = bf16[128,4,1,4,256]{4,0,3,1,2:T(8,128)(2,1)S(1)} fusion(f32[4,256,2048,1]{2,1,0,3:T(8,128)} %fusion.5, f32[128,4,2048,1]{2,1,0,3:T(4,128)} %bitcast.437), kind=kOutput, calls=%fused_computation.67 | convolution fusion | flops 6442975232 | bytes 13631488 | tf_op jit(solution)/shard_map/mc,nm->cn/dot_general | solution.py:71
  160.6 13.0 %fusion.57 = bf16[128,4,1,4,256]{4,0,3,1,2:T(8,128)(2,1)S(1)} fusion(f32[4,256,2048,1]{2,1,0,3:T(8,128)} %fusion.5, f32[128,4,2048,1]{2,1,0,3:T(4,128)S(1)} %bitcast.434), kind=kOutput, calls=%fused_computation.68 | convolution fusion | flops 6442975232 | bytes 13631488 | tf_op jit(solution)/shard_map/mc,nm->cn/dot_general | solution.py:71
  176.8 10.8 %all-to-all-start = ((bf16[128,4,4,2,256]{4,2,1,3,0:T(4,128)(2,1)}), bf16[128,4,4,2,256]{4,2,1,3,0:T(4,128)(2,1)}, u32[]{:S(2)}, u32[]{:S(2)}) async-start(bf16[128,4,4,2,256]{4,2,1,3,0:T(4,128)(2,1)} %copy.138), calls=%async_computation | async-start | bytes 4194304 | tf_op jit(solution)/shard_map/all_to_all | solution.py:79
  192.4 23.6 %all-to-all-done = bf16[128,4,4,2,256]{4,2,1,3,0:T(4,128)(2,1)} async-done(((bf16[128,4,4,2,256]{4,2,1,3,0:T(4,128)(2,1)}), bf16[128,4,4,2,256]{4,2,1,3,0:T(4,128)(2,1)}, u32[]{:S(2)}, u32[]{:S(2)}) %all-to-all-start) | async-done | bytes 2097184 | tf_op jit(solution)/shard_map/all_to_all | solution.py:79
  223.8 5.6 gather_fusion.4
  229.4 5.5 gather_fusion.3
  242.5 5.2 fusion.34
  247.7 4.1 copy.167
  263.9 4.5 copy.145
  270.7 4.9 fusion.8
  279.2 4.4 copy.170
  301.7 5.1 all-to-all-start.5
  306.7 4.1 fusion.14
  331.7 7.3 %all-to-all-start.6 = ((f32[16,8,1024]{2,1,0:T(8,128)}), f32[16,8,1024]{2,1,0:T(8,128)S(1)}, u32[]{:S(2)}, u32[]{:S(2)}) async-start(f32[16,8,1024]{2,1,0:T(8,128)} %broadcast_multiply_fusion.2), calls=%async_computation.6 | async-start | bytes 1048576 | tf_op jit(solution)/shard_map/all_to_all | solution.py:109
  340.7 5.0 broadcast_multiply_fusion.1
  345.7 4.3 all-to-all-done.6
  350.8 5.7 all-to-all-start.2
  364.6 47.7 %all-to-all-done.2 = f32[16,4,2,32,256]{4,3,2,1,0:T(8,128)} async-done(((f32[16,4,2,32,256]{4,3,2,1,0:T(8,128)}), f32[16,4,2,32,256]{4,3,2,1,0:T(8,128)}, u32[]{:S(2)}, u32[]{:S(2)}) %all-to-all-start.2) | async-done | bytes 4194336 | tf_op jit(solution)/shard_map/all_to_all | solution.py:105
  412.2 7.2 %all-to-all-start.4 = ((f32[16,4,2,32,256]{4,3,2,1,0:T(8,128)}), f32[16,4,2,32,256]{4,3,2,1,0:T(8,128)}, u32[]{:S(2)}, u32[]{:S(2)}) async-start(f32[16,4,2,32,256]{4,3,2,1,0:T(8,128)} %broadcast_multiply_fusion), calls=%async_computation.4 | async-start | bytes 8388608 | tf_op jit(solution)/shard_map/all_to_all | solution.py:105
  423.8 4.1 fusion.60
  428.0 4.1 fusion.69
  432.1 6.0 reshape.566
  438.1 6.7 %copy.304 = f32[16,4,16384]{2,0,1:T(8,128)} copy(f32[16,4,16384]{2,1,0:T(4,128)} %reshape.566) | data formatting | bytes 8388608 | tf_op jit(solution)/shard_map/reshape | solution.py:106
  444.8 30.3 %all-to-all-done.4 = f32[16,4,2,32,256]{4,3,2,1,0:T(8,128)} async-done(((f32[16,4,2,32,256]{4,3,2,1,0:T(8,128)}), f32[16,4,2,32,256]{4,3,2,1,0:T(8,128)}, u32[]{:S(2)}, u32[]{:S(2)}) %all-to-all-start.4) | async-done | bytes 4194336 | tf_op jit(solution)/shard_map/all_to_all | solution.py:105
  475.1 5.8 reshape.567
  480.8 6.6 %copy.303 = f32[16,4,16384]{2,0,1:T(8,128)} copy(f32[16,4,16384]{2,1,0:T(4,128)} %reshape.567) | data formatting | bytes 8388608 | tf_op jit(solution)/shard_map/reshape | solution.py:106
  487.4 10.8 %dot_general.92 = f32[2,32,8,32,16,4]{3,2,1,0,4,5:T(8,128)} reshape(f32[16384,16,4]{0,1,2:T(8,128)} %bitcast.424) | data formatting | bytes 8388608 | tf_op jit(solution)/shard_map/bkx,bkc->xc/dot_general | solution.py:107
  498.2 10.8 %dot_general.80 = f32[2,32,8,32,16,4]{3,2,1,0,4,5:T(8,128)} reshape(f32[16384,16,4]{0,1,2:T(8,128)} %bitcast.423) | data formatting | bytes 8388608 | tf_op jit(solution)/shard_map/bkx,bkc->xc/dot_general | solution.py:107
  509.0 38.0 %fusion = f32[2,32,8,32,128,1]{4,3,5,2,1,0:T(8,128)S(1)} fusion(f32[16,4,128,1,1,1]{2,0,1,5,4,3:T(8,128)S(1)} %copy-done.17, f32[2,32,8,32,16,4]{3,2,1,0,4,5:T(8,128)} %dot_general.92), kind=kOutput, calls=%fused_computation.7 | convolution fusion | flops 1610612736 | bytes 12615680 | tf_op jit(solution)/shard_map/bkx,bkc->xc/dot_general | solution.py:107
  547.1 31.8 %bitcast_add_fusion = f32[2,32,8,32,128]{4,3,2,1,0:T(8,128)S(1)} fusion(f32[2,32,8,32,128,1]{4,3,5,2,1,0:T(8,128)S(1)} %fusion, f32[16,4,128,1,1,1]{2,0,1,5,4,3:T(8,128)S(1)} %copy-done.14, f32[2,32,8,32,16,4]{3,2,1,0,4,5:T(8,128)S(1)} %copy-done.4), kind=kOutput, calls=%fused_computation.20 | convolution fusion | flops 1612709888 | bytes 21004288 | tf_op jit(solution)/shard_map/bkx,bkc->xc/dot_general | solution.py:107
  578.9 4.8 maximum_bitcast_fusion
  583.7 15.0 %copy.191 = f32[2,9,32,32,128]{4,3,2,1,0:T(8,128)} copy(f32[2,9,32,32,128]{4,2,1,3,0:T(8,128)} %maximum_bitcast_fusion) | data formatting | bytes 18874368 | tf_op jit(solution)/shard_map/transpose | solution.py:121
  (197 shorter events, 110.2 us)
Async XLA Ops:
  0.0 42.5 %copy-start = (s32[1024]{0:T(1024)S(1)}, s32[1024]{0:T(1024)}, u32[]{:S(2)}) copy-start(s32[1024]{0:T(1024)} %param.18) | copy-start | bytes 12292
  1.3 37.5 %all-to-all-start.1 = ((f32[128,1,32]{2,1,0:T(1,128)}), f32[128,1,32]{2,1,0:T(1,128)S(1)}, u32[]{:S(2)}, u32[]{:S(2)}) async-start(f32[128,1,32]{2,1,0:T(1,128)} %broadcast_in_dim.17), calls=%async_computation.1 | async-start | bytes 131072 | tf_op jit(solution)/shard_map/all_to_all | solution.py:54
  21.6 17.2 %copy-start.18 = (s32[512]{0:T(512)S(1)}, s32[512]{0:T(512)}, u32[]{:S(2)}) copy-start(s32[512]{0:T(512)} %constant.95) | copy-start | bytes 6148
  21.6 20.8 %copy-start.20 = (s32[512]{0:T(512)S(1)}, s32[512]{0:T(512)}, u32[]{:S(2)}) copy-start(s32[512]{0:T(512)} %constant.96) | copy-start | bytes 6148
  38.8 6.6 %copy-start.19 = (s32[512]{0:T(512)S(1)}, s32[512]{0:T(512)}, u32[]{:S(2)}) copy-start(s32[512]{0:T(512)} %constant.94) | copy-start | bytes 6148
  74.5 14.4 %copy-start.11 = (f32[128,4,2048]{2,1,0:T(4,128)S(1)}, f32[128,4,2048]{2,1,0:T(4,128)}, u32[]{:S(2)}) copy-start(f32[128,4,2048]{2,1,0:T(4,128)} %dot_general.83) | copy-start | bytes 12582916
  105.1 71.6 %all-to-all-start.3 = ((bf16[128,4,4,2,256]{4,2,1,3,0:T(4,128)(2,1)}), bf16[128,4,4,2,256]{4,2,1,3,0:T(4,128)(2,1)S(1)}, u32[]{:S(2)}, u32[]{:S(2)}) async-start(bf16[128,4,4,2,256]{4,2,1,3,0:T(4,128)(2,1)} %copy.163), calls=%async_computation.3 | async-start | bytes 4194304 | tf_op jit(solution)/shard_map/all_to_all | solution.py:79
  146.4 14.2 %copy-start.10 = (f32[128,4,2048]{2,1,0:T(4,128)S(1)}, f32[128,4,2048]{2,1,0:T(4,128)}, u32[]{:S(2)}) copy-start(f32[128,4,2048]{2,1,0:T(4,128)} %dot_general.71) | copy-start | bytes 12582916
  176.8 39.3 %all-to-all-start = ((bf16[128,4,4,2,256]{4,2,1,3,0:T(4,128)(2,1)}), bf16[128,4,4,2,256]{4,2,1,3,0:T(4,128)(2,1)}, u32[]{:S(2)}, u32[]{:S(2)}) async-start(bf16[128,4,4,2,256]{4,2,1,3,0:T(4,128)(2,1)} %copy.138), calls=%async_computation | async-start | bytes 4194304 | tf_op jit(solution)/shard_map/all_to_all | solution.py:79
  257.2 2.0 copy-start.8
  257.2 2.6 copy-start.9
  263.9 4.5 copy-start.7
  275.6 3.6 copy-start.2
  279.2 4.4 copy-start.6
  286.2 20.6 %copy-start.12 = (bf16[4,512,2,256]{1,3,2,0:T(8,128)(2,1)S(1)}, bf16[4,512,2,256]{1,3,2,0:T(8,128)(2,1)}, u32[]{:S(2)}) copy-start(bf16[4,512,2,256]{1,3,2,0:T(8,128)(2,1)} %copy.170) | copy-start | bytes 6291460
  301.7 30.1 %all-to-all-start.5 = ((f32[16,8,1024]{2,1,0:T(8,128)}), f32[16,8,1024]{2,1,0:T(8,128)S(1)}, u32[]{:S(2)}, u32[]{:S(2)}) async-start(f32[16,8,1024]{2,1,0:T(8,128)} %broadcast_multiply_fusion.3), calls=%async_computation.5 | async-start | bytes 1048576 | tf_op jit(solution)/shard_map/all_to_all | solution.py:109
  310.8 3.4 copy-start.3
  316.4 4.1 slice-start
  318.5 2.4 slice-start.1
  331.7 18.3 %all-to-all-start.6 = ((f32[16,8,1024]{2,1,0:T(8,128)}), f32[16,8,1024]{2,1,0:T(8,128)S(1)}, u32[]{:S(2)}, u32[]{:S(2)}) async-start(f32[16,8,1024]{2,1,0:T(8,128)} %broadcast_multiply_fusion.2), calls=%async_computation.6 | async-start | bytes 1048576 | tf_op jit(solution)/shard_map/all_to_all | solution.py:109
  350.0 0.8 copy-start.13
  350.8 61.4 %all-to-all-start.2 = ((f32[16,4,2,32,256]{4,3,2,1,0:T(8,128)}), f32[16,4,2,32,256]{4,3,2,1,0:T(8,128)}, u32[]{:S(2)}, u32[]{:S(2)}) async-start(f32[16,4,2,32,256]{4,3,2,1,0:T(8,128)} %broadcast_multiply_fusion.1), calls=%async_computation.2 | async-start | bytes 8388608 | tf_op jit(solution)/shard_map/all_to_all | solution.py:105
  356.5 2.7 slice-start.2
  357.9 2.6 slice-start.3
  412.2 62.9 %all-to-all-start.4 = ((f32[16,4,2,32,256]{4,3,2,1,0:T(8,128)}), f32[16,4,2,32,256]{4,3,2,1,0:T(8,128)}, u32[]{:S(2)}, u32[]{:S(2)}) async-start(f32[16,4,2,32,256]{4,3,2,1,0:T(8,128)} %broadcast_multiply_fusion), calls=%async_computation.4 | async-start | bytes 8388608 | tf_op jit(solution)/shard_map/all_to_all | solution.py:105
  419.4 4.4 copy-start.16
  419.7 8.2 %copy-start.15 = (f32[16,4,128,1,1]{2,0,1,4,3:T(8,128)S(1)}, f32[16,4,128,1,1]{2,0,1,4,3:T(8,128)}, u32[]{:S(2)}) copy-start(f32[16,4,128,1,1]{2,0,1,4,3:T(8,128)} %constant.100) | copy-start | bytes 98308
  423.8 4.2 copy-start.5
  498.2 10.8 %copy-start.17 = (f32[16,4,128,1,1,1]{2,0,1,5,4,3:T(8,128)S(1)}, f32[16,4,128,1,1,1]{2,0,1,5,4,3:T(8,128)}, u32[]{:S(2)}) copy-start(f32[16,4,128,1,1,1]{2,0,1,5,4,3:T(8,128)} %constant.98) | copy-start | bytes 98308
  509.0 38.0 %copy-start.4 = (f32[2,32,8,32,16,4]{3,2,1,0,4,5:T(8,128)S(1)}, f32[2,32,8,32,16,4]{3,2,1,0,4,5:T(8,128)}, u32[]{:S(2)}) copy-start(f32[2,32,8,32,16,4]{3,2,1,0,4,5:T(8,128)} %dot_general.80) | copy-start | bytes 12582916
  509.0 38.0 %copy-start.14 = (f32[16,4,128,1,1,1]{2,0,1,5,4,3:T(8,128)S(1)}, f32[16,4,128,1,1,1]{2,0,1,5,4,3:T(8,128)}, u32[]{:S(2)}) copy-start(f32[16,4,128,1,1,1]{2,0,1,5,4,3:T(8,128)} %constant.97) | copy-start | bytes 98308
  583.7 15.0 %copy-start.1 = (s32[1024]{0:T(1024)S(1)}, s32[1024]{0:T(1024)}, u32[]{:S(2)}) copy-start(s32[1024]{0:T(1024)} %param.18) | copy-start | bytes 12292

commit v11 on v8

--- a/solution.py
+++ b/solution.py
@@ -12,7 +12,7 @@
 
 def phase_table(chans, rows, period):
     sample_index = jnp.arange(rows, dtype=jnp.int32)
-    product = sample_index[:, None] * chans[None, :] % period
+    product = chans[:, None] * sample_index[None, :] % period
     phase_arg = product.astype(jnp.float32) * (math.pi / (period // 2))
     return jnp.cos(phase_arg), jnp.sin(phase_arg)
 
@@ -25,10 +25,10 @@
     outer_chans = chans * inner_rows % period
     outer_cos, outer_sin = phase_table(outer_chans, outer_rows, period)
     scale = 1.0 / math.sqrt(channel_count)
-    cos = outer_cos[:, None, :] * inner_cos[None] - outer_sin[:, None, :] * inner_sin[None]
-    sin = outer_sin[:, None, :] * inner_cos[None] + outer_cos[:, None, :] * inner_sin[None]
+    cos = outer_cos[:, :, None] * inner_cos[:, None, :] - outer_sin[:, :, None] * inner_sin[:, None, :]
+    sin = outer_sin[:, :, None] * inner_cos[:, None, :] + outer_cos[:, :, None] * inner_sin[:, None, :]
     columns = chans.shape[0]
-    return (cos * scale).reshape(period, columns), (sin * -scale).reshape(period, columns)
+    return (cos * scale).reshape(columns, period), (sin * -scale).reshape(columns, period)
 
 
 def per_device(raw_voltages, filter_taps, input_order, chan_order):
@@ -65,7 +65,7 @@
         position = (dest_f * width + dest_b * chunk + within).reshape(-1)
         cos_table, sin_table = make_table(chan_order[position], channel_count)
         parts = [
-            jnp.einsum("mc,nm->cn", part, filtered, precision=lax.Precision.HIGH)
+            jnp.einsum("cm,nm->cn", part, filtered, precision=lax.Precision.HIGH)
             for part in (cos_table, sin_table)
         ]
         spectra = jnp.stack(parts, axis=1).astype(jnp.bfloat16)

time: 477 us -> 481 us (level)
  other arithmetic: 43.8 us -> 55.2 us
  local copies, waits for them, and re-layouts: 125 us -> 116 us
    dot_general x8 -> x0, local copies, waits for them, and re-layouts: 42.4 us -> none  [half_spectra(): jnp.einsum('mc,nm->cn', part, filtered, precision=lax.Precision.HIGH)]
    mul x0 -> x4, local copies, waits for them, and re-layouts: none -> 33.2 us  [the longest x2 16.6 us: make_table(): sin * -scale]
    mul x2, other arithmetic: 9.09 us -> 17.8 us  [make_table(): cos * scale]
  transfers between devices with their start and end apart: 5 -> 5, of which waited for: 3 -> 3; matrix products, arithmetic and copies ran while one was open for 40% -> 41% of each run, Pallas kernels for 0% -> 0%
where the time goes in v11:
time: 481 us; the launch traced here: 472 us
  waiting for transfers between devices  152 us (32%)
  local copies, waits for them, and re-layouts  116 us (24%)
  matrix products  103 us (21%)
  other arithmetic  55.2 us (11%)
  starting transfers between devices  44.7 us (9%)
    all_to_all x2, waiting for transfers between devices, half_output(): returned = lax.all_to_all(banded, 'blk', 0, 0, tiled=True)  132 us
    dot_general x4, matrix products, half_spectra(): jnp.einsum('cm,nm->cn', part, filtered, precision=lax.Precision.HIGH)  57 us
    dot_general x2, matrix products, half_output(): jnp.einsum('ax,ac->xc', returned, jnp.asarray(select), precision=lax.Prec...  36.4 us
    all_to_all x2, starting transfers between devices, half_band(): gathered = lax.all_to_all(spectra, ('blk', 'freq'), 0, 0, tiled=True)  20.6 us
    all_to_all x2, waiting for transfers between devices, half_band(): gathered = lax.all_to_all(spectra, ('blk', 'freq'), 0, 0, tiled=True)  20.1 us
    mul x2, other arithmetic, make_table(): cos * scale  17.8 us
    mul x2, local copies, waits for them, and re-layouts, make_table(): sin * -scale  16.6 us
    mul x2, local copies, waits for them, and re-layouts, make_table(): cos * scale  16.6 us
  transfers between devices with their start and end apart: 5, of which 3 were waited for; matrix products, arithmetic and copies ran while one was open for 41% of the time, Pallas kernels for 0%

profile of v11, /device:TPU:1, one launch (start us, length us, event | category | flops | bytes accessed | tf_op | source)
XLA Modules:
  0.0 471.7 jit_solution(8690315711304367038)
XLA Ops:
  1.3 11.5 %all-to-all-start.1 = ((f32[128,1,32]{2,1,0:T(1,128)}), f32[128,1,32]{2,1,0:T(1,128)S(1)}, u32[]{:S(2)}, u32[]{:S(2)}) async-start(f32[128,1,32]{2,1,0:T(1,128)} %broadcast_in_dim.13), calls=%async_computation.1 | async-start | bytes 131072 | tf_op jit(solution)/shard_map/all_to_all | solution.py:51
  13.5 2.3 gather_fusion
  15.8 1.1 fusion.113
  17.9 1.1 fusion.117
  19.0 7.9 %reshape.427 = f32[4,259,2048]{2,1,0:T(8,128)} reshape(bf16[4,530432]{1,0:T(4,128)(2,1)} %param.12) | data formatting | bytes 12730368 | tf_op jit(solution)/shard_map/reshape | solution.py:54
  26.8 8.8 %subtract_multiply_fusion.1 = (f32[512,32,64]{2,1,0:T(8,128)}, f32[512,32,64]{2,1,0:T(8,128)}) fusion(f32[512,64]{1,0:T(8,128)S(1)} %get-tuple-element.25, f32[512,32]{1,0:T(8,128)S(1)} %get-tuple-element.23, f32[512,64]{1,0:T(8,128)S(1)} %get-tuple-element.24, f32[512,32]{1,0:T(8,128)S(1)} %get-tuple-element.22), kind=kLoop, calls=%fused_computation.17 | loop fusion | flops 8388608 | bytes 8781824 | tf_op jit(solution)/shard_map/mul | solution.py:31
  35.7 8.3 %mul.388 = f32[128,4,2048]{2,1,0:T(4,128)} reshape(f32[512,32,64]{2,1,0:T(8,128)} %get-tuple-element.12) | data formatting | bytes 8388608 | tf_op jit(solution)/shard_map/mul | solution.py:31
  44.0 8.3 %mul.404 = f32[128,4,2048]{2,1,0:T(4,128)} reshape(f32[512,32,64]{2,1,0:T(8,128)} %get-tuple-element.13) | data formatting | bytes 8388608 | tf_op jit(solution)/shard_map/mul | solution.py:31
  52.3 14.0 %fusion.1 = f32[4,256,2048,1]{2,1,0,3:T(8,128)S(1)} fusion(f32[4,259,2048]{2,1,0:T(8,128)} %reshape.427, f32[2048]{0:T(1024)S(1)} %bitcast.297, f32[2048]{0:T(1024)S(1)} %bitcast.298, f32[2048]{0:T(1024)S(1)} %bitcast.296, f32[2048]{0:T(1024)S(1)} %bitcast.295), kind=kLoop, calls=%fused_computation.8 | loop fusion | flops 14680064 | bytes 41975808 | tf_op jit(solution)/shard_map/add | solution.py:57
  66.3 9.2 %fusion.47 = bf16[128,4,1,4,256]{4,0,3,1,2:T(8,128)(2,1)S(1)} fusion(f32[4,256,2048,1]{2,1,0,3:T(8,128)S(1)} %fusion.1, f32[128,4,2048,1]{2,1,0,3:T(4,128)S(1)} %bitcast.290), kind=kOutput, calls=%fused_computation.53 | convolution fusion | flops 6442975232 | bytes 13631488 | tf_op jit(solution)/shard_map/cm,nm->cn/dot_general | solution.py:68
  75.6 20.4 %fusion.44 = bf16[128,4,1,4,256]{4,0,3,1,2:T(8,128)(2,1)S(1)} fusion(f32[4,256,2048,1]{2,1,0,3:T(8,128)S(1)} %fusion.1, f32[128,4,2048,1]{2,1,0,3:T(4,128)S(1)} %bitcast.291), kind=kOutput, calls=%fused_computation.52 | convolution fusion | flops 6442975232 | bytes 13631488 | tf_op jit(solution)/shard_map/cm,nm->cn/dot_general | solution.py:68
  96.2 3.0 copy.69
  99.1 9.8 %all-to-all-start = ((bf16[128,4,4,2,256]{4,2,1,3,0:T(4,128)(2,1)}), bf16[128,4,4,2,256]{4,2,1,3,0:T(4,128)(2,1)S(1)}, u32[]{:S(2)}, u32[]{:S(2)}) async-start(bf16[128,4,4,2,256]{4,2,1,3,0:T(4,128)(2,1)} %copy.69), calls=%async_computation | async-start | bytes 4194304 | tf_op jit(solution)/shard_map/all_to_all | solution.py:76
  109.1 2.3 gather_fusion.1
  113.6 8.9 %subtract_multiply_fusion = (f32[512,32,64]{2,1,0:T(8,128)}, f32[512,32,64]{2,1,0:T(8,128)}) fusion(f32[512,64]{1,0:T(8,128)S(1)} %get-tuple-element.21, f32[512,32]{1,0:T(8,128)S(1)} %get-tuple-element.19, f32[512,64]{1,0:T(8,128)S(1)} %get-tuple-element.20, f32[512,32]{1,0:T(8,128)S(1)} %get-tuple-element.18), kind=kLoop, calls=%fused_computation.15 | loop fusion | flops 8388608 | bytes 8781824 | tf_op jit(solution)/shard_map/mul | solution.py:31
  122.5 8.3 %mul.422 = f32[128,4,2048]{2,1,0:T(4,128)} reshape(f32[512,32,64]{2,1,0:T(8,128)} %get-tuple-element.10) | data formatting | bytes 8388608 | tf_op jit(solution)/shard_map/mul | solution.py:31
  130.8 8.3 %mul.426 = f32[128,4,2048]{2,1,0:T(4,128)} reshape(f32[512,32,64]{2,1,0:T(8,128)} %get-tuple-element.11) | data formatting | bytes 8388608 | tf_op jit(solution)/shard_map/mul | solution.py:31
  139.1 14.2 %fusion.41 = bf16[128,4,1,4,256]{4,0,3,1,2:T(8,128)(2,1)S(1)} fusion(f32[4,256,2048,1]{2,1,0,3:T(8,128)} %copy-done.2, f32[128,4,2048,1]{2,1,0,3:T(4,128)} %bitcast.292), kind=kOutput, calls=%fused_computation.51 | convolution fusion | flops 6442975232 | bytes 13631488 | tf_op jit(solution)/shard_map/cm,nm->cn/dot_general | solution.py:68
  153.3 13.2 %fusion.38 = bf16[128,4,1,4,256]{4,0,3,1,2:T(8,128)(2,1)S(1)} fusion(f32[4,256,2048,1]{2,1,0,3:T(8,128)} %copy-done.2, f32[128,4,2048,1]{2,1,0,3:T(4,128)S(1)} %bitcast.293), kind=kOutput, calls=%fused_computation.50 | convolution fusion | flops 6442975232 | bytes 13631488 | tf_op jit(solution)/shard_map/cm,nm->cn/dot_general | solution.py:68
  166.7 2.9 copy.87
  169.7 10.8 %all-to-all-start.3 = ((bf16[128,4,4,2,256]{4,2,1,3,0:T(4,128)(2,1)}), bf16[128,4,4,2,256]{4,2,1,3,0:T(4,128)(2,1)}, u32[]{:S(2)}, u32[]{:S(2)}) async-start(bf16[128,4,4,2,256]{4,2,1,3,0:T(4,128)(2,1)} %copy.87), calls=%async_computation.3 | async-start | bytes 4194304 | tf_op jit(solution)/shard_map/all_to_all | solution.py:76
  180.5 2.2 copy.70
  182.7 2.7 copy.71
  185.4 3.8 gather_fusion.2
  189.1 20.1 %all-to-all-done.3 = bf16[128,4,4,2,256]{4,2,1,3,0:T(4,128)(2,1)} async-done(((bf16[128,4,4,2,256]{4,2,1,3,0:T(4,128)(2,1)}), bf16[128,4,4,2,256]{4,2,1,3,0:T(4,128)(2,1)}, u32[]{:S(2)}, u32[]{:S(2)}) %all-to-all-start.3) | async-done | bytes 2097184 | tf_op jit(solution)/shard_map/all_to_all | solution.py:76
  209.2 3.7 copy.88
  213.0 2.7 copy.89
  215.7 4.0 gather_fusion.3
  219.6 5.2 %fusion.24 = (bf16[4,512,2,256]{3,1,0,2:T(8,128)(2,1)S(1)}, bf16[4,512,2,256]{3,1,0,2:T(8,128)(2,1)}) fusion(bf16[512,4,2,256]{3,1,2,0:T(4,128)(2,1)} %gather_fusion.3, pred[512]{0:T(512)(128)(4,1)S(1)} %compare_and_fusion, bf16[512,4,2,256]{3,1,2,0:T(4,128)(2,1)} %gather_fusion.2), kind=kLoop, calls=%fused_computation.43 | loop fusion | flops 2097152 | bytes 8389120 | tf_op jit(solution)/shard_map/jit(_take)/select_n | solution.py:78
  224.8 4.1 copy.73
  228.9 2.7 slice_bitcast_fusion.1
  231.6 2.4 copy.91
  234.0 4.2 copy.92
  238.3 4.1 copy.74
  242.4 4.9 %fusion.4 = f32[4,1024,512]{2,1,0:T(8,128)S(1)} fusion(bf16[4,512,512]{1,2,0:T(8,128)(2,1)} %bitcast.287, bf16[4,512,256]{2,1,0:T(8,128)(2,1)} %get-tuple-element.9, bf16[4,512,256]{2,1,0:T(8,128)(2,1)S(1)} %get-tuple-element.8, bf16[4,512,512]{2,1,0:T(8,128)(2,1)} %copy.74), kind=kOutput, calls=%fused_computation.18 | convolution fusion | flops 2160066560 | bytes 14680064 | tf_op jit(solution)/shard_map/kat,kpt->kap/dot_general | solution.py:82
  249.7 3.4 broadcast_multiply_fusion.1
  253.1 6.1 %all-to-all-start.2 = ((f32[16,4,2,32,288]{4,3,2,1,0:T(8,128)}), f32[16,4,2,32,288]{4,3,2,1,0:T(8,128)}, u32[]{:S(2)}, u32[]{:S(2)}) async-start(f32[16,4,2,32,288]{4,3,2,1,0:T(8,128)} %broadcast_multiply_fusion.1), calls=%async_computation.2 | async-start | bytes 12582912 | tf_op jit(solution)/shard_map/all_to_all | solution.py:92
  259.3 4.6 fusion.10
  266.3 3.3 broadcast_multiply_fusion
  269.6 73.6 %all-to-all-done.2 = f32[16,4,2,32,288]{4,3,2,1,0:T(8,128)} async-done(((f32[16,4,2,32,288]{4,3,2,1,0:T(8,128)}), f32[16,4,2,32,288]{4,3,2,1,0:T(8,128)}, u32[]{:S(2)}, u32[]{:S(2)}) %all-to-all-start.2) | async-done | bytes 4718624 | tf_op jit(solution)/shard_map/all_to_all | solution.py:92
  343.2 6.5 %all-to-all-start.4 = ((f32[16,4,2,32,288]{4,3,2,1,0:T(8,128)}), f32[16,4,2,32,288]{4,3,2,1,0:T(8,128)}, u32[]{:S(2)}, u32[]{:S(2)}) async-start(f32[16,4,2,32,288]{4,3,2,1,0:T(8,128)} %broadcast_multiply_fusion), calls=%async_computation.4 | async-start | bytes 12582912 | tf_op jit(solution)/shard_map/all_to_all | solution.py:92
  349.7 7.0 %reshape.420 = f32[64,18432]{1,0:T(8,128)} reshape(f32[16,4,2,32,288]{4,3,2,1,0:T(8,128)} %all-to-all-done.2) | data formatting | bytes 9437184 | tf_op jit(solution)/shard_map/reshape | solution.py:93
  356.7 18.3 %fusion.124 = f32[18432,128]{1,0:T(8,128)} fusion(f32[64,18432]{1,0:T(8,128)} %reshape.420, f32[64,128]{1,0:T(8,128)S(1)} %copy-done.7), kind=kOutput, calls=%fused_computation.188 | convolution fusion | flops 1811939328 | bytes 14188544 | tf_op jit(solution)/shard_map/ax,ac->xc/dot_general | solution.py:96
  375.0 58.8 %all-to-all-done.4 = f32[16,4,2,32,288]{4,3,2,1,0:T(8,128)} async-done(((f32[16,4,2,32,288]{4,3,2,1,0:T(8,128)}), f32[16,4,2,32,288]{4,3,2,1,0:T(8,128)}, u32[]{:S(2)}, u32[]{:S(2)}) %all-to-all-start.4) | async-done | bytes 4718624 | tf_op jit(solution)/shard_map/all_to_all | solution.py:92
  433.8 6.9 %reshape.424 = f32[64,18432]{1,0:T(8,128)} reshape(f32[16,4,2,32,288]{4,3,2,1,0:T(8,128)} %all-to-all-done.4) | data formatting | bytes 9437184 | tf_op jit(solution)/shard_map/reshape | solution.py:93
  440.7 18.1 %convolution_add_fusion = f32[18432,128]{1,0:T(8,128)S(1)} fusion(f32[18432,128]{1,0:T(8,128)} %fusion.124, f32[64,18432]{1,0:T(8,128)} %reshape.424, f32[64,128]{1,0:T(8,128)S(1)} %copy-done.6), kind=kOutput, calls=%fused_computation.4 | convolution fusion | flops 1814298624 | bytes 23625728 | tf_op jit(solution)/shard_map/ax,ac->xc/dot_general | solution.py:96
  458.9 7.6 %copy.104 = f32[2,32,9,32,128]{4,1,3,2,0:T(8,128)S(1)} copy(f32[2,32,9,32,128]{4,3,2,1,0:T(8,128)S(1)} %bitcast.282) | data formatting | bytes 18874368 | tf_op jit(solution)/shard_map/reshape | solution.py:103
  466.4 4.9 %reverse_bitcast_fusion = f32[2,9,32,32,128]{4,3,2,1,0:T(8,128)} fusion(f32[2,32,9,32,128]{4,1,3,2,0:T(8,128)S(1)} %copy.104), kind=kLoop, calls=%fused_computation.5 | loop fusion | bytes 18874368 | tf_op jit(solution)/shard_map/transpose | solution.py:104
  (68 shorter events, 10.6 us)
Async XLA Ops:
  0.0 13.5 %copy-start = (s32[1024]{0:T(1024)S(1)}, s32[1024]{0:T(1024)}, u32[]{:S(2)}) copy-start(s32[1024]{0:T(1024)} %param.15) | copy-start | bytes 12292
  1.3 97.8 %all-to-all-start.1 = ((f32[128,1,32]{2,1,0:T(1,128)}), f32[128,1,32]{2,1,0:T(1,128)S(1)}, u32[]{:S(2)}, u32[]{:S(2)}) async-start(f32[128,1,32]{2,1,0:T(1,128)} %broadcast_in_dim.13), calls=%async_computation.1 | async-start | bytes 131072 | tf_op jit(solution)/shard_map/all_to_all | solution.py:51
  52.3 14.0 %copy-start.3 = (f32[128,4,2048]{2,1,0:T(4,128)S(1)}, f32[128,4,2048]{2,1,0:T(4,128)}, u32[]{:S(2)}) copy-start(f32[128,4,2048]{2,1,0:T(4,128)} %mul.388) | copy-start | bytes 12582916
  66.3 9.2 %copy-start.2 = (f32[4,256,2048,1]{2,1,0,3:T(8,128)}, f32[4,256,2048,1]{2,1,0,3:T(8,128)S(1)}, u32[]{:S(2)}) copy-start(f32[4,256,2048,1]{2,1,0,3:T(8,128)S(1)} %fusion.1) | copy-start | bytes 25165828
  66.3 9.2 %copy-start.4 = (f32[128,4,2048]{2,1,0:T(4,128)S(1)}, f32[128,4,2048]{2,1,0:T(4,128)}, u32[]{:S(2)}) copy-start(f32[128,4,2048]{2,1,0:T(4,128)} %mul.404) | copy-start | bytes 12582916
  96.0 13.1 %copy-start.8 = (s32[512]{0:T(512)S(1)}, s32[512]{0:T(512)}, u32[]{:S(2)}) copy-start(s32[512]{0:T(512)} %constant.88) | copy-start | bytes 6148
  99.1 70.5 %all-to-all-start = ((bf16[128,4,4,2,256]{4,2,1,3,0:T(4,128)(2,1)}), bf16[128,4,4,2,256]{4,2,1,3,0:T(4,128)(2,1)S(1)}, u32[]{:S(2)}, u32[]{:S(2)}) async-start(bf16[128,4,4,2,256]{4,2,1,3,0:T(4,128)(2,1)} %copy.69), calls=%async_computation | async-start | bytes 4194304 | tf_op jit(solution)/shard_map/all_to_all | solution.py:76
  139.1 14.2 %copy-start.5 = (f32[128,4,2048]{2,1,0:T(4,128)S(1)}, f32[128,4,2048]{2,1,0:T(4,128)}, u32[]{:S(2)}) copy-start(f32[128,4,2048]{2,1,0:T(4,128)} %mul.426) | copy-start | bytes 12582916
  169.7 39.5 %all-to-all-start.3 = ((bf16[128,4,4,2,256]{4,2,1,3,0:T(4,128)(2,1)}), bf16[128,4,4,2,256]{4,2,1,3,0:T(4,128)(2,1)}, u32[]{:S(2)}, u32[]{:S(2)}) async-start(bf16[128,4,4,2,256]{4,2,1,3,0:T(4,128)(2,1)} %copy.87), calls=%async_computation.3 | async-start | bytes 4194304 | tf_op jit(solution)/shard_map/all_to_all | solution.py:76
  253.1 90.0 %all-to-all-start.2 = ((f32[16,4,2,32,288]{4,3,2,1,0:T(8,128)}), f32[16,4,2,32,288]{4,3,2,1,0:T(8,128)}, u32[]{:S(2)}, u32[]{:S(2)}) async-start(f32[16,4,2,32,288]{4,3,2,1,0:T(8,128)} %broadcast_multiply_fusion.1), calls=%async_computation.2 | async-start | bytes 12582912 | tf_op jit(solution)/shard_map/all_to_all | solution.py:92
  343.2 90.6 %all-to-all-start.4 = ((f32[16,4,2,32,288]{4,3,2,1,0:T(8,128)}), f32[16,4,2,32,288]{4,3,2,1,0:T(8,128)}, u32[]{:S(2)}, u32[]{:S(2)}) async-start(f32[16,4,2,32,288]{4,3,2,1,0:T(8,128)} %broadcast_multiply_fusion), calls=%async_computation.4 | async-start | bytes 12582912 | tf_op jit(solution)/shard_map/all_to_all | solution.py:92
  349.7 7.0 %copy-start.7 = (f32[64,128]{1,0:T(8,128)S(1)}, f32[64,128]{1,0:T(8,128)}, u32[]{:S(2)}) copy-start(f32[64,128]{1,0:T(8,128)} %constant.82.clone) | copy-start | bytes 98308
  375.0 65.7 %copy-start.6 = (f32[64,128]{1,0:T(8,128)S(1)}, f32[64,128]{1,0:T(8,128)}, u32[]{:S(2)}) copy-start(f32[64,128]{1,0:T(8,128)} %constant.83.clone) | copy-start | bytes 98308
  458.9 12.4 %copy-start.1 = (s32[1024]{0:T(1024)S(1)}, s32[1024]{0:T(1024)}, u32[]{:S(2)}) copy-start(s32[1024]{0:T(1024)} %param.15) | copy-start | bytes 12292

commit v12 on v8

--- a/solution.py
+++ b/solution.py
@@ -5,6 +5,7 @@
 import jax.numpy as jnp
 from jax import lax
 from jax.sharding import PartitionSpec as P
+
 
 TAPS = 4
 SPECTRA = 256
@@ -46,6 +47,9 @@
     total_inputs = n_dev * local_inputs
     frame = 2 * channel_count
     rows = steps * tile
+    reverse_tiles = (
+        (n_blk - 1 - np.arange(n_blk))[:, None] * tile + np.arange(tile)[None, :]
+    ).reshape(-1)
 
     spread = jnp.broadcast_to(input_order.astype(jnp.float32)[None], (n_dev, tile))
     slot_order = lax.all_to_all(spread, ("blk", "freq"), 0, 0, tiled=True)
@@ -72,19 +76,23 @@
         spectra = spectra.reshape(n_dev, part_chunk, 2, local_inputs, SPECTRA)
         return spectra.transpose(0, 1, 3, 2, 4)
 
-    def half_band(spectra):
+    def half_band(spectra, earlier):
         gathered = lax.all_to_all(spectra, ("blk", "freq"), 0, 0, tiled=True)
+        if earlier is not None:
+            earlier, gathered = lax.optimization_barrier((earlier, gathered))
         gathered = gathered.transpose(1, 0, 2, 3, 4).reshape(part_chunk, total_inputs, 2, SPECTRA)
         slotted = jnp.take(gathered, slot_order, axis=1)
         plain = slotted.reshape(part_chunk, total_inputs, 2 * SPECTRA)
         rotated = jnp.concatenate([slotted[:, :, 1], -slotted[:, :, 0]], axis=2)
         both = jnp.concatenate([plain, rotated], axis=1)
-        gram = jnp.einsum("kat,kpt->kap", both, plain, preferred_element_type=jnp.float32)
+        partners = jnp.take(gathered, slot_order[reverse_tiles], axis=1)
+        partners = partners.reshape(part_chunk, total_inputs, 2 * SPECTRA)
+        gram = jnp.einsum("kat,kpt->kap", both, partners, preferred_element_type=jnp.float32)
         gram = gram.reshape(part_chunk, 2, n_blk, tile, total_inputs)
         doubled = jnp.concatenate([gram, gram], axis=-1)
         blocks = []
         for own in range(n_blk):
-            start = (own - steps + 1) % n_blk * tile
+            start = (n_blk - 1 - own) * tile
             blocks.append(doubled[:, :, own, :, start : start + rows])
         return jnp.stack(blocks) * (1.0 / SPECTRA)
 
@@ -96,11 +104,13 @@
         return jnp.einsum("ax,ac->xc", returned, jnp.asarray(select), precision=lax.Precision.HIGHEST)
 
     spectra_parts = [half_spectra(half) for half in range(halves)]
-    band_parts = [half_band(spectra) for spectra in spectra_parts]
+    band_parts = []
+    for spectra in spectra_parts:
+        band_parts.append(half_band(spectra, band_parts[-1] if band_parts else None))
     turned = half_output(band_parts[0], 0)
     for half in range(1, halves):
         turned = turned + half_output(band_parts[half], half)
-    turned = turned.reshape(2, tile, steps, tile, n_blk * chunk)[:, :, ::-1]
+    turned = turned.reshape(2, tile, steps, tile, n_blk * chunk)
     return turned.transpose(0, 2, 3, 1, 4)
 
 

time: 477 us -> 468 us (0.981)
  waiting for transfers between devices: 152 us -> 115 us
  local copies, waits for them, and re-layouts: 125 us -> 143 us
  other arithmetic: 43.8 us -> 51.8 us
    all_to_all x2, waiting for transfers between devices: 20.1 us -> 0.01 us  [half_band(): gathered = lax.all_to_all(spectra, ('blk', 'freq'), 0, 0, tiled=True)]
    all_to_all x2, waiting for transfers between devices: 132 us -> 115 us  [half_output(): returned = lax.all_to_all(banded, 'blk', 0, 0, tiled=True)]
    gather x0 -> x3, local copies, waits for them, and re-layouts: none -> 13 us  [half_band(): partners = jnp.take(gathered, slot_order[reverse_tiles], axis=1)]
    select_n x0 -> x2, local copies, waits for them, and re-layouts: none -> 8.57 us  [half_band(): partners = jnp.take(gathered, slot_order[reverse_tiles], axis=1)]
    select_n x0 -> x3, other arithmetic: none -> 8.01 us  [half_band(): partners = jnp.take(gathered, slot_order[reverse_tiles], axis=1)]
    transpose x1 -> x0, local copies, waits for them, and re-layouts: 4.86 us -> none  [per_device(): return turned.transpose(0, 2, 3, 1, 4)]
  transfers between devices with their start and end apart: 5 -> 5, of which waited for: 3 -> 2; matrix products, arithmetic and copies ran while one was open for 40% -> 39% of each run, Pallas kernels for 0% -> 0%
where the time goes in v12:
time: 468 us; the launch traced here: 459 us
  local copies, waits for them, and re-layouts  143 us (31%)
  waiting for transfers between devices  115 us (25%)
  matrix products  101 us (22%)
  other arithmetic  51.8 us (11%)
  starting transfers between devices  46.9 us (10%)
    all_to_all x2, waiting for transfers between devices, half_output(): returned = lax.all_to_all(banded, 'blk', 0, 0, tiled=True)  115 us
    dot_general x4, matrix products, half_spectra(): jnp.einsum('mc,nm->cn', part, filtered, precision=lax.Precision.HIGH)  55 us
    dot_general x8, local copies, waits for them, and re-layouts, half_spectra(): jnp.einsum('mc,nm->cn', part, filtered, precision=lax.Precision.HIGH)  42.4 us
    dot_general x2, matrix products, half_output(): jnp.einsum('ax,ac->xc', returned, jnp.asarray(select), precision=lax.Prec...  36.5 us
    all_to_all x2, starting transfers between devices, half_band(): gathered = lax.all_to_all(spectra, ('blk', 'freq'), 0, 0, tiled=True)  20.3 us
    add x1, other arithmetic, per_device(): filtered + filter_taps[tap_index] * frames[:, tap_index:tap_index + SPECTRA]  17.1 us
    all_to_all x2, starting transfers between devices, half_output(): returned = lax.all_to_all(banded, 'blk', 0, 0, tiled=True)  15.1 us
    reshape x2, local copies, waits for them, and re-layouts, half_output(): returned = returned.reshape(n_blk * part_chunk, 2 * tile * rows)  13.9 us
  transfers between devices with their start and end apart: 5, of which 2 were waited for; matrix products, arithmetic and copies ran while one was open for 39% of the time, Pallas kernels for 0%

profile of v12, /device:TPU:1, one launch (start us, length us, event | category | flops | bytes accessed | tf_op | source)
XLA Modules:
  0.0 458.7 jit_solution(17026772104524833388)
XLA Ops:
  1.3 11.5 %all-to-all-start.1 = ((f32[128,1,32]{2,1,0:T(1,128)}), f32[128,1,32]{2,1,0:T(1,128)S(1)}, u32[]{:S(2)}, u32[]{:S(2)}) async-start(f32[128,1,32]{2,1,0:T(1,128)} %broadcast_in_dim.17), calls=%async_computation.1 | async-start | bytes 131072 | tf_op jit(solution)/shard_map/all_to_all | solution.py:55
  13.8 7.9 %reshape.403 = f32[4,259,2048]{2,1,0:T(8,128)} reshape(bf16[4,530432]{1,0:T(4,128)(2,1)} %param.15) | data formatting | bytes 12730368 | tf_op jit(solution)/shard_map/reshape | solution.py:58
  21.6 17.1 %fusion.1 = f32[4,256,2048,1]{2,1,0,3:T(8,128)} fusion(f32[4,259,2048]{2,1,0:T(8,128)} %reshape.403, f32[2048]{0:T(1024)S(1)} %bitcast.320, f32[2048]{0:T(1024)S(1)} %bitcast.321, f32[2048]{0:T(1024)S(1)} %bitcast.319, f32[2048]{0:T(1024)S(1)} %bitcast.318), kind=kLoop, calls=%fused_computation.11 | loop fusion | flops 14680064 | bytes 41975808 | tf_op jit(solution)/shard_map/add | solution.py:61
  41.8 3.5 gather_fusion.1
  48.5 4.6 %subtract_multiply_fusion.1 = (f32[32,64,512]{2,1,0:T(8,128)}, f32[32,64,512]{2,1,0:T(8,128)}) fusion(f32[64,512]{1,0:T(8,128)S(1)} %get-tuple-element.27, f32[32,512]{1,0:T(8,128)S(1)} %get-tuple-element.25, f32[64,512]{1,0:T(8,128)S(1)} %get-tuple-element.26, f32[32,512]{1,0:T(8,128)S(1)} %get-tuple-element.24), kind=kLoop, calls=%fused_computation.40 | loop fusion | flops 8388608 | bytes 8781824 | tf_op jit(solution)/shard_map/mul | solution.py:32
  53.1 5.5 %copy.114 = f32[512,2048]{1,0:T(8,128)} copy(f32[512,2048]{0,1:T(8,128)} %bitcast.304) | data formatting | bytes 8388608 | tf_op jit(solution)/shard_map/mc,nm->cn/dot_general | solution.py:72
  58.5 5.2 %dot_general.49 = f32[128,4,2048]{2,1,0:T(4,128)} reshape(f32[512,2048]{1,0:T(8,128)} %copy.114) | data formatting | bytes 8388608 | tf_op jit(solution)/shard_map/mc,nm->cn/dot_general | solution.py:72
  63.7 5.3 %copy.116 = f32[512,2048]{1,0:T(8,128)} copy(f32[512,2048]{0,1:T(8,128)} %bitcast.302) | data formatting | bytes 8388608 | tf_op jit(solution)/shard_map/mc,nm->cn/dot_general | solution.py:72
  69.1 5.2 %dot_general.53 = f32[128,4,2048]{2,1,0:T(4,128)} reshape(f32[512,2048]{1,0:T(8,128)} %copy.116) | data formatting | bytes 8388608 | tf_op jit(solution)/shard_map/mc,nm->cn/dot_general | solution.py:72
  74.3 14.3 %fusion.47 = bf16[128,4,1,4,256]{4,0,3,1,2:T(8,128)(2,1)S(1)} fusion(f32[4,256,2048,1]{2,1,0,3:T(8,128)} %fusion.1, f32[128,4,2048,1]{2,1,0,3:T(4,128)} %bitcast.311), kind=kOutput, calls=%fused_computation.58 | convolution fusion | flops 6442975232 | bytes 13631488 | tf_op jit(solution)/shard_map/mc,nm->cn/dot_general | solution.py:72
  88.6 13.0 %fusion.44 = bf16[128,4,1,4,256]{4,0,3,1,2:T(8,128)(2,1)S(1)} fusion(f32[4,256,2048,1]{2,1,0,3:T(8,128)} %fusion.1, f32[128,4,2048,1]{2,1,0,3:T(4,128)S(1)} %bitcast.314), kind=kOutput, calls=%fused_computation.57 | convolution fusion | flops 6442975232 | bytes 13631488 | tf_op jit(solution)/shard_map/mc,nm->cn/dot_general | solution.py:72
  101.8 3.0 copy.118
  104.8 9.8 %all-to-all-start = ((bf16[128,4,4,2,256]{4,2,1,3,0:T(4,128)(2,1)}), bf16[128,4,4,2,256]{4,2,1,3,0:T(4,128)(2,1)S(1)}, u32[]{:S(2)}, u32[]{:S(2)}) async-start(bf16[128,4,4,2,256]{4,2,1,3,0:T(4,128)(2,1)} %copy.118), calls=%async_computation | async-start | bytes 4194304 | tf_op jit(solution)/shard_map/all_to_all | solution.py:80
  114.9 4.6 %subtract_multiply_fusion = (f32[32,64,512]{2,1,0:T(8,128)}, f32[32,64,512]{2,1,0:T(8,128)}) fusion(f32[64,512]{1,0:T(8,128)S(1)} %get-tuple-element.23, f32[32,512]{1,0:T(8,128)S(1)} %get-tuple-element.21, f32[64,512]{1,0:T(8,128)S(1)} %get-tuple-element.22, f32[32,512]{1,0:T(8,128)S(1)} %get-tuple-element.20), kind=kLoop, calls=%fused_computation.38 | loop fusion | flops 8388608 | bytes 8781824 | tf_op jit(solution)/shard_map/mul | solution.py:32
  119.5 5.4 %copy.138 = f32[512,2048]{1,0:T(8,128)} copy(f32[512,2048]{0,1:T(8,128)} %bitcast.305) | data formatting | bytes 8388608 | tf_op jit(solution)/shard_map/mc,nm->cn/dot_general | solution.py:72
  124.9 5.2 %dot_general.63 = f32[128,4,2048]{2,1,0:T(4,128)} reshape(f32[512,2048]{1,0:T(8,128)} %copy.138) | data formatting | bytes 8388608 | tf_op jit(solution)/shard_map/mc,nm->cn/dot_general | solution.py:72
  130.1 5.4 %copy.136 = f32[512,2048]{1,0:T(8,128)} copy(f32[512,2048]{0,1:T(8,128)} %bitcast.303) | data formatting | bytes 8388608 | tf_op jit(solution)/shard_map/mc,nm->cn/dot_general | solution.py:72
  135.6 5.2 %dot_general.59 = f32[128,4,2048]{2,1,0:T(4,128)} reshape(f32[512,2048]{1,0:T(8,128)} %copy.136) | data formatting | bytes 8388608 | tf_op jit(solution)/shard_map/mc,nm->cn/dot_general | solution.py:72
  140.7 14.2 %fusion.38 = bf16[128,4,1,4,256]{4,0,3,1,2:T(8,128)(2,1)S(1)} fusion(f32[4,256,2048,1]{2,1,0,3:T(8,128)} %fusion.1, f32[128,4,2048,1]{2,1,0,3:T(4,128)} %bitcast.312), kind=kOutput, calls=%fused_computation.55 | convolution fusion | flops 6442975232 | bytes 13631488 | tf_op jit(solution)/shard_map/mc,nm->cn/dot_general | solution.py:72
  154.9 13.4 %fusion.41 = bf16[128,4,1,4,256]{4,0,3,1,2:T(8,128)(2,1)S(1)} fusion(f32[4,256,2048,1]{2,1,0,3:T(8,128)} %fusion.1, f32[128,4,2048,1]{2,1,0,3:T(4,128)S(1)} %bitcast.313), kind=kOutput, calls=%fused_computation.56 | convolution fusion | flops 6442975232 | bytes 13631488 | tf_op jit(solution)/shard_map/mc,nm->cn/dot_general | solution.py:72
  168.5 3.0 copy.140
  171.5 10.6 %all-to-all-start.3 = ((bf16[128,4,4,2,256]{4,2,1,3,0:T(4,128)(2,1)}), bf16[128,4,4,2,256]{4,2,1,3,0:T(4,128)(2,1)}, u32[]{:S(2)}, u32[]{:S(2)}) async-start(bf16[128,4,4,2,256]{4,2,1,3,0:T(4,128)(2,1)} %copy.140), calls=%async_computation.3 | async-start | bytes 4194304 | tf_op jit(solution)/shard_map/all_to_all | solution.py:80
  184.3 2.7 copy.120
  188.3 3.8 gather_fusion.3
  197.7 5.6 %gather_fusion.4 = bf16[512,4,2,256]{3,1,2,0:T(4,128)(2,1)} fusion(bf16[4,512,2,256]{3,0,2,1:T(4,128)(2,1)} %copy-done.2, s32[1024]{0:T(1024)S(1)} %get-tuple-element.29), kind=kCustom, calls=%fused_computation.1.clone | custom fusion | bytes 4196352 | tf_op jit(solution)/shard_map/jit(_take)/gather | solution.py:88
  203.4 3.9 select_bitcast_fusion.1
  207.3 4.3 copy.125
  211.6 2.5 copy.123
  214.2 4.9 %fusion.4 = f32[4,1024,512]{2,1,0:T(8,128)S(1)} fusion(bf16[4,512,512]{1,2,0:T(8,128)(2,1)} %bitcast.316, bf16[4,512,256]{2,1,0:T(8,128)(2,1)} %get-tuple-element.11, bf16[4,512,256]{2,1,0:T(8,128)(2,1)S(1)} %get-tuple-element.10, bf16[4,512,512]{2,1,0:T(8,128)(2,1)} %copy.123), kind=kOutput, calls=%fused_computation.17 | convolution fusion | flops 2160066560 | bytes 14680064 | tf_op jit(solution)/shard_map/kat,kpt->kap/dot_general | solution.py:90
  221.5 3.4 broadcast_multiply_fusion.1
  224.9 3.7 copy.141
  228.6 2.7 copy.142
  231.4 3.8 gather_fusion.5
  235.2 3.9 gather_fusion.6
  239.1 8.1 %all-to-all-start.2 = ((f32[16,4,2,32,288]{4,3,2,1,0:T(8,128)}), f32[16,4,2,32,288]{4,3,2,1,0:T(8,128)}, u32[]{:S(2)}, u32[]{:S(2)}) async-start(f32[16,4,2,32,288]{4,3,2,1,0:T(8,128)} %broadcast_multiply_fusion.1), calls=%async_computation.2 | async-start | bytes 12582912 | tf_op jit(solution)/shard_map/all_to_all | solution.py:100
  251.7 4.2 copy.145
  255.9 4.1 select_bitcast_fusion
  260.0 4.3 copy.147
  264.4 4.6 fusion.10
  271.4 3.3 broadcast_multiply_fusion
  274.7 56.4 %all-to-all-done.2 = f32[16,4,2,32,288]{4,3,2,1,0:T(8,128)} async-done(((f32[16,4,2,32,288]{4,3,2,1,0:T(8,128)}), f32[16,4,2,32,288]{4,3,2,1,0:T(8,128)}, u32[]{:S(2)}, u32[]{:S(2)}) %all-to-all-start.2) | async-done | bytes 4718624 | tf_op jit(solution)/shard_map/all_to_all | solution.py:100
  331.1 6.9 %all-to-all-start.4 = ((f32[16,4,2,32,288]{4,3,2,1,0:T(8,128)}), f32[16,4,2,32,288]{4,3,2,1,0:T(8,128)}, u32[]{:S(2)}, u32[]{:S(2)}) async-start(f32[16,4,2,32,288]{4,3,2,1,0:T(8,128)} %broadcast_multiply_fusion), calls=%async_computation.4 | async-start | bytes 12582912 | tf_op jit(solution)/shard_map/all_to_all | solution.py:100
  338.1 7.0 %reshape.395 = f32[64,18432]{1,0:T(8,128)} reshape(f32[16,4,2,32,288]{4,3,2,1,0:T(8,128)} %all-to-all-done.2) | data formatting | bytes 9437184 | tf_op jit(solution)/shard_map/reshape | solution.py:101
  345.0 18.3 %fusion.124 = f32[18432,128]{1,0:T(8,128)} fusion(f32[64,18432]{1,0:T(8,128)} %reshape.395, f32[64,128]{1,0:T(8,128)S(1)} %copy-done.7), kind=kOutput, calls=%fused_computation.197 | convolution fusion | flops 1811939328 | bytes 14188544 | tf_op jit(solution)/shard_map/ax,ac->xc/dot_general | solution.py:104
  363.3 58.6 %all-to-all-done.4 = f32[16,4,2,32,288]{4,3,2,1,0:T(8,128)} async-done(((f32[16,4,2,32,288]{4,3,2,1,0:T(8,128)}), f32[16,4,2,32,288]{4,3,2,1,0:T(8,128)}, u32[]{:S(2)}, u32[]{:S(2)}) %all-to-all-start.4) | async-done | bytes 4718624 | tf_op jit(solution)/shard_map/all_to_all | solution.py:100
  421.9 6.9 %reshape.400 = f32[64,18432]{1,0:T(8,128)} reshape(f32[16,4,2,32,288]{4,3,2,1,0:T(8,128)} %all-to-all-done.4) | data formatting | bytes 9437184 | tf_op jit(solution)/shard_map/reshape | solution.py:101
  428.9 18.2 %convolution_add_fusion = f32[18432,128]{1,0:T(8,128)S(1)} fusion(f32[18432,128]{1,0:T(8,128)} %fusion.124, f32[64,18432]{1,0:T(8,128)} %reshape.400, f32[64,128]{1,0:T(8,128)S(1)} %copy-done.6), kind=kOutput, calls=%fused_computation.7 | convolution fusion | flops 1814298624 | bytes 23625728 | tf_op jit(solution)/shard_map/ax,ac->xc/dot_general | solution.py:104
  447.1 11.3 %copy.238 = f32[2,32,9,32,128]{4,1,3,2,0:T(8,128)} copy(f32[2,32,9,32,128]{4,3,2,1,0:T(8,128)S(1)} %bitcast.301) | data formatting | bytes 18874368 | tf_op jit(solution)/shard_map/reshape | solution.py:113
  (86 shorter events, 27.5 us)
Async XLA Ops:
  0.0 38.9 %copy-start = (s32[1024]{0:T(1024)S(1)}, s32[1024]{0:T(1024)}, u32[]{:S(2)}) copy-start(s32[1024]{0:T(1024)} %param.18) | copy-start | bytes 12292
  1.3 37.5 %all-to-all-start.1 = ((f32[128,1,32]{2,1,0:T(1,128)}), f32[128,1,32]{2,1,0:T(1,128)S(1)}, u32[]{:S(2)}, u32[]{:S(2)}) async-start(f32[128,1,32]{2,1,0:T(1,128)} %broadcast_in_dim.17), calls=%async_computation.1 | async-start | bytes 131072 | tf_op jit(solution)/shard_map/all_to_all | solution.py:55
  21.6 17.1 %copy-start.8 = (s32[512]{0:T(512)S(1)}, s32[512]{0:T(512)}, u32[]{:S(2)}) copy-start(s32[512]{0:T(512)} %constant.94) | copy-start | bytes 6148
  21.6 17.3 %copy-start.10 = (s32[512]{0:T(512)S(1)}, s32[512]{0:T(512)}, u32[]{:S(2)}) copy-start(s32[512]{0:T(512)} %constant.93) | copy-start | bytes 6148
  21.6 23.7 %copy-start.9 = (s32[512]{0:T(512)S(1)}, s32[512]{0:T(512)}, u32[]{:S(2)}) copy-start(s32[512]{0:T(512)} %constant.95) | copy-start | bytes 6148
  74.3 14.3 %copy-start.5 = (f32[128,4,2048]{2,1,0:T(4,128)S(1)}, f32[128,4,2048]{2,1,0:T(4,128)}, u32[]{:S(2)}) copy-start(f32[128,4,2048]{2,1,0:T(4,128)} %dot_general.53) | copy-start | bytes 12582916
  104.8 66.7 %all-to-all-start = ((bf16[128,4,4,2,256]{4,2,1,3,0:T(4,128)(2,1)}), bf16[128,4,4,2,256]{4,2,1,3,0:T(4,128)(2,1)S(1)}, u32[]{:S(2)}, u32[]{:S(2)}) async-start(bf16[128,4,4,2,256]{4,2,1,3,0:T(4,128)(2,1)} %copy.118), calls=%async_computation | async-start | bytes 4194304 | tf_op jit(solution)/shard_map/all_to_all | solution.py:80
  140.7 14.2 %copy-start.4 = (f32[128,4,2048]{2,1,0:T(4,128)S(1)}, f32[128,4,2048]{2,1,0:T(4,128)}, u32[]{:S(2)}) copy-start(f32[128,4,2048]{2,1,0:T(4,128)} %dot_general.59) | copy-start | bytes 12582916
  171.5 53.4 %all-to-all-start.3 = ((bf16[128,4,4,2,256]{4,2,1,3,0:T(4,128)(2,1)}), bf16[128,4,4,2,256]{4,2,1,3,0:T(4,128)(2,1)}, u32[]{:S(2)}, u32[]{:S(2)}) async-start(bf16[128,4,4,2,256]{4,2,1,3,0:T(4,128)(2,1)} %copy.140), calls=%async_computation.3 | async-start | bytes 4194304 | tf_op jit(solution)/shard_map/all_to_all | solution.py:80
  187.0 1.3 copy-start.2
  197.7 13.9 %copy-start.3 = (bf16[4,512,2,256]{1,3,2,0:T(8,128)(2,1)S(1)}, bf16[4,512,2,256]{1,3,2,0:T(8,128)(2,1)}, u32[]{:S(2)}) copy-start(bf16[4,512,2,256]{1,3,2,0:T(8,128)(2,1)} %copy.122) | copy-start | bytes 6291460
  239.1 92.0 %all-to-all-start.2 = ((f32[16,4,2,32,288]{4,3,2,1,0:T(8,128)}), f32[16,4,2,32,288]{4,3,2,1,0:T(8,128)}, u32[]{:S(2)}, u32[]{:S(2)}) async-start(f32[16,4,2,32,288]{4,3,2,1,0:T(8,128)} %broadcast_multiply_fusion.1), calls=%async_computation.2 | async-start | bytes 12582912 | tf_op jit(solution)/shard_map/all_to_all | solution.py:100
  331.1 90.8 %all-to-all-start.4 = ((f32[16,4,2,32,288]{4,3,2,1,0:T(8,128)}), f32[16,4,2,32,288]{4,3,2,1,0:T(8,128)}, u32[]{:S(2)}, u32[]{:S(2)}) async-start(f32[16,4,2,32,288]{4,3,2,1,0:T(8,128)} %broadcast_multiply_fusion), calls=%async_computation.4 | async-start | bytes 12582912 | tf_op jit(solution)/shard_map/all_to_all | solution.py:100
  338.0 7.0 %copy-start.7 = (f32[64,128]{1,0:T(8,128)S(1)}, f32[64,128]{1,0:T(8,128)}, u32[]{:S(2)}) copy-start(f32[64,128]{1,0:T(8,128)} %constant.87.clone) | copy-start | bytes 98308
  363.3 65.6 %copy-start.6 = (f32[64,128]{1,0:T(8,128)S(1)}, f32[64,128]{1,0:T(8,128)}, u32[]{:S(2)}) copy-start(f32[64,128]{1,0:T(8,128)} %constant.88.clone) | copy-start | bytes 98308
  447.1 11.3 %copy-start.1 = (s32[1024]{0:T(1024)S(1)}, s32[1024]{0:T(1024)}, u32[]{:S(2)}) copy-start(s32[1024]{0:T(1024)} %param.18) | copy-start | bytes 12292

commit v13 on v8

--- a/solution.py
+++ b/solution.py
@@ -5,6 +5,7 @@
 import jax.numpy as jnp
 from jax import lax
 from jax.sharding import PartitionSpec as P
+
 
 TAPS = 4
 SPECTRA = 256
@@ -72,8 +73,10 @@
         spectra = spectra.reshape(n_dev, part_chunk, 2, local_inputs, SPECTRA)
         return spectra.transpose(0, 1, 3, 2, 4)
 
-    def half_band(spectra):
+    def half_band(spectra, earlier):
         gathered = lax.all_to_all(spectra, ("blk", "freq"), 0, 0, tiled=True)
+        if earlier is not None:
+            earlier, gathered = lax.optimization_barrier((earlier, gathered))
         gathered = gathered.transpose(1, 0, 2, 3, 4).reshape(part_chunk, total_inputs, 2, SPECTRA)
         slotted = jnp.take(gathered, slot_order, axis=1)
         plain = slotted.reshape(part_chunk, total_inputs, 2 * SPECTRA)
@@ -93,10 +96,18 @@
         returned = returned.reshape(n_blk * part_chunk, 2 * tile * rows)
         source = np.arange(n_blk)[:, None] * chunk + half * part_chunk + np.arange(part_chunk)[None, :]
         select = (source.reshape(-1, 1) == np.arange(n_blk * chunk)[None, :]).astype(np.float32)
-        return jnp.einsum("ax,ac->xc", returned, jnp.asarray(select), precision=lax.Precision.HIGHEST)
+        high = returned.astype(jnp.bfloat16)
+        rest = returned - high.astype(jnp.float32)
+        middle = rest.astype(jnp.bfloat16)
+        low = (rest - middle.astype(jnp.float32)).astype(jnp.bfloat16)
+        pieces = jnp.concatenate([high, middle, low], axis=0)
+        select = jnp.asarray(np.concatenate([select] * 3, axis=0), dtype=jnp.bfloat16)
+        return jnp.einsum("ax,ac->xc", pieces, select, preferred_element_type=jnp.float32)
 
     spectra_parts = [half_spectra(half) for half in range(halves)]
-    band_parts = [half_band(spectra) for spectra in spectra_parts]
+    band_parts = []
+    for spectra in spectra_parts:
+        band_parts.append(half_band(spectra, band_parts[-1] if band_parts else None))
     turned = half_output(band_parts[0], 0)
     for half in range(1, halves):
         turned = turned + half_output(band_parts[half], half)

time: 477 us -> 435 us (0.912)
  waiting for transfers between devices: 152 us -> 123 us
  matrix products: 102 us -> 90.6 us
    all_to_all x2, waiting for transfers between devices: 20.1 us -> 1.64 us  [half_band(): gathered = lax.all_to_all(spectra, ('blk', 'freq'), 0, 0, tiled=True)]
    dot_general x2 -> x6, matrix products: 36.4 us -> 25.3 us  [half_output(): jnp.einsum('ax,ac->xc', pieces, select, preferred_element_type=jnp.float32)]
    all_to_all x2, waiting for transfers between devices: 132 us -> 121 us  [half_output(): returned = lax.all_to_all(banded, 'blk', 0, 0, tiled=True)]
  transfers between devices with their start and end apart: 5 -> 5, of which waited for: 3 -> 3; matrix products, arithmetic and copies ran while one was open for 40% -> 51% of each run, Pallas kernels for 0% -> 0%
where the time goes in v13:
time: 435 us; the launch traced here: 427 us
  local copies, waits for them, and re-layouts  126 us (29%)
  waiting for transfers between devices  123 us (28%)
  matrix products  90.6 us (21%)
  starting transfers between devices  45.4 us (10%)
  other arithmetic  41.2 us (9%)
    all_to_all x2, waiting for transfers between devices, half_output(): returned = lax.all_to_all(banded, 'blk', 0, 0, tiled=True)  121 us
    dot_general x4, matrix products, half_spectra(): jnp.einsum('mc,nm->cn', part, filtered, precision=lax.Precision.HIGH)  56.4 us
    dot_general x8, local copies, waits for them, and re-layouts, half_spectra(): jnp.einsum('mc,nm->cn', part, filtered, precision=lax.Precision.HIGH)  42.3 us
    dot_general x6, matrix products, half_output(): jnp.einsum('ax,ac->xc', pieces, select, preferred_element_type=jnp.float32)  25.3 us
    all_to_all x2, starting transfers between devices, half_band(): gathered = lax.all_to_all(spectra, ('blk', 'freq'), 0, 0, tiled=True)  20.6 us
    add x1, other arithmetic, per_device(): filtered + filter_taps[tap_index] * frames[:, tap_index:tap_index + SPECTRA]  14 us
    reshape x2, local copies, waits for them, and re-layouts, half_output(): returned = returned.reshape(n_blk * part_chunk, 2 * tile * rows)  13.8 us
    all_to_all x2, starting transfers between devices, half_output(): returned = lax.all_to_all(banded, 'blk', 0, 0, tiled=True)  13.3 us
  transfers between devices with their start and end apart: 5, of which 3 were waited for; matrix products, arithmetic and copies ran while one was open for 51% of the time, Pallas kernels for 0%

profile of v13, /device:TPU:1, one launch (start us, length us, event | category | flops | bytes accessed | tf_op | source)
XLA Modules:
  0.0 427.0 jit_solution(4850233607230449985)
XLA Ops:
  1.3 11.5 %all-to-all-start.1 = ((f32[128,1,32]{2,1,0:T(1,128)}), f32[128,1,32]{2,1,0:T(1,128)S(1)}, u32[]{:S(2)}, u32[]{:S(2)}) async-start(f32[128,1,32]{2,1,0:T(1,128)} %broadcast_in_dim.13), calls=%async_computation.1 | async-start | bytes 131072 | tf_op jit(solution)/shard_map/all_to_all | solution.py:52
  17.3 7.9 %reshape.395 = f32[4,259,2048]{2,1,0:T(8,128)} reshape(bf16[4,530432]{1,0:T(4,128)(2,1)} %param.12) | data formatting | bytes 12730368 | tf_op jit(solution)/shard_map/reshape | solution.py:55
  25.5 4.6 %subtract_multiply_fusion.1 = (f32[32,64,512]{2,1,0:T(8,128)}, f32[32,64,512]{2,1,0:T(8,128)}) fusion(f32[64,512]{1,0:T(8,128)S(1)} %get-tuple-element.27, f32[32,512]{1,0:T(8,128)S(1)} %get-tuple-element.25, f32[64,512]{1,0:T(8,128)S(1)} %get-tuple-element.26, f32[32,512]{1,0:T(8,128)S(1)} %get-tuple-element.24), kind=kLoop, calls=%fused_computation.45 | loop fusion | flops 8388608 | bytes 8781824 | tf_op jit(solution)/shard_map/mul | solution.py:32
  30.1 5.3 %copy.107 = f32[512,2048]{1,0:T(8,128)} copy(f32[512,2048]{0,1:T(8,128)} %bitcast.301) | data formatting | bytes 8388608 | tf_op jit(solution)/shard_map/mc,nm->cn/dot_general | solution.py:69
  35.4 5.3 %dot_general.49 = f32[128,4,2048]{2,1,0:T(4,128)} reshape(f32[512,2048]{1,0:T(8,128)} %copy.107) | data formatting | bytes 8388608 | tf_op jit(solution)/shard_map/mc,nm->cn/dot_general | solution.py:69
  40.7 5.3 %copy.109 = f32[512,2048]{1,0:T(8,128)} copy(f32[512,2048]{0,1:T(8,128)} %bitcast.299) | data formatting | bytes 8388608 | tf_op jit(solution)/shard_map/mc,nm->cn/dot_general | solution.py:69
  46.0 5.2 %dot_general.53 = f32[128,4,2048]{2,1,0:T(4,128)} reshape(f32[512,2048]{1,0:T(8,128)} %copy.109) | data formatting | bytes 8388608 | tf_op jit(solution)/shard_map/mc,nm->cn/dot_general | solution.py:69
  51.2 14.0 %fusion.2 = f32[4,256,2048,1]{2,1,0,3:T(8,128)S(1)} fusion(f32[4,259,2048]{2,1,0:T(8,128)} %reshape.395, f32[2048]{0:T(1024)S(1)} %bitcast.317, f32[2048]{0:T(1024)S(1)} %bitcast.318, f32[2048]{0:T(1024)S(1)} %bitcast.316, f32[2048]{0:T(1024)S(1)} %bitcast.315), kind=kLoop, calls=%fused_computation.12 | loop fusion | flops 14680064 | bytes 41975808 | tf_op jit(solution)/shard_map/add | solution.py:58
  65.3 9.2 %fusion.56 = bf16[128,4,1,4,256]{4,0,3,1,2:T(8,128)(2,1)S(1)} fusion(f32[4,256,2048,1]{2,1,0,3:T(8,128)S(1)} %fusion.2, f32[128,4,2048,1]{2,1,0,3:T(4,128)S(1)} %bitcast.310), kind=kOutput, calls=%fused_computation.67 | convolution fusion | flops 6442975232 | bytes 13631488 | tf_op jit(solution)/shard_map/mc,nm->cn/dot_general | solution.py:69
  74.5 19.8 %fusion.53 = bf16[128,4,1,4,256]{4,0,3,1,2:T(8,128)(2,1)S(1)} fusion(f32[4,256,2048,1]{2,1,0,3:T(8,128)S(1)} %fusion.2, f32[128,4,2048,1]{2,1,0,3:T(4,128)S(1)} %bitcast.311), kind=kOutput, calls=%fused_computation.66 | convolution fusion | flops 6442975232 | bytes 13631488 | tf_op jit(solution)/shard_map/mc,nm->cn/dot_general | solution.py:69
  94.5 2.9 copy.111
  97.5 9.8 %all-to-all-start = ((bf16[128,4,4,2,256]{4,2,1,3,0:T(4,128)(2,1)}), bf16[128,4,4,2,256]{4,2,1,3,0:T(4,128)(2,1)S(1)}, u32[]{:S(2)}, u32[]{:S(2)}) async-start(bf16[128,4,4,2,256]{4,2,1,3,0:T(4,128)(2,1)} %copy.111), calls=%async_computation | async-start | bytes 4194304 | tf_op jit(solution)/shard_map/all_to_all | solution.py:77
  107.4 2.3 gather_fusion.1
  110.5 4.5 %subtract_multiply_fusion = (f32[32,64,512]{2,1,0:T(8,128)}, f32[32,64,512]{2,1,0:T(8,128)}) fusion(f32[64,512]{1,0:T(8,128)S(1)} %get-tuple-element.23, f32[32,512]{1,0:T(8,128)S(1)} %get-tuple-element.21, f32[64,512]{1,0:T(8,128)S(1)} %get-tuple-element.22, f32[32,512]{1,0:T(8,128)S(1)} %get-tuple-element.20), kind=kLoop, calls=%fused_computation.43 | loop fusion | flops 8388608 | bytes 8781824 | tf_op jit(solution)/shard_map/mul | solution.py:32
  115.1 5.3 %copy.129 = f32[512,2048]{1,0:T(8,128)} copy(f32[512,2048]{0,1:T(8,128)} %bitcast.302) | data formatting | bytes 8388608 | tf_op jit(solution)/shard_map/mc,nm->cn/dot_general | solution.py:69
  120.4 5.3 %dot_general.63 = f32[128,4,2048]{2,1,0:T(4,128)} reshape(f32[512,2048]{1,0:T(8,128)} %copy.129) | data formatting | bytes 8388608 | tf_op jit(solution)/shard_map/mc,nm->cn/dot_general | solution.py:69
  125.7 5.3 %copy.127 = f32[512,2048]{1,0:T(8,128)} copy(f32[512,2048]{0,1:T(8,128)} %bitcast.300) | data formatting | bytes 8388608 | tf_op jit(solution)/shard_map/mc,nm->cn/dot_general | solution.py:69
  131.0 5.2 %dot_general.59 = f32[128,4,2048]{2,1,0:T(4,128)} reshape(f32[512,2048]{1,0:T(8,128)} %copy.127) | data formatting | bytes 8388608 | tf_op jit(solution)/shard_map/mc,nm->cn/dot_general | solution.py:69
  136.2 14.2 %fusion.47 = bf16[128,4,1,4,256]{4,0,3,1,2:T(8,128)(2,1)S(1)} fusion(f32[4,256,2048,1]{2,1,0,3:T(8,128)} %copy-done.4, f32[128,4,2048,1]{2,1,0,3:T(4,128)} %bitcast.312), kind=kOutput, calls=%fused_computation.64 | convolution fusion | flops 6442975232 | bytes 13631488 | tf_op jit(solution)/shard_map/mc,nm->cn/dot_general | solution.py:69
  150.4 13.2 %fusion.50 = bf16[128,4,1,4,256]{4,0,3,1,2:T(8,128)(2,1)S(1)} fusion(f32[4,256,2048,1]{2,1,0,3:T(8,128)} %copy-done.4, f32[128,4,2048,1]{2,1,0,3:T(4,128)S(1)} %bitcast.313), kind=kOutput, calls=%fused_computation.65 | convolution fusion | flops 6442975232 | bytes 13631488 | tf_op jit(solution)/shard_map/mc,nm->cn/dot_general | solution.py:69
  163.8 3.0 copy.131
  166.8 10.8 %all-to-all-start.3 = ((bf16[128,4,4,2,256]{4,2,1,3,0:T(4,128)(2,1)}), bf16[128,4,4,2,256]{4,2,1,3,0:T(4,128)(2,1)}, u32[]{:S(2)}, u32[]{:S(2)}) async-start(bf16[128,4,4,2,256]{4,2,1,3,0:T(4,128)(2,1)} %copy.131), calls=%async_computation.3 | async-start | bytes 4194304 | tf_op jit(solution)/shard_map/all_to_all | solution.py:77
  179.8 2.7 copy.113
  182.5 3.8 gather_fusion.2
  188.4 2.4 copy.115
  191.9 2.8 copy.116
  194.6 4.3 fusion.5
  201.4 3.4 broadcast_multiply_fusion.1
  206.4 6.4 %all-to-all-start.2 = ((f32[16,4,2,32,288]{4,3,2,1,0:T(8,128)}), f32[16,4,2,32,288]{4,3,2,1,0:T(8,128)}, u32[]{:S(2)}, u32[]{:S(2)}) async-start(f32[16,4,2,32,288]{4,3,2,1,0:T(8,128)} %broadcast_multiply_fusion.1), calls=%async_computation.2 | async-start | bytes 12582912 | tf_op jit(solution)/shard_map/all_to_all | solution.py:95
  212.8 3.7 copy.132
  216.6 2.7 copy.133
  219.3 3.9 gather_fusion.3
  225.2 2.4 copy.135
  227.7 4.2 copy.136
  232.0 4.6 %fusion.11 = f32[4,1024,512]{2,1,0:T(8,128)S(1)} fusion(bf16[4,512,512]{1,2,0:T(8,128)(2,1)} %bitcast.307, bf16[4,512,256]{2,1,0:T(8,128)(2,1)S(1)} %get-tuple-element.9, bf16[4,512,256]{2,1,0:T(8,128)(2,1)S(1)} %get-tuple-element.8, bf16[4,512,512]{2,1,0:T(8,128)(2,1)} %copy.136), kind=kOutput, calls=%fused_computation.28 | convolution fusion | flops 2160066560 | bytes 14680064 | tf_op jit(solution)/shard_map/kat,kpt->kap/dot_general | solution.py:85
  239.0 3.3 broadcast_multiply_fusion
  242.3 54.3 %all-to-all-done.2 = f32[16,4,2,32,288]{4,3,2,1,0:T(8,128)} async-done(((f32[16,4,2,32,288]{4,3,2,1,0:T(8,128)}), f32[16,4,2,32,288]{4,3,2,1,0:T(8,128)}, u32[]{:S(2)}, u32[]{:S(2)}) %all-to-all-start.2) | async-done | bytes 4718624 | tf_op jit(solution)/shard_map/all_to_all | solution.py:95
  296.6 6.9 %all-to-all-start.4 = ((f32[16,4,2,32,288]{4,3,2,1,0:T(8,128)}), f32[16,4,2,32,288]{4,3,2,1,0:T(8,128)}, u32[]{:S(2)}, u32[]{:S(2)}) async-start(f32[16,4,2,32,288]{4,3,2,1,0:T(8,128)} %broadcast_multiply_fusion), calls=%async_computation.4 | async-start | bytes 12582912 | tf_op jit(solution)/shard_map/all_to_all | solution.py:95
  303.5 6.9 %reshape.388 = f32[64,18432]{1,0:T(8,128)} reshape(f32[16,4,2,32,288]{4,3,2,1,0:T(8,128)} %all-to-all-done.2) | data formatting | bytes 9437184 | tf_op jit(solution)/shard_map/reshape | solution.py:96
  310.4 3.5 fusion.26
  315.6 4.6 %convolution_add_fusion.2 = f32[18432,128]{1,0:T(8,128)} fusion(f32[18432,128]{1,0:T(8,128)S(1)} %convolution_add_fusion.3, bf16[64,128]{1,0:T(8,128)(2,1)S(1)} %copy-done.9, f32[64,18432]{1,0:T(8,128)S(1)} %copy-done.3), kind=kOutput, calls=%fused_computation.7 | convolution fusion | flops 312606720 | bytes 23609344 | tf_op jit(solution)/shard_map/ax,ac->xc/dot_general | solution.py:105
  320.2 67.1 %all-to-all-done.4 = f32[16,4,2,32,288]{4,3,2,1,0:T(8,128)} async-done(((f32[16,4,2,32,288]{4,3,2,1,0:T(8,128)}), f32[16,4,2,32,288]{4,3,2,1,0:T(8,128)}, u32[]{:S(2)}, u32[]{:S(2)}) %all-to-all-start.4) | async-done | bytes 4718624 | tf_op jit(solution)/shard_map/all_to_all | solution.py:95
  387.4 6.9 %reshape.392 = f32[64,18432]{1,0:T(8,128)} reshape(f32[16,4,2,32,288]{4,3,2,1,0:T(8,128)} %all-to-all-done.4) | data formatting | bytes 9437184 | tf_op jit(solution)/shard_map/reshape | solution.py:96
  394.3 3.5 fusion.30
  398.1 4.9 %convolution_add_fusion.1 = f32[18432,128]{1,0:T(8,128)} fusion(f32[18432,128]{1,0:T(8,128)S(1)} %fusion.30, bf16[64,128]{1,0:T(8,128)(2,1)S(1)} %copy-done.8, f32[64,18432]{1,0:T(8,128)S(1)} %copy-done.2), kind=kOutput, calls=%fused_computation.6 | convolution fusion | flops 309067776 | bytes 23609344 | tf_op jit(solution)/shard_map/ax,ac->xc/dot_general | solution.py:105
  403.1 7.3 %fusion = f32[18432,128]{1,0:T(8,128)} fusion(f32[18432,128]{1,0:T(8,128)S(1)} %bitcast.297, f32[18432,128]{1,0:T(8,128)} %convolution_add_fusion.1, bf16[64,128]{1,0:T(8,128)(2,1)S(1)} %copy-done.8, f32[64,18432]{1,0:T(8,128)S(1)} %copy-done.2), kind=kOutput, calls=%fused_computation.5 | convolution fusion | flops 314966016 | bytes 33046528 | tf_op jit(solution)/shard_map/ax,ac->xc/dot_general | solution.py:105
  410.5 11.3 %copy.148 = f32[2,32,9,32,128]{4,1,3,2,0:T(8,128)S(1)} copy(f32[2,32,9,32,128]{4,3,2,1,0:T(8,128)} %bitcast.298) | data formatting | bytes 18874368 | tf_op jit(solution)/shard_map/reshape | solution.py:114
  421.7 4.9 %reverse_bitcast_fusion = f32[2,9,32,32,128]{4,3,2,1,0:T(8,128)} fusion(f32[2,32,9,32,128]{4,1,3,2,0:T(8,128)S(1)} %copy.148), kind=kLoop, calls=%fused_computation.9 | loop fusion | bytes 18874368 | tf_op jit(solution)/shard_map/transpose | solution.py:115
  (88 shorter events, 23.3 us)
Async XLA Ops:
  0.0 13.5 %copy-start = (s32[1024]{0:T(1024)S(1)}, s32[1024]{0:T(1024)}, u32[]{:S(2)}) copy-start(s32[1024]{0:T(1024)} %param.15) | copy-start | bytes 12292
  1.3 96.1 %all-to-all-start.1 = ((f32[128,1,32]{2,1,0:T(1,128)}), f32[128,1,32]{2,1,0:T(1,128)S(1)}, u32[]{:S(2)}, u32[]{:S(2)}) async-start(f32[128,1,32]{2,1,0:T(1,128)} %broadcast_in_dim.13), calls=%async_computation.1 | async-start | bytes 131072 | tf_op jit(solution)/shard_map/all_to_all | solution.py:52
  51.2 14.0 %copy-start.5 = (f32[128,4,2048]{2,1,0:T(4,128)S(1)}, f32[128,4,2048]{2,1,0:T(4,128)}, u32[]{:S(2)}) copy-start(f32[128,4,2048]{2,1,0:T(4,128)} %dot_general.49) | copy-start | bytes 12582916
  65.2 9.2 %copy-start.4 = (f32[4,256,2048,1]{2,1,0,3:T(8,128)}, f32[4,256,2048,1]{2,1,0,3:T(8,128)S(1)}, u32[]{:S(2)}) copy-start(f32[4,256,2048,1]{2,1,0,3:T(8,128)S(1)} %fusion.2) | copy-start | bytes 25165828
  65.3 9.2 %copy-start.6 = (f32[128,4,2048]{2,1,0:T(4,128)S(1)}, f32[128,4,2048]{2,1,0:T(4,128)}, u32[]{:S(2)}) copy-start(f32[128,4,2048]{2,1,0:T(4,128)} %dot_general.53) | copy-start | bytes 12582916
  94.3 13.0 %copy-start.10 = (s32[512]{0:T(512)S(1)}, s32[512]{0:T(512)}, u32[]{:S(2)}) copy-start(s32[512]{0:T(512)} %constant.94) | copy-start | bytes 6148
  97.5 69.4 %all-to-all-start = ((bf16[128,4,4,2,256]{4,2,1,3,0:T(4,128)(2,1)}), bf16[128,4,4,2,256]{4,2,1,3,0:T(4,128)(2,1)S(1)}, u32[]{:S(2)}, u32[]{:S(2)}) async-start(bf16[128,4,4,2,256]{4,2,1,3,0:T(4,128)(2,1)} %copy.111), calls=%async_computation | async-start | bytes 4194304 | tf_op jit(solution)/shard_map/all_to_all | solution.py:77
  136.2 14.2 %copy-start.7 = (f32[128,4,2048]{2,1,0:T(4,128)S(1)}, f32[128,4,2048]{2,1,0:T(4,128)}, u32[]{:S(2)}) copy-start(f32[128,4,2048]{2,1,0:T(4,128)} %dot_general.59) | copy-start | bytes 12582916
  166.8 39.5 %all-to-all-start.3 = ((bf16[128,4,4,2,256]{4,2,1,3,0:T(4,128)(2,1)}), bf16[128,4,4,2,256]{4,2,1,3,0:T(4,128)(2,1)}, u32[]{:S(2)}, u32[]{:S(2)}) async-start(bf16[128,4,4,2,256]{4,2,1,3,0:T(4,128)(2,1)} %copy.131), calls=%async_computation.3 | async-start | bytes 4194304 | tf_op jit(solution)/shard_map/all_to_all | solution.py:77
  206.4 90.2 %all-to-all-start.2 = ((f32[16,4,2,32,288]{4,3,2,1,0:T(8,128)}), f32[16,4,2,32,288]{4,3,2,1,0:T(8,128)}, u32[]{:S(2)}, u32[]{:S(2)}) async-start(f32[16,4,2,32,288]{4,3,2,1,0:T(8,128)} %broadcast_multiply_fusion.1), calls=%async_computation.2 | async-start | bytes 12582912 | tf_op jit(solution)/shard_map/all_to_all | solution.py:95
  296.6 90.8 %all-to-all-start.4 = ((f32[16,4,2,32,288]{4,3,2,1,0:T(8,128)}), f32[16,4,2,32,288]{4,3,2,1,0:T(8,128)}, u32[]{:S(2)}, u32[]{:S(2)}) async-start(f32[16,4,2,32,288]{4,3,2,1,0:T(8,128)} %broadcast_multiply_fusion), calls=%async_computation.4 | async-start | bytes 12582912 | tf_op jit(solution)/shard_map/all_to_all | solution.py:95
  303.5 6.9 %copy-start.9 = (bf16[64,128]{1,0:T(8,128)(2,1)S(1)}, bf16[64,128]{1,0:T(8,128)(2,1)}, u32[]{:S(2)}) copy-start(bf16[64,128]{1,0:T(8,128)(2,1)} %constant.86) | copy-start | bytes 49156
  310.4 3.8 copy-start.3
  320.2 74.1 %copy-start.8 = (bf16[64,128]{1,0:T(8,128)(2,1)S(1)}, bf16[64,128]{1,0:T(8,128)(2,1)}, u32[]{:S(2)}) copy-start(bf16[64,128]{1,0:T(8,128)(2,1)} %constant.90) | copy-start | bytes 49156
  394.3 3.8 copy-start.2
  394.3 8.7 %slice-start = ((s8[9437184]{0:T(1024)(128)(4,1)}), s8[4194304]{0:T(1024)(128)(4,1)S(1)}, s32[]{:S(2)}) async-start(s8[9437184]{0:T(1024)(128)(4,1)} %bitcast.296), calls=%async_computation.5 | async-start | bytes 8388608
  394.3 8.7 %slice-start.1 = ((s8[9437184]{0:T(1024)(128)(4,1)}), s8[4194304]{0:T(1024)(128)(4,1)S(1)}, s32[]{:S(2)}) async-start(s8[9437184]{0:T(1024)(128)(4,1)} %bitcast.296), calls=%async_computation.6 | async-start | bytes 8388608
  398.1 5.0 %slice-start.2 = ((s8[9437184]{0:T(1024)(128)(4,1)}), s8[1048576]{0:T(1024)(128)(4,1)S(1)}, s32[]{:S(2)}) async-start(s8[9437184]{0:T(1024)(128)(4,1)} %bitcast.296), calls=%async_computation.7 | async-start | bytes 2097152
  410.4 16.1 %copy-start.1 = (s32[1024]{0:T(1024)S(1)}, s32[1024]{0:T(1024)}, u32[]{:S(2)}) copy-start(s32[1024]{0:T(1024)} %param.15) | copy-start | bytes 12292

commit v14 on v13

--- a/solution.py
+++ b/solution.py
@@ -89,20 +89,15 @@
         for own in range(n_blk):
             start = (own - steps + 1) % n_blk * tile
             blocks.append(doubled[:, :, own, :, start : start + rows])
-        return jnp.stack(blocks) * (1.0 / SPECTRA)
+        return jnp.stack(blocks)
 
     def half_output(banded, half):
         returned = lax.all_to_all(banded, "blk", 0, 0, tiled=True)
         returned = returned.reshape(n_blk * part_chunk, 2 * tile * rows)
         source = np.arange(n_blk)[:, None] * chunk + half * part_chunk + np.arange(part_chunk)[None, :]
         select = (source.reshape(-1, 1) == np.arange(n_blk * chunk)[None, :]).astype(np.float32)
-        high = returned.astype(jnp.bfloat16)
-        rest = returned - high.astype(jnp.float32)
-        middle = rest.astype(jnp.bfloat16)
-        low = (rest - middle.astype(jnp.float32)).astype(jnp.bfloat16)
-        pieces = jnp.concatenate([high, middle, low], axis=0)
-        select = jnp.asarray(np.concatenate([select] * 3, axis=0), dtype=jnp.bfloat16)
-        return jnp.einsum("ax,ac->xc", pieces, select, preferred_element_type=jnp.float32)
+        select = select * (1.0 / SPECTRA)
+        return jnp.einsum("ax,ac->xc", returned, jnp.asarray(select), precision=lax.Precision.HIGHEST)
 
     spectra_parts = [half_spectra(half) for half in range(halves)]
     band_parts = []

time: 435 us -> 442 us (1.016)
  waiting for transfers between devices: 123 us -> 104 us
  matrix products: 90.6 us -> 102 us
  local copies, waits for them, and re-layouts: 126 us -> 134 us
  other arithmetic: 41.2 us -> 46.6 us
    all_to_all x2, waiting for transfers between devices: 121 us -> 104 us  [half_output(): returned = lax.all_to_all(banded, 'blk', 0, 0, tiled=True)]
    unnamed x17 -> x16, other arithmetic: 2.59 us -> 14.6 us
    dot_general x6 -> x2, matrix products: 25.3 us -> 36.4 us  [half_output(): jnp.einsum('ax,ac->xc', returned, jnp.asarray(select), precision=lax.Prec...]
    unnamed x42 -> x32, local copies, waits for them, and re-layouts: 2.4 us -> 12.4 us
    mul x2 -> x0, other arithmetic: 6.69 us -> none  [half_band(): return jnp.stack(blocks) * (1.0 / SPECTRA)]
  transfers between devices with their start and end apart: 5 -> 5, of which waited for: 3 -> 2; matrix products, arithmetic and copies ran while one was open for 51% -> 56% of each run, Pallas kernels for 0% -> 0%
where the time goes in v14:
time: 442 us; the launch traced here: 434 us
  local copies, waits for them, and re-layouts  134 us (30%)
  waiting for transfers between devices  104 us (24%)
  matrix products  102 us (23%)
  starting transfers between devices  46.8 us (11%)
  other arithmetic  46.6 us (11%)
    all_to_all x2, waiting for transfers between devices, half_output(): returned = lax.all_to_all(banded, 'blk', 0, 0, tiled=True)  104 us
    dot_general x4, matrix products, half_spectra(): jnp.einsum('mc,nm->cn', part, filtered, precision=lax.Precision.HIGH)  56.4 us
    dot_general x8, local copies, waits for them, and re-layouts, half_spectra(): jnp.einsum('mc,nm->cn', part, filtered, precision=lax.Precision.HIGH)  42.3 us
    dot_general x2, matrix products, half_output(): jnp.einsum('ax,ac->xc', returned, jnp.asarray(select), precision=lax.Prec...  36.4 us
    all_to_all x2, starting transfers between devices, half_band(): gathered = lax.all_to_all(spectra, ('blk', 'freq'), 0, 0, tiled=True)  20.6 us
    all_to_all x2, starting transfers between devices, half_output(): returned = lax.all_to_all(banded, 'blk', 0, 0, tiled=True)  14.7 us
    unnamed x16, other arithmetic  14.6 us
    add x1, other arithmetic, per_device(): filtered + filter_taps[tap_index] * frames[:, tap_index:tap_index + SPECTRA]  14 us
  transfers between devices with their start and end apart: 5, of which 2 were waited for; matrix products, arithmetic and copies ran while one was open for 56% of the time, Pallas kernels for 0%

profile of v14, /device:TPU:1, one launch (start us, length us, event | category | flops | bytes accessed | tf_op | source)
XLA Modules:
  0.0 433.8 jit_solution(17210299708409216267)
XLA Ops:
  1.3 11.5 %all-to-all-start.1 = ((f32[128,1,32]{2,1,0:T(1,128)}), f32[128,1,32]{2,1,0:T(1,128)S(1)}, u32[]{:S(2)}, u32[]{:S(2)}) async-start(f32[128,1,32]{2,1,0:T(1,128)} %broadcast_in_dim.13), calls=%async_computation.1 | async-start | bytes 131072 | tf_op jit(solution)/shard_map/all_to_all | solution.py:52
  13.5 2.3 gather_fusion
  17.3 7.9 %reshape.395 = f32[4,259,2048]{2,1,0:T(8,128)} reshape(bf16[4,530432]{1,0:T(4,128)(2,1)} %param.12) | data formatting | bytes 12730368 | tf_op jit(solution)/shard_map/reshape | solution.py:55
  25.5 4.6 %subtract_multiply_fusion.1 = (f32[32,64,512]{2,1,0:T(8,128)}, f32[32,64,512]{2,1,0:T(8,128)}) fusion(f32[64,512]{1,0:T(8,128)S(1)} %get-tuple-element.27, f32[32,512]{1,0:T(8,128)S(1)} %get-tuple-element.25, f32[64,512]{1,0:T(8,128)S(1)} %get-tuple-element.26, f32[32,512]{1,0:T(8,128)S(1)} %get-tuple-element.24), kind=kLoop, calls=%fused_computation.37 | loop fusion | flops 8388608 | bytes 8781824 | tf_op jit(solution)/shard_map/mul | solution.py:32
  30.0 5.4 %copy.104 = f32[512,2048]{1,0:T(8,128)} copy(f32[512,2048]{0,1:T(8,128)} %bitcast.295) | data formatting | bytes 8388608 | tf_op jit(solution)/shard_map/mc,nm->cn/dot_general | solution.py:69
  35.4 5.3 %dot_general.49 = f32[128,4,2048]{2,1,0:T(4,128)} reshape(f32[512,2048]{1,0:T(8,128)} %copy.104) | data formatting | bytes 8388608 | tf_op jit(solution)/shard_map/mc,nm->cn/dot_general | solution.py:69
  40.7 5.4 %copy.106 = f32[512,2048]{1,0:T(8,128)} copy(f32[512,2048]{0,1:T(8,128)} %bitcast.293) | data formatting | bytes 8388608 | tf_op jit(solution)/shard_map/mc,nm->cn/dot_general | solution.py:69
  46.0 5.2 %dot_general.53 = f32[128,4,2048]{2,1,0:T(4,128)} reshape(f32[512,2048]{1,0:T(8,128)} %copy.106) | data formatting | bytes 8388608 | tf_op jit(solution)/shard_map/mc,nm->cn/dot_general | solution.py:69
  51.2 14.0 %fusion.1 = f32[4,256,2048,1]{2,1,0,3:T(8,128)S(1)} fusion(f32[4,259,2048]{2,1,0:T(8,128)} %reshape.395, f32[2048]{0:T(1024)S(1)} %bitcast.311, f32[2048]{0:T(1024)S(1)} %bitcast.312, f32[2048]{0:T(1024)S(1)} %bitcast.310, f32[2048]{0:T(1024)S(1)} %bitcast.309), kind=kLoop, calls=%fused_computation.8 | loop fusion | flops 14680064 | bytes 41975808 | tf_op jit(solution)/shard_map/add | solution.py:58
  65.2 9.2 %fusion.47 = bf16[128,4,1,4,256]{4,0,3,1,2:T(8,128)(2,1)S(1)} fusion(f32[4,256,2048,1]{2,1,0,3:T(8,128)S(1)} %fusion.1, f32[128,4,2048,1]{2,1,0,3:T(4,128)S(1)} %bitcast.304), kind=kOutput, calls=%fused_computation.51 | convolution fusion | flops 6442975232 | bytes 13631488 | tf_op jit(solution)/shard_map/mc,nm->cn/dot_general | solution.py:69
  74.5 19.8 %fusion.44 = bf16[128,4,1,4,256]{4,0,3,1,2:T(8,128)(2,1)S(1)} fusion(f32[4,256,2048,1]{2,1,0,3:T(8,128)S(1)} %fusion.1, f32[128,4,2048,1]{2,1,0,3:T(4,128)S(1)} %bitcast.305), kind=kOutput, calls=%fused_computation.50 | convolution fusion | flops 6442975232 | bytes 13631488 | tf_op jit(solution)/shard_map/mc,nm->cn/dot_general | solution.py:69
  94.5 2.9 copy.108
  97.5 9.8 %all-to-all-start = ((bf16[128,4,4,2,256]{4,2,1,3,0:T(4,128)(2,1)}), bf16[128,4,4,2,256]{4,2,1,3,0:T(4,128)(2,1)S(1)}, u32[]{:S(2)}, u32[]{:S(2)}) async-start(bf16[128,4,4,2,256]{4,2,1,3,0:T(4,128)(2,1)} %copy.108), calls=%async_computation | async-start | bytes 4194304 | tf_op jit(solution)/shard_map/all_to_all | solution.py:77
  107.4 2.3 gather_fusion.1
  110.5 4.6 %subtract_multiply_fusion = (f32[32,64,512]{2,1,0:T(8,128)}, f32[32,64,512]{2,1,0:T(8,128)}) fusion(f32[64,512]{1,0:T(8,128)S(1)} %get-tuple-element.23, f32[32,512]{1,0:T(8,128)S(1)} %get-tuple-element.21, f32[64,512]{1,0:T(8,128)S(1)} %get-tuple-element.22, f32[32,512]{1,0:T(8,128)S(1)} %get-tuple-element.20), kind=kLoop, calls=%fused_computation.35 | loop fusion | flops 8388608 | bytes 8781824 | tf_op jit(solution)/shard_map/mul | solution.py:32
  115.0 5.4 %copy.126 = f32[512,2048]{1,0:T(8,128)} copy(f32[512,2048]{0,1:T(8,128)} %bitcast.296) | data formatting | bytes 8388608 | tf_op jit(solution)/shard_map/mc,nm->cn/dot_general | solution.py:69
  120.4 5.3 %dot_general.63 = f32[128,4,2048]{2,1,0:T(4,128)} reshape(f32[512,2048]{1,0:T(8,128)} %copy.126) | data formatting | bytes 8388608 | tf_op jit(solution)/shard_map/mc,nm->cn/dot_general | solution.py:69
  125.7 5.4 %copy.124 = f32[512,2048]{1,0:T(8,128)} copy(f32[512,2048]{0,1:T(8,128)} %bitcast.294) | data formatting | bytes 8388608 | tf_op jit(solution)/shard_map/mc,nm->cn/dot_general | solution.py:69
  131.0 5.2 %dot_general.59 = f32[128,4,2048]{2,1,0:T(4,128)} reshape(f32[512,2048]{1,0:T(8,128)} %copy.124) | data formatting | bytes 8388608 | tf_op jit(solution)/shard_map/mc,nm->cn/dot_general | solution.py:69
  136.2 14.2 %fusion.38 = bf16[128,4,1,4,256]{4,0,3,1,2:T(8,128)(2,1)S(1)} fusion(f32[4,256,2048,1]{2,1,0,3:T(8,128)} %copy-done.2, f32[128,4,2048,1]{2,1,0,3:T(4,128)} %bitcast.306), kind=kOutput, calls=%fused_computation.48 | convolution fusion | flops 6442975232 | bytes 13631488 | tf_op jit(solution)/shard_map/mc,nm->cn/dot_general | solution.py:69
  150.4 13.2 %fusion.41 = bf16[128,4,1,4,256]{4,0,3,1,2:T(8,128)(2,1)S(1)} fusion(f32[4,256,2048,1]{2,1,0,3:T(8,128)} %copy-done.2, f32[128,4,2048,1]{2,1,0,3:T(4,128)S(1)} %bitcast.307), kind=kOutput, calls=%fused_computation.49 | convolution fusion | flops 6442975232 | bytes 13631488 | tf_op jit(solution)/shard_map/mc,nm->cn/dot_general | solution.py:69
  163.8 3.0 copy.128
  166.8 10.8 %all-to-all-start.3 = ((bf16[128,4,4,2,256]{4,2,1,3,0:T(4,128)(2,1)}), bf16[128,4,4,2,256]{4,2,1,3,0:T(4,128)(2,1)}, u32[]{:S(2)}, u32[]{:S(2)}) async-start(bf16[128,4,4,2,256]{4,2,1,3,0:T(4,128)(2,1)} %copy.128), calls=%async_computation.3 | async-start | bytes 4194304 | tf_op jit(solution)/shard_map/all_to_all | solution.py:77
  177.7 2.2 copy.109
  179.8 2.7 copy.110
  182.5 3.8 gather_fusion.2
  186.3 2.0 fusion.25
  188.4 2.4 copy.112
  190.7 1.2 slice_bitcast_fusion.1
  191.9 2.8 copy.113
  194.7 4.3 fusion.4
  213.3 8.1 %all-to-all-start.2 = ((f32[16,4,2,32,288]{4,3,2,1,0:T(8,128)}), f32[16,4,2,32,288]{4,3,2,1,0:T(8,128)}, u32[]{:S(2)}, u32[]{:S(2)}) async-start(f32[16,4,2,32,288]{4,3,2,1,0:T(8,128)} %fusion.69), calls=%async_computation.2 | async-start | bytes 12582912 | tf_op jit(solution)/shard_map/all_to_all | solution.py:95
  221.4 3.7 copy.129
  225.1 2.7 copy.130
  227.8 3.9 gather_fusion.3
  231.7 2.0 fusion.24
  233.8 2.4 copy.132
  236.2 4.2 copy.133
  240.6 4.6 %fusion.10 = f32[4,1024,512]{2,1,0:T(8,128)S(1)} fusion(bf16[4,512,512]{1,2,0:T(8,128)(2,1)} %bitcast.301, bf16[4,512,256]{2,1,0:T(8,128)(2,1)S(1)} %get-tuple-element.9, bf16[4,512,256]{2,1,0:T(8,128)(2,1)S(1)} %get-tuple-element.8, bf16[4,512,512]{2,1,0:T(8,128)(2,1)} %copy.133), kind=kOutput, calls=%fused_computation.20 | convolution fusion | flops 2160066560 | bytes 14680064 | tf_op jit(solution)/shard_map/kat,kpt->kap/dot_general | solution.py:85
  259.7 45.6 %all-to-all-done.2 = f32[16,4,2,32,288]{4,3,2,1,0:T(8,128)} async-done(((f32[16,4,2,32,288]{4,3,2,1,0:T(8,128)}), f32[16,4,2,32,288]{4,3,2,1,0:T(8,128)}, u32[]{:S(2)}, u32[]{:S(2)}) %all-to-all-start.2) | async-done | bytes 4718624 | tf_op jit(solution)/shard_map/all_to_all | solution.py:95
  305.3 6.7 %all-to-all-start.4 = ((f32[16,4,2,32,288]{4,3,2,1,0:T(8,128)}), f32[16,4,2,32,288]{4,3,2,1,0:T(8,128)}, u32[]{:S(2)}, u32[]{:S(2)}) async-start(f32[16,4,2,32,288]{4,3,2,1,0:T(8,128)} %fusion.52), calls=%async_computation.4 | async-start | bytes 12582912 | tf_op jit(solution)/shard_map/all_to_all | solution.py:95
  312.0 6.9 %reshape.388 = f32[64,18432]{1,0:T(8,128)} reshape(f32[16,4,2,32,288]{4,3,2,1,0:T(8,128)} %all-to-all-done.2) | data formatting | bytes 9437184 | tf_op jit(solution)/shard_map/reshape | solution.py:96
  318.9 18.3 %fusion.124 = f32[18432,128]{1,0:T(8,128)} fusion(f32[64,18432]{1,0:T(8,128)} %reshape.388, f32[64,128]{1,0:T(8,128)S(1)} %copy-done.7), kind=kOutput, calls=%fused_computation.186 | convolution fusion | flops 1811939328 | bytes 14188544 | tf_op jit(solution)/shard_map/ax,ac->xc/dot_general | solution.py:100
  337.2 58.6 %all-to-all-done.4 = f32[16,4,2,32,288]{4,3,2,1,0:T(8,128)} async-done(((f32[16,4,2,32,288]{4,3,2,1,0:T(8,128)}), f32[16,4,2,32,288]{4,3,2,1,0:T(8,128)}, u32[]{:S(2)}, u32[]{:S(2)}) %all-to-all-start.4) | async-done | bytes 4718624 | tf_op jit(solution)/shard_map/all_to_all | solution.py:95
  395.8 6.9 %reshape.392 = f32[64,18432]{1,0:T(8,128)} reshape(f32[16,4,2,32,288]{4,3,2,1,0:T(8,128)} %all-to-all-done.4) | data formatting | bytes 9437184 | tf_op jit(solution)/shard_map/reshape | solution.py:96
  402.8 18.1 %convolution_add_fusion = f32[18432,128]{1,0:T(8,128)S(1)} fusion(f32[18432,128]{1,0:T(8,128)} %fusion.124, f32[64,18432]{1,0:T(8,128)} %reshape.392, f32[64,128]{1,0:T(8,128)S(1)} %copy-done.6), kind=kOutput, calls=%fused_computation.4 | convolution fusion | flops 1814298624 | bytes 23625728 | tf_op jit(solution)/shard_map/ax,ac->xc/dot_general | solution.py:100
  420.9 7.6 %copy.144 = f32[2,32,9,32,128]{4,1,3,2,0:T(8,128)S(1)} copy(f32[2,32,9,32,128]{4,3,2,1,0:T(8,128)S(1)} %bitcast.292) | data formatting | bytes 18874368 | tf_op jit(solution)/shard_map/reshape | solution.py:109
  428.5 4.9 %reverse_bitcast_fusion = f32[2,9,32,32,128]{4,3,2,1,0:T(8,128)} fusion(f32[2,32,9,32,128]{4,1,3,2,0:T(8,128)S(1)} %copy.144), kind=kLoop, calls=%fused_computation.5 | loop fusion | bytes 18874368 | tf_op jit(solution)/shard_map/transpose | solution.py:110
  (71 shorter events, 34.1 us)
Async XLA Ops:
  0.0 13.5 %copy-start = (s32[1024]{0:T(1024)S(1)}, s32[1024]{0:T(1024)}, u32[]{:S(2)}) copy-start(s32[1024]{0:T(1024)} %param.15) | copy-start | bytes 12292
  1.3 96.1 %all-to-all-start.1 = ((f32[128,1,32]{2,1,0:T(1,128)}), f32[128,1,32]{2,1,0:T(1,128)S(1)}, u32[]{:S(2)}, u32[]{:S(2)}) async-start(f32[128,1,32]{2,1,0:T(1,128)} %broadcast_in_dim.13), calls=%async_computation.1 | async-start | bytes 131072 | tf_op jit(solution)/shard_map/all_to_all | solution.py:52
  51.2 14.0 %copy-start.3 = (f32[128,4,2048]{2,1,0:T(4,128)S(1)}, f32[128,4,2048]{2,1,0:T(4,128)}, u32[]{:S(2)}) copy-start(f32[128,4,2048]{2,1,0:T(4,128)} %dot_general.49) | copy-start | bytes 12582916
  65.2 9.2 %copy-start.2 = (f32[4,256,2048,1]{2,1,0,3:T(8,128)}, f32[4,256,2048,1]{2,1,0,3:T(8,128)S(1)}, u32[]{:S(2)}) copy-start(f32[4,256,2048,1]{2,1,0,3:T(8,128)S(1)} %fusion.1) | copy-start | bytes 25165828
  65.2 9.2 %copy-start.4 = (f32[128,4,2048]{2,1,0:T(4,128)S(1)}, f32[128,4,2048]{2,1,0:T(4,128)}, u32[]{:S(2)}) copy-start(f32[128,4,2048]{2,1,0:T(4,128)} %dot_general.53) | copy-start | bytes 12582916
  94.3 13.0 %copy-start.8 = (s32[512]{0:T(512)S(1)}, s32[512]{0:T(512)}, u32[]{:S(2)}) copy-start(s32[512]{0:T(512)} %constant.86) | copy-start | bytes 6148
  97.5 69.4 %all-to-all-start = ((bf16[128,4,4,2,256]{4,2,1,3,0:T(4,128)(2,1)}), bf16[128,4,4,2,256]{4,2,1,3,0:T(4,128)(2,1)S(1)}, u32[]{:S(2)}, u32[]{:S(2)}) async-start(bf16[128,4,4,2,256]{4,2,1,3,0:T(4,128)(2,1)} %copy.108), calls=%async_computation | async-start | bytes 4194304 | tf_op jit(solution)/shard_map/all_to_all | solution.py:77
  136.2 14.2 %copy-start.5 = (f32[128,4,2048]{2,1,0:T(4,128)S(1)}, f32[128,4,2048]{2,1,0:T(4,128)}, u32[]{:S(2)}) copy-start(f32[128,4,2048]{2,1,0:T(4,128)} %dot_general.59) | copy-start | bytes 12582916
  166.8 46.4 %all-to-all-start.3 = ((bf16[128,4,4,2,256]{4,2,1,3,0:T(4,128)(2,1)}), bf16[128,4,4,2,256]{4,2,1,3,0:T(4,128)(2,1)}, u32[]{:S(2)}, u32[]{:S(2)}) async-start(bf16[128,4,4,2,256]{4,2,1,3,0:T(4,128)(2,1)} %copy.128), calls=%async_computation.3 | async-start | bytes 4194304 | tf_op jit(solution)/shard_map/all_to_all | solution.py:77
  213.3 92.0 %all-to-all-start.2 = ((f32[16,4,2,32,288]{4,3,2,1,0:T(8,128)}), f32[16,4,2,32,288]{4,3,2,1,0:T(8,128)}, u32[]{:S(2)}, u32[]{:S(2)}) async-start(f32[16,4,2,32,288]{4,3,2,1,0:T(8,128)} %fusion.69), calls=%async_computation.2 | async-start | bytes 12582912 | tf_op jit(solution)/shard_map/all_to_all | solution.py:95
  305.3 90.6 %all-to-all-start.4 = ((f32[16,4,2,32,288]{4,3,2,1,0:T(8,128)}), f32[16,4,2,32,288]{4,3,2,1,0:T(8,128)}, u32[]{:S(2)}, u32[]{:S(2)}) async-start(f32[16,4,2,32,288]{4,3,2,1,0:T(8,128)} %fusion.52), calls=%async_computation.4 | async-start | bytes 12582912 | tf_op jit(solution)/shard_map/all_to_all | solution.py:95
  311.9 7.0 %copy-start.7 = (f32[64,128]{1,0:T(8,128)S(1)}, f32[64,128]{1,0:T(8,128)}, u32[]{:S(2)}) copy-start(f32[64,128]{1,0:T(8,128)} %constant.80.clone) | copy-start | bytes 98308
  337.2 65.6 %copy-start.6 = (f32[64,128]{1,0:T(8,128)S(1)}, f32[64,128]{1,0:T(8,128)}, u32[]{:S(2)}) copy-start(f32[64,128]{1,0:T(8,128)} %constant.81.clone) | copy-start | bytes 98308
  420.9 12.4 %copy-start.1 = (s32[1024]{0:T(1024)S(1)}, s32[1024]{0:T(1024)}, u32[]{:S(2)}) copy-start(s32[1024]{0:T(1024)} %param.15) | copy-start | bytes 12292
